TPU v7x, 512 devices: a whole 4x4x16 slice. The times are simulated.
512 devices in a mesh: dp: 8 (over y, core), tensor: 64 (over x, z).
Axes of the slice: x: 4, y: 4, z: 16, core: 2. Of those that a mesh axis runs over, the one named last changes fastest.
Arguments:
- tokens: bfloat16 [8, 128, 4544], P('dp', 'tensor'), may hold values from -6 to 6
- ln_gain: float32 [4544], replicated, may hold values from 0.1 to 1.9
- ln_bias: float32 [4544], replicated, may hold values from -3 to 3
- q_weight: bfloat16 [4544, 4096], P(None, 'tensor'), may hold values from -0.09375 to 0.09375
- kv_weight: bfloat16 [4544, 128], replicated, may hold values from -0.25 to 0.25
- dense_weight: bfloat16 [4096, 4544], P('tensor'), may hold values from -0.09375 to 0.09375
- up_weight: bfloat16 [4544, 9088], P(None, 'tensor'), may hold values from -0.09375 to 0.09375
- down_weight: bfloat16 [9088, 4544], P('tensor'), may hold values from -0.0625 to 0.0625
- kv_cache: bfloat16 [8, 512, 64, 128], P(None, 'tensor', 'dp'), may hold values from -96 to 96
- cache_lengths: int32 [8], replicated, may hold values from 512 to 32768, as said below
Outputs:
- layer_out: bfloat16 [8, 128, 4544], P('dp', 'tensor')
Inputs may be any that keep to these rules, and one draw needn't show every extreme that they name: `cache_lengths`: exactly one request has 32768 cached positions; each other has between 512 and 2048.
All inputs are finite; a program needn't handle non-finite values.
Results may differ from a plain program's by a relative error of at most 0.04.
Values may be sent and summed in bfloat16 or wider, within the bound.
No kernel may reach another device: no remote copies, remote signals or barrier semaphores. Data moves between devices by JAX's collectives and lax.ppermute only.
A program may use at most 128 MiB of HBM per device.

v0:
```python
import math

import jax
import jax.numpy as jnp
from jax import lax
from jax.sharding import PartitionSpec as P

NEGATIVE = -1e30


def norm_rows(rows, gain, shift):
    widened = rows.astype(jnp.float32)
    center = jnp.mean(widened, axis=-1, keepdims=True)
    centered = widened - center
    variance = jnp.mean(centered * centered, axis=-1, keepdims=True)
    return (centered * lax.rsqrt(variance + 1e-05) * gain + shift).astype(jnp.bfloat16)


def rotary_tables(places, width):
    half = width // 2
    freqs = jnp.exp(jnp.arange(half, dtype=jnp.float32) * (-2.0 * math.log(10000.0) / width))
    angle = places.astype(jnp.float32)[..., None] * freqs
    cosine = jnp.concatenate([jnp.cos(angle), jnp.cos(angle)], axis=-1)
    sine = jnp.concatenate([jnp.sin(angle), jnp.sin(angle)], axis=-1)
    return (cosine, sine)


def rotate(values, cosine, sine):
    half = values.shape[-1] // 2
    turned = jnp.concatenate([-values[..., half:], values[..., :half]], axis=-1)
    return values * cosine + turned * sine


def combine(first, second):
    first_values, first_top, first_total = first
    second_values, second_top, second_total = second
    best = jnp.maximum(first_top, second_top)
    first_scale = jnp.exp(first_top - best)
    second_scale = jnp.exp(second_top - best)
    return (
        first_values * first_scale[..., None] + second_values * second_scale[..., None],
        best,
        first_total * first_scale + second_total * second_scale,
    )


def absorb(state, queries, key_rows, value_rows, valid):
    scores = jnp.dot(queries, key_rows.T, preferred_element_type=jnp.float32) * (
        1.0 / math.sqrt(queries.shape[-1])
    )
    scores = jnp.where(valid, scores, NEGATIVE)
    best = jnp.max(scores, axis=1)
    weights = jnp.exp(scores - best[:, None])
    block = (
        jnp.dot(weights.astype(jnp.bfloat16), value_rows, preferred_element_type=jnp.float32),
        best,
        jnp.sum(weights, axis=1),
    )
    return combine(state, block)


def fold_keys(state, queries, keys, valid):
    width = queries.shape[-1]
    return absorb(state, queries, keys[:, :width], keys[:, width:], valid)


def empty_state(rows, width, lead):
    return (
        jnp.zeros(lead + (rows, width), jnp.float32),
        jnp.full(lead + (rows,), NEGATIVE, jnp.float32),
        jnp.zeros(lead + (rows,), jnp.float32),
    )


def local(
    tokens,
    ln_gain,
    ln_bias,
    q_weight,
    kv_weight,
    dense_weight,
    up_weight,
    down_weight,
    kv_cache,
    cache_lengths,
):
    width = kv_weight.shape[1] // 2
    query_cols = q_weight.shape[1]
    heads_here = query_cols // width
    normed = norm_rows(tokens[0], ln_gain, ln_bias)
    piece = lax.all_gather(normed, "tensor", axis=0, tiled=True)
    projected = jnp.concatenate(
        [
            jnp.dot(piece, q_weight, preferred_element_type=jnp.float32),
            jnp.dot(piece, kv_weight, preferred_element_type=jnp.float32),
            jnp.dot(piece, up_weight, preferred_element_type=jnp.float32),
        ],
        axis=1,
    )
    span = projected.shape[0]
    group = lax.axis_index("dp")
    own_length = lax.dynamic_index_in_dim(cache_lengths, group, 0, keepdims=False)
    places = own_length + jnp.arange(span, dtype=jnp.int32)
    cosine, sine = rotary_tables(places, width)
    queries = rotate(
        projected[:, :query_cols].reshape(span, heads_here, width),
        cosine[:, None, :],
        sine[:, None, :],
    ).astype(jnp.bfloat16)
    new_keys = rotate(projected[:, query_cols : query_cols + width], cosine, sine).astype(
        jnp.bfloat16
    )
    new_values = projected[:, query_cols + width : query_cols + 2 * width].astype(jnp.bfloat16)
    hidden = jax.nn.gelu(projected[:, query_cols + 2 * width :], approximate=False).astype(
        jnp.bfloat16
    )
    rows = span * heads_here
    query_rows = queries.reshape(rows, width)
    mine = lax.all_to_all(kv_cache, "dp", split_axis=0, concat_axis=2, tiled=True)
    inner_all = mine.shape[2]
    flat_keys = lax.all_gather(mine, "tensor", axis=1, tiled=True)[0].reshape(-1, 2 * width)
    places_piece = jnp.arange(flat_keys.shape[0], dtype=jnp.int32)
    valid = (places_piece < own_length)[None, :]
    state = lax.cond(
        jnp.int32(0) * inner_all < own_length,
        lambda carry: fold_keys(carry, query_rows, flat_keys, valid),
        lambda carry: carry,
        empty_state(rows, width, ()),
    )
    token_of_row = jnp.arange(rows, dtype=jnp.int32) // heads_here
    causal = jnp.arange(span, dtype=jnp.int32)[None, :] <= token_of_row[:, None]
    summed, best, total = absorb(state, query_rows, new_keys, new_values, causal)
    attn = (summed / total[:, None]).astype(jnp.bfloat16)
    layer_rows = lax.psum_scatter(
        jnp.dot(attn, dense_weight, preferred_element_type=jnp.float32)
        + jnp.dot(hidden, down_weight, preferred_element_type=jnp.float32),
        "tensor",
        scatter_dimension=0,
        tiled=True,
    )
    return (tokens[0].astype(jnp.float32) + layer_rows).astype(jnp.bfloat16)[None]


def solution(mesh):
    return jax.shard_map(
        local,
        mesh=mesh,
        in_specs=(
            P("dp", "tensor", None),
            P(),
            P(),
            P(None, "tensor"),
            P(),
            P("tensor", None),
            P(None, "tensor"),
            P("tensor", None),
            P(None, "tensor", "dp", None),
            P(),
        ),
        out_specs=P("dp", "tensor", None),
        check_vma=False,
    )
```

profile of v0, /device:TPU:8, one launch (start us, length us, event | category | flops | bytes accessed | tf_op | source)
XLA Modules:
  0.0 637.8 jit_solution(12326027038590986792)
XLA Ops:
  6.5 0.0 copy-start
  6.5 0.0 copy-start.2
  6.5 0.0 all-gather.6.cloned.1.call-start
  6.5 1.0 convert_reduce_fusion
  7.6 0.9 fusion.40
  8.5 1.5 fusion.87
  10.0 0.0 all-gather.6.cloned.1.call-update
  10.0 0.0 all-gather.4.cloned.1.call-start
  10.1 13.7 %all_to_all.18 = bf16[8,8,8,128]{3,2,1,0:T(8,128)(2,1)S(1)} all-to-all(bf16[8,8,8,128]{3,2,1,0:T(8,128)(2,1)} %param.20), channel_id=1, replica_groups=mesh['dp'=8,'tensor'=64] {'dp'}, dimensions={0} | all-to-all | bytes 262144 | tf_op jit(solution)/shard_map/all_to_all | solution.py:119
  23.8 0.7 copy_bitcast_fusion
  24.5 0.0 all-gather.4.cloned.1.call-update
  24.5 0.0 all-reduce.3.cloned.1.call-start
  24.5 1.3 dynamic_slice.4
  26.5 0.7 add_convert_fusion
  27.2 0.1 multiply_sine_fusion
  27.4 127.4 %all-gather.6.cloned.1.call-done = bf16[64,2,4544]{2,1,0:T(2,128)(2,1)} async-done(((bf16[1,2,4544]{2,1,0:T(2,128)(2,1)}), bf16[64,2,4544]{2,1,0:T(2,128)(2,1)}) %all-gather.6.cloned.1.call-update) | async-done | bytes 1163280 | tf_op jit(solution)/shard_map/all_gather | solution.py:91
  154.8 1.9 reshape.54
  156.7 0.0 copy-done.2
  156.7 0.5 fusion.132
  157.3 1.8 fusion.133
  159.1 0.2 fusion.129
  159.4 0.0 copy-done
  159.4 4.5 fusion.38
  163.9 145.9 %all-gather.4.cloned.1.call-done = bf16[1,512,64,128]{3,2,0,1:T(8,128)(2,1)} async-done(((bf16[1,8,64,128]{3,2,0,1:T(8,128)(2,1)}), bf16[1,512,64,128]{3,2,0,1:T(8,128)(2,1)}) %all-gather.4.cloned.1.call-update) | async-done | bytes 8388624 | tf_op jit(solution)/shard_map/all_gather | solution.py:121
  309.8 0.1 iota.22
  309.8 0.0 copy-start.1
  309.9 37.5 %conditional.1 = (f32[128,64]{0,1:T(8,128)S(1)}, f32[128]{0:T(128)}, f32[128]{0:T(128)S(1)}) conditional(s32[]{:T(128)} %convert_element_type.45, () %tuple.13, (s32[]{:T(128)}, s32[1,32768]{1,0:T(1,128)S(1)}, bf16[1,512,64,128]{3,2,0,1:T(8,128)(2,1)}, bf16[128,64]{0,1:T(8,128)(2,1)S(1)}) %tuple.14), branch_computations={%region_2.3_spmd, %region_3.6_spmd} | conditional | flops 1103151872 | bytes 67361304 | solution.py:124
  310.1 1.1 compare_reduce_fusion
  311.2 11.5 %fusion.128 = (f32[128]{0:T(128)S(1)}, f32[128,32768]{1,0:T(8,128)}) fusion(bf16[128,64]{0,1:T(8,128)(2,1)S(1)} %get-tuple-element.37, bf16[32768,128]{1,0:T(8,128)(2,1)} %bitcast.55, pred[32768]{0:T(1024)(128)(4,1)S(1)} %compare_reduce_fusion), kind=kOutput, calls=%fused_computation.153 | convolution fusion | flops 549453696 | bytes 25215488 | tf_op jit(solution)/shard_map/cond/branch_1_fun/dot_general | solution.py:48
  322.7 8.2 %fusion.1 = f32[128]{0:T(128)S(1)} fusion(f32[128,32768]{1,0:T(8,128)} %get-tuple-element.45, f32[128]{0:T(128)S(1)} %get-tuple-element.44), kind=kLoop, calls=%fused_computation.3 | loop fusion | flops 8388480 | bytes 16778240 | tf_op jit(solution)/shard_map/cond/branch_1_fun/reduce_sum | solution.py:57
  330.9 0.5 multiply_add_fusion
  331.4 0.7 exponential_multiply_fusion
  332.1 15.1 %fusion.13 = f32[128,64]{0,1:T(8,128)S(1)} fusion(bf16[32768,128]{1,0:T(8,128)(2,1)} %bitcast.56, f32[128,32768]{1,0:T(8,128)} %get-tuple-element.45, f32[128]{0:T(128)S(1)} %get-tuple-element.44, f32[128]{0:T(128)S(1)} %get-tuple-element.39, f32[128]{0:T(128)S(1)} %exponential_multiply_fusion), kind=kOutput, calls=%fused_computation.10 | convolution fusion | flops 545275904 | bytes 25200128 | tf_op jit(solution)/shard_map/cond/branch_1_fun/dot_general | solution.py:55
  347.4 0.7 multiply_add_fusion.1
  348.0 0.0 copy-done.1
  348.0 3.8 convolution_add_fusion
  351.8 0.0 copy-start.3
  351.8 0.0 all-reduce.3.cloned.1.call-update
  351.9 1.3 dynamic-slice
  353.8 275.9 %all-reduce.3.cloned.1.call-done = f32[128,4544]{1,0:T(8,128)} async-done(((f32[128,4544]{1,0:T(8,128)}), f32[128,4544]{1,0:T(8,128)}) %all-reduce.3.cloned.1.call-update) | async-done | bytes 2326544
  629.7 0.0 copy-done.3
  629.7 1.5 fusion.86
  (7 shorter events, 0.1 us)
Async XLA Ops:
  6.5 152.9 %copy-start = (bf16[142,4544]{1,0:T(8,128)(2,1)S(1)}, bf16[142,4544]{1,0:T(8,128)(2,1)}, u32[]{:S(2)}) copy-start(bf16[142,4544]{1,0:T(8,128)(2,1)} %param.19) | copy-start | bytes 3871492
  6.5 150.2 %copy-start.2 = (bf16[4544,64]{0,1:T(8,128)(2,1)S(1)}, bf16[4544,64]{0,1:T(8,128)(2,1)}, u32[]{:S(2)}) copy-start(bf16[4544,64]{0,1:T(8,128)(2,1)} %param.15) | copy-start | bytes 1744900
  6.5 148.3 %all-gather.6.cloned.1.call-start = ((), (), s32[]{:S(2)}) async-start(), calls=%async_computation.2 | async-start | bytes 1198080 | tf_op jit(solution)/shard_map/all_gather | solution.py:91
  10.0 299.8 %all-gather.4.cloned.1.call-start = ((), (), s32[]{:S(2)}) async-start(), calls=%async_computation.1 | async-start | bytes 8519680 | tf_op jit(solution)/shard_map/all_gather | solution.py:121
  24.5 605.2 %all-reduce.3.cloned.1.call-start = ((), (), s32[]{:S(2)}) async-start(), calls=%async_computation.3 | async-start | bytes 4718592
  309.8 38.2 %copy-start.1 = (bf16[64,4544]{1,0:T(8,128)(2,1)S(1)}, bf16[64,4544]{1,0:T(8,128)(2,1)}, u32[]{:S(2)}) copy-start(bf16[64,4544]{1,0:T(8,128)(2,1)} %param.17) | copy-start | bytes 1744900
  351.8 277.9 %copy-start.3 = (bf16[1,2,4544]{2,1,0:T(2,128)(2,1)S(1)}, bf16[1,2,4544]{2,1,0:T(2,128)(2,1)}, u32[]{:S(2)}) copy-start(bf16[1,2,4544]{2,1,0:T(2,128)(2,1)} %param.12) | copy-start | bytes 54532
Sparse Core Ops, SparseCore 0:
  10.3 144.4 all-gather.5
  157.7 151.9 all-gather.3
  352.0 277.6 all-reduce.2
where the time goes:
time: 638 us
  waiting for transfers between devices  549 us (86%)
  matrix products  37.5 us (6%)
  other arithmetic  17 us (3%)
  between operations  14.6 us (2%)
  blocking collectives  13.7 us (2%)
    unnamed x4, waiting for transfers between devices  276 us
    all_gather x1, waiting for transfers between devices, local(): lax.all_gather(mine, 'tensor', axis=1, tiled=True)[0].reshape(-1, 2 * width)  146 us
    all_gather x1, waiting for transfers between devices, local(): piece = lax.all_gather(normed, 'tensor', axis=0, tiled=True)  127 us
    dot_general x1, matrix products, absorb(): jnp.dot(weights.astype(jnp.bfloat16), value_rows, preferred_element_type=...  15.1 us
    all_to_all x1, blocking collectives, local(): lax.all_to_all(kv_cache, 'dp', split_axis=0, concat_axis=2, tiled=True)  13.7 us
  transfers between devices with their start and end apart: 3, of which 3 were waited for; matrix products, arithmetic and copies ran while one was open for 2% of the time, Pallas kernels for 0%

commit v1 on v0

--- a/solution.py
+++ b/solution.py
@@ -3,9 +3,11 @@
 import jax
 import jax.numpy as jnp
 from jax import lax
+from jax.sharding import Mesh
 from jax.sharding import PartitionSpec as P
 
 NEGATIVE = -1e30
+TENSOR = ("tx", "tz")
 
 
 def norm_rows(rows, gain, shift):
@@ -70,6 +72,42 @@
         jnp.full(lead + (rows,), NEGATIVE, jnp.float32),
         jnp.zeros(lead + (rows,), jnp.float32),
     )
+
+
+def tensor_index():
+    return lax.axis_index("tx") * lax.axis_size("tz") + lax.axis_index("tz")
+
+
+def bit_reversed(index, bits):
+    out = jnp.zeros_like(index)
+    for b in range(bits):
+        out = out | (((index >> b) & 1) << (bits - 1 - b))
+    return out
+
+
+def gather_rounds(piece, n):
+    bits = n.bit_length() - 1
+    me = tensor_index()
+    buf = piece[None]
+    for b in reversed(range(bits)):
+        other = lax.ppermute(buf, TENSOR, [(i, i ^ (1 << b)) for i in range(n)])
+        low = ((me >> b) & 1) == 0
+        buf = jnp.concatenate(
+            [jnp.where(low, buf, other), jnp.where(low, other, buf)], axis=0
+        )
+    return buf
+
+
+def scatter_rounds(partial, n):
+    bits = n.bit_length() - 1
+    me = tensor_index()
+    buf = partial.reshape((2,) * bits + partial.shape[1:])
+    for b in range(bits):
+        mine = (me >> b) & 1
+        keep = lax.dynamic_index_in_dim(buf, mine, 0, keepdims=False)
+        send = lax.dynamic_index_in_dim(buf, 1 - mine, 0, keepdims=False)
+        buf = keep + lax.ppermute(send, TENSOR, [(i, i ^ (1 << b)) for i in range(n)])
+    return buf
 
 
 def local(
@@ -84,11 +122,22 @@
     kv_cache,
     cache_lengths,
 ):
+    n = lax.axis_size("tx") * lax.axis_size("tz")
+    bits = n.bit_length() - 1
     width = kv_weight.shape[1] // 2
     query_cols = q_weight.shape[1]
     heads_here = query_cols // width
+    width_model = tokens.shape[-1]
+    per_device = tokens.shape[1]
+
+    mine = lax.all_to_all(kv_cache, "dp", split_axis=0, concat_axis=2, tiled=True)
+    inner_all = mine.shape[2]
+    gathered = lax.all_gather(mine, "tz", axis=1, tiled=True)
+    gathered = lax.all_gather(gathered, "tx", axis=1, tiled=True)
+    flat_keys = gathered[0].reshape(-1, 2 * width)
+
     normed = norm_rows(tokens[0], ln_gain, ln_bias)
-    piece = lax.all_gather(normed, "tensor", axis=0, tiled=True)
+    piece = gather_rounds(normed, n).reshape(n * per_device, width_model)
     projected = jnp.concatenate(
         [
             jnp.dot(piece, q_weight, preferred_element_type=jnp.float32),
@@ -98,9 +147,11 @@
         axis=1,
     )
     span = projected.shape[0]
+    row = jnp.arange(span, dtype=jnp.int32)
+    token_pos = bit_reversed(row // per_device, bits) * per_device + row % per_device
     group = lax.axis_index("dp")
     own_length = lax.dynamic_index_in_dim(cache_lengths, group, 0, keepdims=False)
-    places = own_length + jnp.arange(span, dtype=jnp.int32)
+    places = own_length + token_pos
     cosine, sine = rotary_tables(places, width)
     queries = rotate(
         projected[:, :query_cols].reshape(span, heads_here, width),
@@ -116,9 +167,6 @@
     )
     rows = span * heads_here
     query_rows = queries.reshape(rows, width)
-    mine = lax.all_to_all(kv_cache, "dp", split_axis=0, concat_axis=2, tiled=True)
-    inner_all = mine.shape[2]
-    flat_keys = lax.all_gather(mine, "tensor", axis=1, tiled=True)[0].reshape(-1, 2 * width)
     places_piece = jnp.arange(flat_keys.shape[0], dtype=jnp.int32)
     valid = (places_piece < own_length)[None, :]
     state = lax.cond(
@@ -127,36 +175,37 @@
         lambda carry: carry,
         empty_state(rows, width, ()),
     )
-    token_of_row = jnp.arange(rows, dtype=jnp.int32) // heads_here
-    causal = jnp.arange(span, dtype=jnp.int32)[None, :] <= token_of_row[:, None]
+    pos_of_row = jnp.repeat(token_pos, heads_here)
+    causal = token_pos[None, :] <= pos_of_row[:, None]
     summed, best, total = absorb(state, query_rows, new_keys, new_values, causal)
     attn = (summed / total[:, None]).astype(jnp.bfloat16)
-    layer_rows = lax.psum_scatter(
-        jnp.dot(attn, dense_weight, preferred_element_type=jnp.float32)
-        + jnp.dot(hidden, down_weight, preferred_element_type=jnp.float32),
-        "tensor",
-        scatter_dimension=0,
-        tiled=True,
-    )
+    partial = jnp.dot(attn, dense_weight, preferred_element_type=jnp.float32) + jnp.dot(
+        hidden, down_weight, preferred_element_type=jnp.float32
+    )
+    layer_rows = scatter_rounds(partial.reshape(n, per_device, width_model), n)
     return (tokens[0].astype(jnp.float32) + layer_rows).astype(jnp.bfloat16)[None]
 
 
 def solution(mesh):
+    dp = mesh.shape["dp"]
+    tensor = mesh.shape["tensor"]
+    tx = 4 if tensor % 4 == 0 else 1
+    mesh3 = Mesh(mesh.devices.reshape(dp, tx, tensor // tx), ("dp", "tx", "tz"))
     return jax.shard_map(
         local,
-        mesh=mesh,
+        mesh=mesh3,
         in_specs=(
-            P("dp", "tensor", None),
-            P(),
-            P(),
-            P(None, "tensor"),
-            P(),
-            P("tensor", None),
-            P(None, "tensor"),
-            P("tensor", None),
-            P(None, "tensor", "dp", None),
+            P("dp", TENSOR, None),
+            P(),
+            P(),
+            P(None, TENSOR),
+            P(),
+            P(TENSOR, None),
+            P(None, TENSOR),
+            P(TENSOR, None),
+            P(None, TENSOR, "dp", None),
             P(),
         ),
-        out_specs=P("dp", "tensor", None),
+        out_specs=P("dp", TENSOR, None),
         check_vma=False,
     )

time: 638 us -> 369 us (0.58)
  the two profiles are of different devices: /device:TPU:8 before, /device:TPU:2 now
where the time goes in v1:
time: 369 us; the launch traced here: 368 us
  waiting for transfers between devices  198 us (54%)
  starting transfers between devices  69.6 us (19%)
  matrix products  37.8 us (10%)
  other arithmetic  25.9 us (7%)
  between operations  14.5 us (4%)
  local copies, waits for them, and re-layouts  11.6 us (3%)
  blocking collectives  10.7 us (3%)
    ppermute x6, waiting for transfers between devices, scatter_rounds(): buf = keep + lax.ppermute(send, TENSOR, [(i, i ^ 1 << b) for i in range(n)])  87.6 us
    all_gather x1, waiting for transfers between devices, local(): gathered = lax.all_gather(mine, 'tz', axis=1, tiled=True)  68.4 us
    ppermute x6, starting transfers between devices, scatter_rounds(): buf = keep + lax.ppermute(send, TENSOR, [(i, i ^ 1 << b) for i in range(n)])  35.7 us
    ppermute x6, starting transfers between devices, gather_rounds(): other = lax.ppermute(buf, TENSOR, [(i, i ^ 1 << b) for i in range(n)])  33.8 us
    ppermute x6, waiting for transfers between devices, gather_rounds(): other = lax.ppermute(buf, TENSOR, [(i, i ^ 1 << b) for i in range(n)])  31.1 us
    dot_general x1, matrix products, absorb(): jnp.dot(weights.astype(jnp.bfloat16), value_rows, preferred_element_type=...  15.1 us
    dot_general x2, matrix products, absorb(): jnp.dot(queries, key_rows.T, preferred_element_type=jnp.float32)  11.8 us
    all_to_all x1, blocking collectives, local(): lax.all_to_all(kv_cache, 'dp', split_axis=0, concat_axis=2, tiled=True)  10.7 us
  transfers between devices with their start and end apart: 14, of which 13 were waited for; matrix products, arithmetic and copies ran while one was open for 6% of the time, Pallas kernels for 0%

profile of v1, /device:TPU:2, one launch (start us, length us, event | category | flops | bytes accessed | tf_op | source)
XLA Modules:
  0.0 368.0 jit_solution(5301556345453204702)
XLA Ops:
  6.6 10.7 %all_to_all.18 = bf16[8,8,8,128]{3,2,1,0:T(8,128)(2,1)S(1)} all-to-all(bf16[8,8,8,128]{3,2,1,0:T(8,128)(2,1)} %param.20), channel_id=1, replica_groups=mesh['dp'=8,'tx'=4,'tz'=16] {'dp'}, dimensions={0} | all-to-all | bytes 262144 | tf_op jit(solution)/shard_map/all_to_all | solution.py:133
  17.3 0.7 copy_bitcast_fusion
  18.0 0.9 convert_reduce_fusion
  18.9 0.9 fusion.39
  19.9 0.9 fusion.44
  20.7 4.0 %collective-permute-start = (bf16[1,2,4544]{2,1,0:T(2,128)(2,1)S(1)}, bf16[1,2,4544]{2,1,0:T(2,128)(2,1)S(1)}, u32[]{:S(2)}, u32[]{:S(2)}) collective-permute-start(bf16[1,2,4544]{2,1,0:T(2,128)(2,1)S(1)} %fusion.44), channel_id=1, source_target_pairs={{0,32},{1,33},{2,34},{3,35},{4,36},{5,37},{6,38},{7,39},{8,40},{9,... | collective-permute-start | bytes 54536 | tf_op jit(solution)/shard_map/ppermute | solution.py:93
  24.8 68.4 %all-gather.3.cloned.1.call-done = bf16[1,128,64,128]{3,2,0,1:T(8,128)(2,1)} async-done(((bf16[1,8,64,128]{3,2,0,1:T(8,128)(2,1)}), bf16[1,128,64,128]{3,2,0,1:T(8,128)(2,1)}) %all-gather.3.cloned.1.call-update) | async-done | bytes 2097168 | tf_op jit(solution)/shard_map/all_gather | solution.py:135
  93.5 2.5 collective-permute-start.1
  96.0 3.4 collective-permute-done.1
  99.6 8.4 %collective-permute-start.2 = (bf16[4,2,4544]{2,1,0:T(2,128)(2,1)S(1)}, bf16[4,2,4544]{2,1,0:T(2,128)(2,1)S(1)}, u32[]{:S(2)}, u32[]{:S(2)}) collective-permute-start(bf16[4,2,4544]{2,1,0:T(2,128)(2,1)S(1)} %pad_maximum_fusion.4), channel_id=1, source_target_pairs={{0,8},{1,9},{2,10},{3,11},{4,12},{5,13},{6,14},{7,15},{8,0},{9,1},... | collective-permute-start | bytes 218120 | tf_op jit(solution)/shard_map/ppermute | solution.py:93
  107.9 6.9 %collective-permute-done.2 = bf16[4,2,4544]{2,1,0:T(2,128)(2,1)S(1)} collective-permute-done((bf16[4,2,4544]{2,1,0:T(2,128)(2,1)S(1)}, bf16[4,2,4544]{2,1,0:T(2,128)(2,1)S(1)}, u32[]{:S(2)}, u32[]{:S(2)}) %collective-permute-start.2) | collective-permute-done | bytes 72736 | tf_op jit(solution)/shard_map/ppermute | solution.py:93
  115.2 5.2 %collective-permute-start.3 = (bf16[8,2,4544]{2,1,0:T(2,128)(2,1)S(1)}, bf16[8,2,4544]{2,1,0:T(2,128)(2,1)S(1)}, u32[]{:S(2)}, u32[]{:S(2)}) collective-permute-start(bf16[8,2,4544]{2,1,0:T(2,128)(2,1)S(1)} %pad_maximum_fusion.3), channel_id=1, source_target_pairs={{0,4},{1,5},{2,6},{3,7},{4,0},{5,1},{6,2},{7,3},{8,12},{9,13},{10,... | collective-permute-start | bytes 436232 | tf_op jit(solution)/shard_map/ppermute | solution.py:93
  120.4 5.8 %collective-permute-done.3 = bf16[8,2,4544]{2,1,0:T(2,128)(2,1)S(1)} collective-permute-done((bf16[8,2,4544]{2,1,0:T(2,128)(2,1)S(1)}, bf16[8,2,4544]{2,1,0:T(2,128)(2,1)S(1)}, u32[]{:S(2)}, u32[]{:S(2)}) %collective-permute-start.3) | collective-permute-done | bytes 145440 | tf_op jit(solution)/shard_map/ppermute | solution.py:93
  126.9 11.8 %collective-permute-start.4 = (bf16[16,2,4544]{2,1,0:T(2,128)(2,1)S(1)}, bf16[16,2,4544]{2,1,0:T(2,128)(2,1)S(1)}, u32[]{:S(2)}, u32[]{:S(2)}) collective-permute-start(bf16[16,2,4544]{2,1,0:T(2,128)(2,1)S(1)} %pad_maximum_fusion.2), channel_id=1, source_target_pairs={{0,2},{1,3},{2,0},{3,1},{4,6},{5,7},{6,4},{7,5},{8,10},{9,11},{10,... | collective-permute-start | bytes 872456 | tf_op jit(solution)/shard_map/ppermute | solution.py:93
  138.7 7.4 %collective-permute-done.4 = bf16[16,2,4544]{2,1,0:T(2,128)(2,1)S(1)} collective-permute-done((bf16[16,2,4544]{2,1,0:T(2,128)(2,1)S(1)}, bf16[16,2,4544]{2,1,0:T(2,128)(2,1)S(1)}, u32[]{:S(2)}, u32[]{:S(2)}) %collective-permute-start.4) | collective-permute-done | bytes 290848 | tf_op jit(solution)/shard_map/ppermute | solution.py:93
  146.8 0.8 pad_maximum_fusion.1
  147.5 1.9 collective-permute-start.5
  150.7 0.7 fusion.92
  151.5 7.8 %collective-permute-done.5 = bf16[32,2,4544]{2,1,0:T(2,128)(2,1)S(1)} collective-permute-done((bf16[32,2,4544]{2,1,0:T(2,128)(2,1)S(1)}, bf16[32,2,4544]{2,1,0:T(2,128)(2,1)S(1)}, u32[]{:S(2)}, u32[]{:S(2)}) %collective-permute-start.5) | collective-permute-done | bytes 581664 | tf_op jit(solution)/shard_map/ppermute | solution.py:93
  159.3 1.3 broadcast_select_fusion.1
  160.6 2.6 pad_maximum_fusion
  163.2 1.9 reshape.169
  165.6 1.8 fusion.133
  167.8 4.9 %fusion.36 = f32[128,4544]{0,1:T(8,128)} fusion(bf16[142,4544]{1,0:T(8,128)(2,1)S(1)} %copy-done, bf16[128,4544]{1,0:T(8,128)(2,1)S(1)} %reshape.169, bf16[4544,142]{0,1:T(8,128)(2,1)} %param.18), kind=kOutput, calls=%fused_computation.76 | convolution fusion | flops 331548416 | bytes 6070784 | tf_op jit(solution)/shard_map/dot_general | solution.py:182
  172.7 10.3 %all-gather.5.cloned.1.call-done = bf16[1,512,64,128]{3,2,0,1:T(8,128)(2,1)} async-done(((bf16[1,128,64,128]{3,2,0,1:T(8,128)(2,1)}), bf16[1,512,64,128]{3,2,0,1:T(8,128)(2,1)}) %all-gather.5.cloned.1.call-update) | async-done | bytes 8388624 | tf_op jit(solution)/shard_map/all_gather | solution.py:136
  183.1 37.5 %conditional.1 = (f32[128,64]{0,1:T(8,128)S(1)}, f32[128]{0:T(128)}, f32[128]{0:T(128)S(1)}) conditional(s32[]{:T(128)} %convert_element_type.47, () %tuple.13, (s32[]{:T(128)}, s32[1,32768]{1,0:T(1,128)S(1)}, bf16[1,512,64,128]{3,2,0,1:T(8,128)(2,1)}, bf16[128,64]{0,1:T(8,128)(2,1)S(1)}) %tuple.14), branch_computations={%region_2.3_spmd, %region_3.6_spmd} | conditional | flops 1103151872 | bytes 67361304 | solution.py:172
  183.3 1.1 compare_reduce_fusion
  184.3 11.5 %fusion.128 = (f32[128]{0:T(128)S(1)}, f32[128,32768]{1,0:T(8,128)}) fusion(bf16[128,64]{0,1:T(8,128)(2,1)S(1)} %get-tuple-element.37, bf16[32768,128]{1,0:T(8,128)(2,1)} %bitcast.70, pred[32768]{0:T(1024)(128)(4,1)S(1)} %compare_reduce_fusion), kind=kOutput, calls=%fused_computation.188 | convolution fusion | flops 549453696 | bytes 25215488 | tf_op jit(solution)/shard_map/cond/branch_1_fun/dot_general | solution.py:50
  195.9 8.2 %fusion.1 = f32[128]{0:T(128)S(1)} fusion(f32[128,32768]{1,0:T(8,128)} %get-tuple-element.45, f32[128]{0:T(128)S(1)} %get-tuple-element.44), kind=kLoop, calls=%fused_computation.3 | loop fusion | flops 8388480 | bytes 16778240 | tf_op jit(solution)/shard_map/cond/branch_1_fun/reduce_sum | solution.py:59
  205.3 15.1 %fusion.13 = f32[128,64]{0,1:T(8,128)S(1)} fusion(bf16[32768,128]{1,0:T(8,128)(2,1)} %bitcast.71, f32[128,32768]{1,0:T(8,128)} %get-tuple-element.45, f32[128]{0:T(128)S(1)} %get-tuple-element.44, f32[128]{0:T(128)S(1)} %get-tuple-element.39, f32[128]{0:T(128)S(1)} %exponential_multiply_fusion), kind=kOutput, calls=%fused_computation.10 | convolution fusion | flops 545275904 | bytes 25200128 | tf_op jit(solution)/shard_map/cond/branch_1_fun/dot_general | solution.py:57
  221.2 3.7 %convolution_add_fusion = f32[128,4544]{0,1:T(8,128)} fusion(f32[128,4544]{0,1:T(8,128)} %fusion.36, bf16[64,4544]{1,0:T(8,128)(2,1)S(1)} %copy-done.1, f32[128,128]{0,1:T(8,128)S(1)} %get-tuple-element.65, f32[128]{0:T(128)S(1)} %get-tuple-element.64, f32[128,64]{0,1:T(8,128)S(1)} %get-tuple-element.23, f32[128,128]{0,1:T(8,128)S(1)} %fusion.133, ...), kind=kOutput, calls=%fused_computation.16 | convolution fusion | flops 77201408 | bytes 5359616 | tf_op jit(solution)/shard_map/dot_general | solution.py:182
  224.9 3.1 copy.19
  228.1 3.7 %reshape_reshape.3 = f32[2,2,2,2,2,2,2,4544]{7,6,5,4,3,2,1,0:T(2,128)} reshape(f32[128,4544]{1,0:T(8,128)} %copy.19) | data formatting | bytes 4653056 | tf_op jit(solution)/shard_map/reshape;reshape | solution.py:104
  231.8 1.4 dynamic-slice_bitcast_fusion
  233.1 3.5 collective-permute-start.6
  236.6 26.1 %collective-permute-done.6 = f32[2,2,2,2,2,2,4544]{6,5,4,3,2,1,0:T(2,128)} collective-permute-done((f32[2,2,2,2,2,2,4544]{6,5,4,3,2,1,0:T(2,128)S(1)}, f32[2,2,2,2,2,2,4544]{6,5,4,3,2,1,0:T(2,128)}, u32[]{:S(2)}, u32[]{:S(2)}) %collective-permute-start.6) | collective-permute-done | bytes 1163296 | tf_op jit(solution)/shard_map/ppermute | solution.py:109
  262.7 2.2 bitcast_add_fusion
  265.0 4.5 %collective-permute-start.7 = (f32[2,2,2,2,2,4544]{5,4,3,2,1,0:T(2,128)S(1)}, f32[2,2,2,2,2,4544]{5,4,3,2,1,0:T(2,128)}, u32[]{:S(2)}, u32[]{:S(2)}) collective-permute-start(f32[2,2,2,2,2,4544]{5,4,3,2,1,0:T(2,128)S(1)} %dynamic-slice_bitcast_fusion.1), channel_id=1, source_target_pairs={{0,2},{1,3},{2,0},{3,1},{4,6},{5,7},{6,4},{7,5},{8,10},{9,11},{10,... | collective-permute-start | bytes 1744904 | tf_op jit(solution)/shard_map/ppermute | solution.py:109
  269.4 25.1 %collective-permute-done.7 = f32[2,2,2,2,2,4544]{5,4,3,2,1,0:T(2,128)} collective-permute-done((f32[2,2,2,2,2,4544]{5,4,3,2,1,0:T(2,128)S(1)}, f32[2,2,2,2,2,4544]{5,4,3,2,1,0:T(2,128)}, u32[]{:S(2)}, u32[]{:S(2)}) %collective-permute-start.7) | collective-permute-done | bytes 581664 | tf_op jit(solution)/shard_map/ppermute | solution.py:109
  294.5 1.4 bitcast_add_fusion.1
  296.0 7.6 %collective-permute-start.8 = (f32[2,2,2,2,4544]{4,3,2,1,0:T(2,128)S(1)}, f32[2,2,2,2,4544]{4,3,2,1,0:T(2,128)S(1)}, u32[]{:S(2)}, u32[]{:S(2)}) collective-permute-start(f32[2,2,2,2,4544]{4,3,2,1,0:T(2,128)S(1)} %dynamic-slice_bitcast_fusion.2), channel_id=1, source_target_pairs={{0,4},{1,5},{2,6},{3,7},{4,0},{5,1},{6,2},{7,3},{8,12},{9,13},{10,... | collective-permute-start | bytes 872456 | tf_op jit(solution)/shard_map/ppermute | solution.py:109
  303.6 24.0 %collective-permute-done.8 = f32[2,2,2,2,4544]{4,3,2,1,0:T(2,128)S(1)} collective-permute-done((f32[2,2,2,2,4544]{4,3,2,1,0:T(2,128)S(1)}, f32[2,2,2,2,4544]{4,3,2,1,0:T(2,128)S(1)}, u32[]{:S(2)}, u32[]{:S(2)}) %collective-permute-start.8) | collective-permute-done | bytes 290848 | tf_op jit(solution)/shard_map/ppermute | solution.py:109
  327.8 14.6 %collective-permute-start.9 = (f32[2,2,2,4544]{3,2,1,0:T(2,128)S(1)}, f32[2,2,2,4544]{3,2,1,0:T(2,128)S(1)}, u32[]{:S(2)}, u32[]{:S(2)}) collective-permute-start(f32[2,2,2,4544]{3,2,1,0:T(2,128)S(1)} %dynamic-slice_bitcast_fusion.3), channel_id=1, source_target_pairs={{0,8},{1,9},{2,10},{3,11},{4,12},{5,13},{6,14},{7,15},{8,0},{9,1},... | collective-permute-start | bytes 436232 | tf_op jit(solution)/shard_map/ppermute | solution.py:109
  342.5 4.3 %collective-permute-done.9 = f32[2,2,2,4544]{3,2,1,0:T(2,128)S(1)} collective-permute-done((f32[2,2,2,4544]{3,2,1,0:T(2,128)S(1)}, f32[2,2,2,4544]{3,2,1,0:T(2,128)S(1)}, u32[]{:S(2)}, u32[]{:S(2)}) %collective-permute-start.9) | collective-permute-done | bytes 145440 | tf_op jit(solution)/shard_map/ppermute | solution.py:109
  346.9 2.4 collective-permute-start.10
  349.3 3.8 %collective-permute-done.10 = f32[2,2,4544]{2,1,0:T(2,128)S(1)} collective-permute-done((f32[2,2,4544]{2,1,0:T(2,128)S(1)}, f32[2,2,4544]{2,1,0:T(2,128)S(1)}, u32[]{:S(2)}, u32[]{:S(2)}) %collective-permute-start.10) | collective-permute-done | bytes 72736 | tf_op jit(solution)/shard_map/ppermute | solution.py:109
  353.2 3.1 collective-permute-start.11
  356.3 4.3 %collective-permute-done.11 = f32[2,4544]{1,0:T(2,128)S(1)} collective-permute-done((f32[2,4544]{1,0:T(2,128)S(1)}, f32[2,4544]{1,0:T(2,128)S(1)}, u32[]{:S(2)}, u32[]{:S(2)}) %collective-permute-start.11) | collective-permute-done | bytes 36384 | tf_op jit(solution)/shard_map/ppermute | solution.py:109
  (52 shorter events, 6.7 us)
Async XLA Ops:
  6.5 161.2 %copy-start = (bf16[142,4544]{1,0:T(8,128)(2,1)S(1)}, bf16[142,4544]{1,0:T(8,128)(2,1)}, u32[]{:S(2)}) copy-start(bf16[142,4544]{1,0:T(8,128)(2,1)} %param.19) | copy-start | bytes 3871492
  6.5 86.7 %copy-start.3 = (bf16[1,2,4544]{2,1,0:T(2,128)(2,1)S(1)}, bf16[1,2,4544]{2,1,0:T(2,128)(2,1)}, u32[]{:S(2)}) copy-start(bf16[1,2,4544]{2,1,0:T(2,128)(2,1)} %param.12) | copy-start | bytes 54532
  6.5 86.7 %copy-start.4 = (f32[4544]{0:T(1024)S(1)}, f32[4544]{0:T(1024)}, u32[]{:S(2)}) copy-start(f32[4544]{0:T(1024)} %param.14) | copy-start | bytes 54532
  6.5 86.8 %copy-start.5 = (f32[4544]{0:T(1024)S(1)}, f32[4544]{0:T(1024)}, u32[]{:S(2)}) copy-start(f32[4544]{0:T(1024)} %param.13) | copy-start | bytes 54532
  6.5 86.7 %all-gather.3.cloned.1.call-start = ((), (), s32[]{:S(2)}) async-start(), calls=%async_computation.1 | async-start | bytes 2228224 | tf_op jit(solution)/shard_map/all_gather | solution.py:135
  18.0 165.0 %all-gather.5.cloned.1.call-start = ((), (), s32[]{:S(2)}) async-start(), calls=%async_computation.2 | async-start | bytes 10485760 | tf_op jit(solution)/shard_map/all_gather | solution.py:136
  20.7 72.5 %collective-permute-start = (bf16[1,2,4544]{2,1,0:T(2,128)(2,1)S(1)}, bf16[1,2,4544]{2,1,0:T(2,128)(2,1)S(1)}, u32[]{:S(2)}, u32[]{:S(2)}) collective-permute-start(bf16[1,2,4544]{2,1,0:T(2,128)(2,1)S(1)} %fusion.44), channel_id=1, source_target_pairs={{0,32},{1,33},{2,34},{3,35},{4,36},{5,37},{6,38},{7,39},{8,40},{9,... | collective-permute-start | bytes 54536 | tf_op jit(solution)/shard_map/ppermute | solution.py:93
  93.5 5.9 %collective-permute-start.1 = (bf16[2,2,4544]{2,1,0:T(2,128)(2,1)S(1)}, bf16[2,2,4544]{2,1,0:T(2,128)(2,1)S(1)}, u32[]{:S(2)}, u32[]{:S(2)}) collective-permute-start(bf16[2,2,4544]{2,1,0:T(2,128)(2,1)S(1)} %pad_maximum_fusion.5), channel_id=1, source_target_pairs={{0,16},{1,17},{2,18},{3,19},{4,20},{5,21},{6,22},{7,23},{8,24},{9,... | collective-permute-start | bytes 109064 | tf_op jit(solution)/shard_map/ppermute | solution.py:93
  99.5 49.9 %copy-start.6 = (s32[8]{0:T(128)S(1)}, s32[8]{0:T(128)}, u32[]{:S(2)}) copy-start(s32[8]{0:T(128)} %param.21) | copy-start | bytes 100
  99.6 15.3 %collective-permute-start.2 = (bf16[4,2,4544]{2,1,0:T(2,128)(2,1)S(1)}, bf16[4,2,4544]{2,1,0:T(2,128)(2,1)S(1)}, u32[]{:S(2)}, u32[]{:S(2)}) collective-permute-start(bf16[4,2,4544]{2,1,0:T(2,128)(2,1)S(1)} %pad_maximum_fusion.4), channel_id=1, source_target_pairs={{0,8},{1,9},{2,10},{3,11},{4,12},{5,13},{6,14},{7,15},{8,0},{9,1},... | collective-permute-start | bytes 218120 | tf_op jit(solution)/shard_map/ppermute | solution.py:93
  115.2 11.0 %collective-permute-start.3 = (bf16[8,2,4544]{2,1,0:T(2,128)(2,1)S(1)}, bf16[8,2,4544]{2,1,0:T(2,128)(2,1)S(1)}, u32[]{:S(2)}, u32[]{:S(2)}) collective-permute-start(bf16[8,2,4544]{2,1,0:T(2,128)(2,1)S(1)} %pad_maximum_fusion.3), channel_id=1, source_target_pairs={{0,4},{1,5},{2,6},{3,7},{4,0},{5,1},{6,2},{7,3},{8,12},{9,13},{10,... | collective-permute-start | bytes 436232 | tf_op jit(solution)/shard_map/ppermute | solution.py:93
  126.9 19.2 %collective-permute-start.4 = (bf16[16,2,4544]{2,1,0:T(2,128)(2,1)S(1)}, bf16[16,2,4544]{2,1,0:T(2,128)(2,1)S(1)}, u32[]{:S(2)}, u32[]{:S(2)}) collective-permute-start(bf16[16,2,4544]{2,1,0:T(2,128)(2,1)S(1)} %pad_maximum_fusion.2), channel_id=1, source_target_pairs={{0,2},{1,3},{2,0},{3,1},{4,6},{5,7},{6,4},{7,5},{8,10},{9,11},{10,... | collective-permute-start | bytes 872456 | tf_op jit(solution)/shard_map/ppermute | solution.py:93
  147.5 11.8 %collective-permute-start.5 = (bf16[32,2,4544]{2,1,0:T(2,128)(2,1)S(1)}, bf16[32,2,4544]{2,1,0:T(2,128)(2,1)S(1)}, u32[]{:S(2)}, u32[]{:S(2)}) collective-permute-start(bf16[32,2,4544]{2,1,0:T(2,128)(2,1)S(1)} %pad_maximum_fusion.1), channel_id=1, source_target_pairs={{0,1},{1,0},{2,3},{3,2},{4,5},{5,4},{6,7},{7,6},{8,9},{9,8},{10,11... | collective-permute-start | bytes 1744904 | tf_op jit(solution)/shard_map/ppermute | solution.py:93
  160.6 4.5 %copy-start.2 = (bf16[4544,64]{0,1:T(8,128)(2,1)S(1)}, bf16[4544,64]{0,1:T(8,128)(2,1)}, u32[]{:S(2)}) copy-start(bf16[4544,64]{0,1:T(8,128)(2,1)} %param.15) | copy-start | bytes 1744900
  183.1 38.1 %copy-start.1 = (bf16[64,4544]{1,0:T(8,128)(2,1)S(1)}, bf16[64,4544]{1,0:T(8,128)(2,1)}, u32[]{:S(2)}) copy-start(bf16[64,4544]{1,0:T(8,128)(2,1)} %param.17) | copy-start | bytes 1744900
  233.1 29.5 %collective-permute-start.6 = (f32[2,2,2,2,2,2,4544]{6,5,4,3,2,1,0:T(2,128)S(1)}, f32[2,2,2,2,2,2,4544]{6,5,4,3,2,1,0:T(2,128)}, u32[]{:S(2)}, u32[]{:S(2)}) collective-permute-start(f32[2,2,2,2,2,2,4544]{6,5,4,3,2,1,0:T(2,128)S(1)} %dynamic-slice_bitcast_fusion), channel_id=1, source_target_pairs={{0,1},{1,0},{2,3},{3,2},{4,5},{5,4},{6,7},{7,6},{8,9},{9,8},{10,11... | collective-permute-start | bytes 3489800 | tf_op jit(solution)/shard_map/ppermute | solution.py:109
  265.0 29.6 %collective-permute-start.7 = (f32[2,2,2,2,2,4544]{5,4,3,2,1,0:T(2,128)S(1)}, f32[2,2,2,2,2,4544]{5,4,3,2,1,0:T(2,128)}, u32[]{:S(2)}, u32[]{:S(2)}) collective-permute-start(f32[2,2,2,2,2,4544]{5,4,3,2,1,0:T(2,128)S(1)} %dynamic-slice_bitcast_fusion.1), channel_id=1, source_target_pairs={{0,2},{1,3},{2,0},{3,1},{4,6},{5,7},{6,4},{7,5},{8,10},{9,11},{10,... | collective-permute-start | bytes 1744904 | tf_op jit(solution)/shard_map/ppermute | solution.py:109
  296.0 31.7 %collective-permute-start.8 = (f32[2,2,2,2,4544]{4,3,2,1,0:T(2,128)S(1)}, f32[2,2,2,2,4544]{4,3,2,1,0:T(2,128)S(1)}, u32[]{:S(2)}, u32[]{:S(2)}) collective-permute-start(f32[2,2,2,2,4544]{4,3,2,1,0:T(2,128)S(1)} %dynamic-slice_bitcast_fusion.2), channel_id=1, source_target_pairs={{0,4},{1,5},{2,6},{3,7},{4,0},{5,1},{6,2},{7,3},{8,12},{9,13},{10,... | collective-permute-start | bytes 872456 | tf_op jit(solution)/shard_map/ppermute | solution.py:109
  327.8 19.0 %collective-permute-start.9 = (f32[2,2,2,4544]{3,2,1,0:T(2,128)S(1)}, f32[2,2,2,4544]{3,2,1,0:T(2,128)S(1)}, u32[]{:S(2)}, u32[]{:S(2)}) collective-permute-start(f32[2,2,2,4544]{3,2,1,0:T(2,128)S(1)} %dynamic-slice_bitcast_fusion.3), channel_id=1, source_target_pairs={{0,8},{1,9},{2,10},{3,11},{4,12},{5,13},{6,14},{7,15},{8,0},{9,1},... | collective-permute-start | bytes 436232 | tf_op jit(solution)/shard_map/ppermute | solution.py:109
  346.9 6.2 %collective-permute-start.10 = (f32[2,2,4544]{2,1,0:T(2,128)S(1)}, f32[2,2,4544]{2,1,0:T(2,128)S(1)}, u32[]{:S(2)}, u32[]{:S(2)}) collective-permute-start(f32[2,2,4544]{2,1,0:T(2,128)S(1)} %dynamic-slice_bitcast_fusion.4), channel_id=1, source_target_pairs={{0,16},{1,17},{2,18},{3,19},{4,20},{5,21},{6,22},{7,23},{8,24},{9,... | collective-permute-start | bytes 218120 | tf_op jit(solution)/shard_map/ppermute | solution.py:109
  353.2 7.4 %collective-permute-start.11 = (f32[2,4544]{1,0:T(2,128)S(1)}, f32[2,4544]{1,0:T(2,128)S(1)}, u32[]{:S(2)}, u32[]{:S(2)}) collective-permute-start(f32[2,4544]{1,0:T(2,128)S(1)} %dynamic-slice_bitcast_fusion.5), channel_id=1, source_target_pairs={{0,32},{1,33},{2,34},{3,35},{4,36},{5,37},{6,38},{7,39},{8,40},{9,... | collective-permute-start | bytes 109064 | tf_op jit(solution)/shard_map/ppermute | solution.py:109
Sparse Core Ops, SparseCore 0:
  18.1 75.0 all-gather.2
  95.3 87.6 all-gather.4

commit v2 on v1

--- a/solution.py
+++ b/solution.py
@@ -85,11 +85,24 @@
     return out
 
 
+def round_bits(n):
+    bits = n.bit_length() - 1
+    low = lax.axis_size("tz").bit_length() - 1
+    return list(reversed(range(low))) + list(reversed(range(low, bits)))
+
+
+def layout_source(index, n):
+    order = round_bits(n)
+    out = jnp.zeros_like(index)
+    for place, b in enumerate(order):
+        out = out | (((index >> place) & 1) << b)
+    return out
+
+
 def gather_rounds(piece, n):
-    bits = n.bit_length() - 1
     me = tensor_index()
     buf = piece[None]
-    for b in reversed(range(bits)):
+    for b in round_bits(n):
         other = lax.ppermute(buf, TENSOR, [(i, i ^ (1 << b)) for i in range(n)])
         low = ((me >> b) & 1) == 0
         buf = jnp.concatenate(
@@ -102,11 +115,14 @@
     bits = n.bit_length() - 1
     me = tensor_index()
     buf = partial.reshape((2,) * bits + partial.shape[1:])
-    for b in range(bits):
+    for b in reversed(round_bits(n)):
         mine = (me >> b) & 1
         keep = lax.dynamic_index_in_dim(buf, mine, 0, keepdims=False)
         send = lax.dynamic_index_in_dim(buf, 1 - mine, 0, keepdims=False)
-        buf = keep + lax.ppermute(send, TENSOR, [(i, i ^ (1 << b)) for i in range(n)])
+        moved = lax.ppermute(
+            send.astype(jnp.bfloat16), TENSOR, [(i, i ^ (1 << b)) for i in range(n)]
+        )
+        buf = keep + moved.astype(jnp.float32)
     return buf
 
 
@@ -148,7 +164,7 @@
     )
     span = projected.shape[0]
     row = jnp.arange(span, dtype=jnp.int32)
-    token_pos = bit_reversed(row // per_device, bits) * per_device + row % per_device
+    token_pos = layout_source(row // per_device, n) * per_device + row % per_device
     group = lax.axis_index("dp")
     own_length = lax.dynamic_index_in_dim(cache_lengths, group, 0, keepdims=False)
     places = own_length + token_pos

time: 369 us -> 330 us (0.89)
  the two profiles are of different devices: /device:TPU:2 before, /device:TPU:10 now
where the time goes in v2:
time: 330 us; the launch traced here: 329 us
  waiting for transfers between devices  168 us (51%)
  starting transfers between devices  61.6 us (19%)
  matrix products  37.8 us (11%)
  other arithmetic  24.5 us (7%)
  between operations  14.5 us (4%)
  local copies, waits for them, and re-layouts  12.2 us (4%)
  blocking collectives  9.7 us (3%)
    all_gather x1, waiting for transfers between devices, local(): gathered = lax.all_gather(mine, 'tz', axis=1, tiled=True)  57.7 us
    ppermute x6, waiting for transfers between devices, gather_rounds(): other = lax.ppermute(buf, TENSOR, [(i, i ^ 1 << b) for i in range(n)])  45.9 us
    ppermute x6, waiting for transfers between devices, scatter_rounds(): lax.ppermute(send.astype(jnp.bfloat16), TENSOR, [(i, i ^ 1 << b) for i in...  42.6 us
    ppermute x6, starting transfers between devices, gather_rounds(): other = lax.ppermute(buf, TENSOR, [(i, i ^ 1 << b) for i in range(n)])  36.2 us
    ppermute x6, starting transfers between devices, scatter_rounds(): lax.ppermute(send.astype(jnp.bfloat16), TENSOR, [(i, i ^ 1 << b) for i in...  25.3 us
    all_gather x1, waiting for transfers between devices, local(): gathered = lax.all_gather(gathered, 'tx', axis=1, tiled=True)  21.7 us
    dot_general x1, matrix products, absorb(): jnp.dot(weights.astype(jnp.bfloat16), value_rows, preferred_element_type=...  15.1 us
    dot_general x2, matrix products, absorb(): jnp.dot(queries, key_rows.T, preferred_element_type=jnp.float32)  11.8 us
  transfers between devices with their start and end apart: 14, of which 13 were waited for; matrix products, arithmetic and copies ran while one was open for 6% of the time, Pallas kernels for 0%

profile of v2, /device:TPU:10, one launch (start us, length us, event | category | flops | bytes accessed | tf_op | source)
XLA Modules:
  0.0 328.6 jit_solution(1418473626582980948)
XLA Ops:
  6.6 9.7 %all_to_all.18 = bf16[8,8,8,128]{3,2,1,0:T(8,128)(2,1)S(1)} all-to-all(bf16[8,8,8,128]{3,2,1,0:T(8,128)(2,1)} %param.20), channel_id=1, replica_groups=mesh['dp'=8,'tx'=4,'tz'=16] {'dp'}, dimensions={0} | all-to-all | bytes 262144 | tf_op jit(solution)/shard_map/all_to_all | solution.py:149
  16.3 0.7 copy_bitcast_fusion
  17.0 0.9 convert_reduce_fusion
  17.9 0.9 fusion.43
  18.9 0.9 fusion.48
  19.7 15.7 %collective-permute-start = (bf16[1,2,4544]{2,1,0:T(2,128)(2,1)S(1)}, bf16[1,2,4544]{2,1,0:T(2,128)(2,1)S(1)}, u32[]{:S(2)}, u32[]{:S(2)}) collective-permute-start(bf16[1,2,4544]{2,1,0:T(2,128)(2,1)S(1)} %fusion.48), channel_id=1, source_target_pairs={{0,8},{1,9},{2,10},{3,11},{4,12},{5,13},{6,14},{7,15},{8,0},{9,1},... | collective-permute-start | bytes 54536 | tf_op jit(solution)/shard_map/ppermute | solution.py:106
  35.5 57.7 %all-gather.3.cloned.1.call-done = bf16[1,128,64,128]{3,2,0,1:T(8,128)(2,1)} async-done(((bf16[1,8,64,128]{3,2,0,1:T(8,128)(2,1)}), bf16[1,128,64,128]{3,2,0,1:T(8,128)(2,1)}) %all-gather.3.cloned.1.call-update) | async-done | bytes 2097168 | tf_op jit(solution)/shard_map/all_gather | solution.py:151
  93.4 6.1 %collective-permute-start.1 = (bf16[2,2,4544]{2,1,0:T(2,128)(2,1)S(1)}, bf16[2,2,4544]{2,1,0:T(2,128)(2,1)S(1)}, u32[]{:S(2)}, u32[]{:S(2)}) collective-permute-start(bf16[2,2,4544]{2,1,0:T(2,128)(2,1)S(1)} %pad_maximum_fusion.5), channel_id=1, source_target_pairs={{0,4},{1,5},{2,6},{3,7},{4,0},{5,1},{6,2},{7,3},{8,12},{9,13},{10,... | collective-permute-start | bytes 109064 | tf_op jit(solution)/shard_map/ppermute | solution.py:106
  99.5 3.7 %collective-permute-done.1 = bf16[2,2,4544]{2,1,0:T(2,128)(2,1)S(1)} collective-permute-done((bf16[2,2,4544]{2,1,0:T(2,128)(2,1)S(1)}, bf16[2,2,4544]{2,1,0:T(2,128)(2,1)S(1)}, u32[]{:S(2)}, u32[]{:S(2)}) %collective-permute-start.1) | collective-permute-done | bytes 36384 | tf_op jit(solution)/shard_map/ppermute | solution.py:106
  103.4 3.9 %collective-permute-start.2 = (bf16[4,2,4544]{2,1,0:T(2,128)(2,1)S(1)}, bf16[4,2,4544]{2,1,0:T(2,128)(2,1)S(1)}, u32[]{:S(2)}, u32[]{:S(2)}) collective-permute-start(bf16[4,2,4544]{2,1,0:T(2,128)(2,1)S(1)} %pad_maximum_fusion.4), channel_id=1, source_target_pairs={{0,2},{1,3},{2,0},{3,1},{4,6},{5,7},{6,4},{7,5},{8,10},{9,11},{10,... | collective-permute-start | bytes 218120 | tf_op jit(solution)/shard_map/ppermute | solution.py:106
  107.3 3.2 collective-permute-done.2
  110.9 4.1 %collective-permute-start.3 = (bf16[8,2,4544]{2,1,0:T(2,128)(2,1)S(1)}, bf16[8,2,4544]{2,1,0:T(2,128)(2,1)S(1)}, u32[]{:S(2)}, u32[]{:S(2)}) collective-permute-start(bf16[8,2,4544]{2,1,0:T(2,128)(2,1)S(1)} %pad_maximum_fusion.3), channel_id=1, source_target_pairs={{0,1},{1,0},{2,3},{3,2},{4,5},{5,4},{6,7},{7,6},{8,9},{9,8},{10,11... | collective-permute-start | bytes 436232 | tf_op jit(solution)/shard_map/ppermute | solution.py:106
  115.0 3.1 collective-permute-done.3
  118.8 4.0 %collective-permute-start.4 = (bf16[16,2,4544]{2,1,0:T(2,128)(2,1)S(1)}, bf16[16,2,4544]{2,1,0:T(2,128)(2,1)S(1)}, u32[]{:S(2)}, u32[]{:S(2)}) collective-permute-start(bf16[16,2,4544]{2,1,0:T(2,128)(2,1)S(1)} %pad_maximum_fusion.2), channel_id=1, source_target_pairs={{0,32},{1,33},{2,34},{3,35},{4,36},{5,37},{6,38},{7,39},{8,40},{9,... | collective-permute-start | bytes 872456 | tf_op jit(solution)/shard_map/ppermute | solution.py:106
  122.8 14.7 %collective-permute-done.4 = bf16[16,2,4544]{2,1,0:T(2,128)(2,1)S(1)} collective-permute-done((bf16[16,2,4544]{2,1,0:T(2,128)(2,1)S(1)}, bf16[16,2,4544]{2,1,0:T(2,128)(2,1)S(1)}, u32[]{:S(2)}, u32[]{:S(2)}) %collective-permute-start.4) | collective-permute-done | bytes 290848 | tf_op jit(solution)/shard_map/ppermute | solution.py:106
  137.5 0.7 broadcast_select_fusion.3
  138.2 0.8 pad_maximum_fusion.1
  138.9 2.4 collective-permute-start.5
  142.6 0.7 fusion.98
  143.4 21.2 %collective-permute-done.5 = bf16[32,2,4544]{2,1,0:T(2,128)(2,1)S(1)} collective-permute-done((bf16[32,2,4544]{2,1,0:T(2,128)(2,1)S(1)}, bf16[32,2,4544]{2,1,0:T(2,128)(2,1)S(1)}, u32[]{:S(2)}, u32[]{:S(2)}) %collective-permute-start.5) | collective-permute-done | bytes 581664 | tf_op jit(solution)/shard_map/ppermute | solution.py:106
  164.6 1.3 broadcast_select_fusion.1
  165.9 2.6 pad_maximum_fusion
  168.5 1.9 reshape.175
  171.0 1.8 fusion.139
  173.1 4.9 %fusion.40 = f32[128,4544]{0,1:T(8,128)} fusion(bf16[142,4544]{1,0:T(8,128)(2,1)S(1)} %copy-done, bf16[128,4544]{1,0:T(8,128)(2,1)S(1)} %reshape.175, bf16[4544,142]{0,1:T(8,128)(2,1)} %param.18), kind=kOutput, calls=%fused_computation.80 | convolution fusion | flops 331548416 | bytes 6070784 | tf_op jit(solution)/shard_map/dot_general | solution.py:198
  178.0 21.7 %all-gather.5.cloned.1.call-done = bf16[1,512,64,128]{3,2,0,1:T(8,128)(2,1)} async-done(((bf16[1,128,64,128]{3,2,0,1:T(8,128)(2,1)}), bf16[1,512,64,128]{3,2,0,1:T(8,128)(2,1)}) %all-gather.5.cloned.1.call-update) | async-done | bytes 8388624 | tf_op jit(solution)/shard_map/all_gather | solution.py:152
  199.8 37.5 %conditional.1 = (f32[128,64]{0,1:T(8,128)S(1)}, f32[128]{0:T(128)}, f32[128]{0:T(128)S(1)}) conditional(s32[]{:T(128)} %convert_element_type.101, () %tuple.13, (s32[]{:T(128)}, s32[1,32768]{1,0:T(1,128)S(1)}, bf16[1,512,64,128]{3,2,0,1:T(8,128)(2,1)}, bf16[128,64]{0,1:T(8,128)(2,1)S(1)}) %tuple.14), branch_computations={%region_2.3_spmd, %region_3.6_spmd} | conditional | flops 1103151872 | bytes 67361304 | solution.py:188
  200.0 1.1 compare_reduce_fusion
  201.1 11.5 %fusion.134 = (f32[128]{0:T(128)S(1)}, f32[128,32768]{1,0:T(8,128)}) fusion(bf16[128,64]{0,1:T(8,128)(2,1)S(1)} %get-tuple-element.37, bf16[32768,128]{1,0:T(8,128)(2,1)} %bitcast.70, pred[32768]{0:T(1024)(128)(4,1)S(1)} %compare_reduce_fusion), kind=kOutput, calls=%fused_computation.194 | convolution fusion | flops 549453696 | bytes 25215488 | tf_op jit(solution)/shard_map/cond/branch_1_fun/dot_general | solution.py:50
  212.6 8.2 %fusion.1 = f32[128]{0:T(128)S(1)} fusion(f32[128,32768]{1,0:T(8,128)} %get-tuple-element.45, f32[128]{0:T(128)S(1)} %get-tuple-element.44), kind=kLoop, calls=%fused_computation.3 | loop fusion | flops 8388480 | bytes 16778240 | tf_op jit(solution)/shard_map/cond/branch_1_fun/reduce_sum | solution.py:59
  222.0 15.1 %fusion.13 = f32[128,64]{0,1:T(8,128)S(1)} fusion(bf16[32768,128]{1,0:T(8,128)(2,1)} %bitcast.71, f32[128,32768]{1,0:T(8,128)} %get-tuple-element.45, f32[128]{0:T(128)S(1)} %get-tuple-element.44, f32[128]{0:T(128)S(1)} %get-tuple-element.39, f32[128]{0:T(128)S(1)} %exponential_multiply_fusion), kind=kOutput, calls=%fused_computation.10 | convolution fusion | flops 545275904 | bytes 25200128 | tf_op jit(solution)/shard_map/cond/branch_1_fun/dot_general | solution.py:57
  237.9 3.7 %convolution_add_fusion = f32[128,4544]{0,1:T(8,128)} fusion(f32[128,4544]{0,1:T(8,128)} %fusion.40, bf16[64,4544]{1,0:T(8,128)(2,1)S(1)} %copy-done.1, f32[128,128]{0,1:T(8,128)S(1)} %get-tuple-element.65, f32[128]{0:T(128)S(1)} %get-tuple-element.64, f32[128,64]{0,1:T(8,128)S(1)} %get-tuple-element.23, f32[128,128]{0,1:T(8,128)S(1)} %fusion.139, ...), kind=kOutput, calls=%fused_computation.16 | convolution fusion | flops 77201408 | bytes 5359616 | tf_op jit(solution)/shard_map/dot_general | solution.py:198
  241.7 3.1 copy.21
  244.8 3.7 %reshape_reshape.3 = f32[2,2,2,2,2,2,2,4544]{7,6,5,4,3,2,1,0:T(2,128)} reshape(f32[128,4544]{1,0:T(8,128)} %copy.21) | data formatting | bytes 4653056 | tf_op jit(solution)/shard_map/reshape;reshape | solution.py:117
  248.5 1.7 fusion.22
  250.2 2.5 collective-permute-start.6
  252.6 14.5 %collective-permute-done.6 = bf16[2,2,2,2,2,2,4544]{6,5,4,3,2,1,0:T(2,128)(2,1)S(1)} collective-permute-done((bf16[2,2,2,2,2,2,4544]{6,5,4,3,2,1,0:T(2,128)(2,1)S(1)}, bf16[2,2,2,2,2,2,4544]{6,5,4,3,2,1,0:T(2,128)(2,1)S(1)}, u32[]{:S(2)}, u32[]{:S(2)}) %collective-permute-start.6) | collective-permute-done | bytes 581664 | tf_op jit(solution)/shard_map/ppermute | solution.py:122
  267.2 1.9 bitcast_add_fusion
  269.3 2.2 collective-permute-start.7
  271.5 9.2 %collective-permute-done.7 = bf16[2,2,2,2,2,4544]{5,4,3,2,1,0:T(2,128)(2,1)S(1)} collective-permute-done((bf16[2,2,2,2,2,4544]{5,4,3,2,1,0:T(2,128)(2,1)S(1)}, bf16[2,2,2,2,2,4544]{5,4,3,2,1,0:T(2,128)(2,1)S(1)}, u32[]{:S(2)}, u32[]{:S(2)}) %collective-permute-start.7) | collective-permute-done | bytes 290848 | tf_op jit(solution)/shard_map/ppermute | solution.py:122
  281.1 2.2 collective-permute-start.8
  283.3 4.8 %collective-permute-done.8 = bf16[2,2,2,2,4544]{4,3,2,1,0:T(2,128)(2,1)S(1)} collective-permute-done((bf16[2,2,2,2,4544]{4,3,2,1,0:T(2,128)(2,1)S(1)}, bf16[2,2,2,2,4544]{4,3,2,1,0:T(2,128)(2,1)S(1)}, u32[]{:S(2)}, u32[]{:S(2)}) %collective-permute-start.8) | collective-permute-done | bytes 145440 | tf_op jit(solution)/shard_map/ppermute | solution.py:122
  288.3 3.2 collective-permute-start.9
  291.5 4.5 %collective-permute-done.9 = bf16[2,2,2,4544]{3,2,1,0:T(2,128)(2,1)S(1)} collective-permute-done((bf16[2,2,2,4544]{3,2,1,0:T(2,128)(2,1)S(1)}, bf16[2,2,2,4544]{3,2,1,0:T(2,128)(2,1)S(1)}, u32[]{:S(2)}, u32[]{:S(2)}) %collective-permute-start.9) | collective-permute-done | bytes 72736 | tf_op jit(solution)/shard_map/ppermute | solution.py:122
  296.1 4.8 %collective-permute-start.10 = (bf16[2,2,4544]{2,1,0:T(2,128)(2,1)S(1)}, bf16[2,2,4544]{2,1,0:T(2,128)(2,1)S(1)}, u32[]{:S(2)}, u32[]{:S(2)}) collective-permute-start(bf16[2,2,4544]{2,1,0:T(2,128)(2,1)S(1)} %fusion.49), channel_id=1, source_target_pairs={{0,4},{1,5},{2,6},{3,7},{4,0},{5,1},{6,2},{7,3},{8,12},{9,13},{10,... | collective-permute-start | bytes 109064 | tf_op jit(solution)/shard_map/ppermute | solution.py:122
  300.9 5.8 %collective-permute-done.10 = bf16[2,2,4544]{2,1,0:T(2,128)(2,1)S(1)} collective-permute-done((bf16[2,2,4544]{2,1,0:T(2,128)(2,1)S(1)}, bf16[2,2,4544]{2,1,0:T(2,128)(2,1)S(1)}, u32[]{:S(2)}, u32[]{:S(2)}) %collective-permute-start.10) | collective-permute-done | bytes 36384 | tf_op jit(solution)/shard_map/ppermute | solution.py:122
  306.7 10.5 %collective-permute-start.11 = (bf16[2,4544]{1,0:T(2,128)(2,1)S(1)}, bf16[2,4544]{1,0:T(2,128)(2,1)S(1)}, u32[]{:S(2)}, u32[]{:S(2)}) collective-permute-start(bf16[2,4544]{1,0:T(2,128)(2,1)S(1)} %fusion.91), channel_id=1, source_target_pairs={{0,8},{1,9},{2,10},{3,11},{4,12},{5,13},{6,14},{7,15},{8,0},{9,1},... | collective-permute-start | bytes 54536 | tf_op jit(solution)/shard_map/ppermute | solution.py:122
  317.3 3.8 %collective-permute-done.11 = bf16[2,4544]{1,0:T(2,128)(2,1)S(1)} collective-permute-done((bf16[2,4544]{1,0:T(2,128)(2,1)S(1)}, bf16[2,4544]{1,0:T(2,128)(2,1)S(1)}, u32[]{:S(2)}, u32[]{:S(2)}) %collective-permute-start.11) | collective-permute-done | bytes 18208 | tf_op jit(solution)/shard_map/ppermute | solution.py:122
  (52 shorter events, 6.7 us)
Async XLA Ops:
  6.5 166.6 %copy-start = (bf16[142,4544]{1,0:T(8,128)(2,1)S(1)}, bf16[142,4544]{1,0:T(8,128)(2,1)}, u32[]{:S(2)}) copy-start(bf16[142,4544]{1,0:T(8,128)(2,1)} %param.19) | copy-start | bytes 3871492
  6.5 86.7 %copy-start.3 = (bf16[1,2,4544]{2,1,0:T(2,128)(2,1)S(1)}, bf16[1,2,4544]{2,1,0:T(2,128)(2,1)}, u32[]{:S(2)}) copy-start(bf16[1,2,4544]{2,1,0:T(2,128)(2,1)} %param.12) | copy-start | bytes 54532
  6.5 86.7 %copy-start.4 = (f32[4544]{0:T(1024)S(1)}, f32[4544]{0:T(1024)}, u32[]{:S(2)}) copy-start(f32[4544]{0:T(1024)} %param.14) | copy-start | bytes 54532
  6.5 86.7 %copy-start.5 = (f32[4544]{0:T(1024)S(1)}, f32[4544]{0:T(1024)}, u32[]{:S(2)}) copy-start(f32[4544]{0:T(1024)} %param.13) | copy-start | bytes 54532
  6.5 86.6 %all-gather.3.cloned.1.call-start = ((), (), s32[]{:S(2)}) async-start(), calls=%async_computation.1 | async-start | bytes 2228224 | tf_op jit(solution)/shard_map/all_gather | solution.py:151
  17.0 182.7 %all-gather.5.cloned.1.call-start = ((), (), s32[]{:S(2)}) async-start(), calls=%async_computation.2 | async-start | bytes 10485760 | tf_op jit(solution)/shard_map/all_gather | solution.py:152
  19.7 73.4 %collective-permute-start = (bf16[1,2,4544]{2,1,0:T(2,128)(2,1)S(1)}, bf16[1,2,4544]{2,1,0:T(2,128)(2,1)S(1)}, u32[]{:S(2)}, u32[]{:S(2)}) collective-permute-start(bf16[1,2,4544]{2,1,0:T(2,128)(2,1)S(1)} %fusion.48), channel_id=1, source_target_pairs={{0,8},{1,9},{2,10},{3,11},{4,12},{5,13},{6,14},{7,15},{8,0},{9,1},... | collective-permute-start | bytes 54536 | tf_op jit(solution)/shard_map/ppermute | solution.py:106
  93.2 48.2 %copy-start.6 = (s32[8]{0:T(128)S(1)}, s32[8]{0:T(128)}, u32[]{:S(2)}) copy-start(s32[8]{0:T(128)} %param.21) | copy-start | bytes 100
  93.4 9.8 %collective-permute-start.1 = (bf16[2,2,4544]{2,1,0:T(2,128)(2,1)S(1)}, bf16[2,2,4544]{2,1,0:T(2,128)(2,1)S(1)}, u32[]{:S(2)}, u32[]{:S(2)}) collective-permute-start(bf16[2,2,4544]{2,1,0:T(2,128)(2,1)S(1)} %pad_maximum_fusion.5), channel_id=1, source_target_pairs={{0,4},{1,5},{2,6},{3,7},{4,0},{5,1},{6,2},{7,3},{8,12},{9,13},{10,... | collective-permute-start | bytes 109064 | tf_op jit(solution)/shard_map/ppermute | solution.py:106
  103.4 7.1 %collective-permute-start.2 = (bf16[4,2,4544]{2,1,0:T(2,128)(2,1)S(1)}, bf16[4,2,4544]{2,1,0:T(2,128)(2,1)S(1)}, u32[]{:S(2)}, u32[]{:S(2)}) collective-permute-start(bf16[4,2,4544]{2,1,0:T(2,128)(2,1)S(1)} %pad_maximum_fusion.4), channel_id=1, source_target_pairs={{0,2},{1,3},{2,0},{3,1},{4,6},{5,7},{6,4},{7,5},{8,10},{9,11},{10,... | collective-permute-start | bytes 218120 | tf_op jit(solution)/shard_map/ppermute | solution.py:106
  110.9 7.2 %collective-permute-start.3 = (bf16[8,2,4544]{2,1,0:T(2,128)(2,1)S(1)}, bf16[8,2,4544]{2,1,0:T(2,128)(2,1)S(1)}, u32[]{:S(2)}, u32[]{:S(2)}) collective-permute-start(bf16[8,2,4544]{2,1,0:T(2,128)(2,1)S(1)} %pad_maximum_fusion.3), channel_id=1, source_target_pairs={{0,1},{1,0},{2,3},{3,2},{4,5},{5,4},{6,7},{7,6},{8,9},{9,8},{10,11... | collective-permute-start | bytes 436232 | tf_op jit(solution)/shard_map/ppermute | solution.py:106
  118.8 18.7 %collective-permute-start.4 = (bf16[16,2,4544]{2,1,0:T(2,128)(2,1)S(1)}, bf16[16,2,4544]{2,1,0:T(2,128)(2,1)S(1)}, u32[]{:S(2)}, u32[]{:S(2)}) collective-permute-start(bf16[16,2,4544]{2,1,0:T(2,128)(2,1)S(1)} %pad_maximum_fusion.2), channel_id=1, source_target_pairs={{0,32},{1,33},{2,34},{3,35},{4,36},{5,37},{6,38},{7,39},{8,40},{9,... | collective-permute-start | bytes 872456 | tf_op jit(solution)/shard_map/ppermute | solution.py:106
  138.9 25.7 %collective-permute-start.5 = (bf16[32,2,4544]{2,1,0:T(2,128)(2,1)S(1)}, bf16[32,2,4544]{2,1,0:T(2,128)(2,1)S(1)}, u32[]{:S(2)}, u32[]{:S(2)}) collective-permute-start(bf16[32,2,4544]{2,1,0:T(2,128)(2,1)S(1)} %pad_maximum_fusion.1), channel_id=1, source_target_pairs={{0,16},{1,17},{2,18},{3,19},{4,20},{5,21},{6,22},{7,23},{8,24},{9,... | collective-permute-start | bytes 1744904 | tf_op jit(solution)/shard_map/ppermute | solution.py:106
  165.9 4.5 %copy-start.2 = (bf16[4544,64]{0,1:T(8,128)(2,1)S(1)}, bf16[4544,64]{0,1:T(8,128)(2,1)}, u32[]{:S(2)}) copy-start(bf16[4544,64]{0,1:T(8,128)(2,1)} %param.15) | copy-start | bytes 1744900
  199.8 38.1 %copy-start.1 = (bf16[64,4544]{1,0:T(8,128)(2,1)S(1)}, bf16[64,4544]{1,0:T(8,128)(2,1)}, u32[]{:S(2)}) copy-start(bf16[64,4544]{1,0:T(8,128)(2,1)} %param.17) | copy-start | bytes 1744900
  250.2 17.0 %collective-permute-start.6 = (bf16[2,2,2,2,2,2,4544]{6,5,4,3,2,1,0:T(2,128)(2,1)S(1)}, bf16[2,2,2,2,2,2,4544]{6,5,4,3,2,1,0:T(2,128)(2,1)S(1)}, u32[]{:S(2)}, u32[]{:S(2)}) collective-permute-start(bf16[2,2,2,2,2,2,4544]{6,5,4,3,2,1,0:T(2,128)(2,1)S(1)} %fusion.22), channel_id=1, source_target_pairs={{0,16},{1,17},{2,18},{3,19},{4,20},{5,21},{6,22},{7,23},{8,24},{9,... | collective-permute-start | bytes 1744904 | tf_op jit(solution)/shard_map/ppermute | solution.py:122
  269.3 11.3 %collective-permute-start.7 = (bf16[2,2,2,2,2,4544]{5,4,3,2,1,0:T(2,128)(2,1)S(1)}, bf16[2,2,2,2,2,4544]{5,4,3,2,1,0:T(2,128)(2,1)S(1)}, u32[]{:S(2)}, u32[]{:S(2)}) collective-permute-start(bf16[2,2,2,2,2,4544]{5,4,3,2,1,0:T(2,128)(2,1)S(1)} %fusion.23), channel_id=1, source_target_pairs={{0,32},{1,33},{2,34},{3,35},{4,36},{5,37},{6,38},{7,39},{8,40},{9,... | collective-permute-start | bytes 872456 | tf_op jit(solution)/shard_map/ppermute | solution.py:122
  281.1 7.0 %collective-permute-start.8 = (bf16[2,2,2,2,4544]{4,3,2,1,0:T(2,128)(2,1)S(1)}, bf16[2,2,2,2,4544]{4,3,2,1,0:T(2,128)(2,1)S(1)}, u32[]{:S(2)}, u32[]{:S(2)}) collective-permute-start(bf16[2,2,2,2,4544]{4,3,2,1,0:T(2,128)(2,1)S(1)} %fusion.24), channel_id=1, source_target_pairs={{0,1},{1,0},{2,3},{3,2},{4,5},{5,4},{6,7},{7,6},{8,9},{9,8},{10,11... | collective-permute-start | bytes 436232 | tf_op jit(solution)/shard_map/ppermute | solution.py:122
  288.3 7.7 %collective-permute-start.9 = (bf16[2,2,2,4544]{3,2,1,0:T(2,128)(2,1)S(1)}, bf16[2,2,2,4544]{3,2,1,0:T(2,128)(2,1)S(1)}, u32[]{:S(2)}, u32[]{:S(2)}) collective-permute-start(bf16[2,2,2,4544]{3,2,1,0:T(2,128)(2,1)S(1)} %fusion.28), channel_id=1, source_target_pairs={{0,2},{1,3},{2,0},{3,1},{4,6},{5,7},{6,4},{7,5},{8,10},{9,11},{10,... | collective-permute-start | bytes 218120 | tf_op jit(solution)/shard_map/ppermute | solution.py:122
  296.1 10.5 %collective-permute-start.10 = (bf16[2,2,4544]{2,1,0:T(2,128)(2,1)S(1)}, bf16[2,2,4544]{2,1,0:T(2,128)(2,1)S(1)}, u32[]{:S(2)}, u32[]{:S(2)}) collective-permute-start(bf16[2,2,4544]{2,1,0:T(2,128)(2,1)S(1)} %fusion.49), channel_id=1, source_target_pairs={{0,4},{1,5},{2,6},{3,7},{4,0},{5,1},{6,2},{7,3},{8,12},{9,13},{10,... | collective-permute-start | bytes 109064 | tf_op jit(solution)/shard_map/ppermute | solution.py:122
  306.7 14.4 %collective-permute-start.11 = (bf16[2,4544]{1,0:T(2,128)(2,1)S(1)}, bf16[2,4544]{1,0:T(2,128)(2,1)S(1)}, u32[]{:S(2)}, u32[]{:S(2)}) collective-permute-start(bf16[2,4544]{1,0:T(2,128)(2,1)S(1)} %fusion.91), channel_id=1, source_target_pairs={{0,8},{1,9},{2,10},{3,11},{4,12},{5,13},{6,14},{7,15},{8,0},{9,1},... | collective-permute-start | bytes 54536 | tf_op jit(solution)/shard_map/ppermute | solution.py:122
Sparse Core Ops, SparseCore 0:
  17.1 75.9 all-gather.2
  95.2 104.4 all-gather.4

commit v3 on v2

--- a/solution.py
+++ b/solution.py
@@ -126,6 +126,36 @@
     return buf
 
 
+def spread_from_first(x, name):
+    size = lax.axis_size(name)
+    me = lax.axis_index(name)
+    have = 1
+    while have < size:
+        pairs = [(i, 2 * have - 1 - i) for i in range(have) if 2 * have - 1 - i < size]
+        got = lax.ppermute(x, name, pairs)
+        x = jnp.where((me >= have) & (me < 2 * have), got, x)
+        have *= 2
+    return x
+
+
+def partial_state(queries, keys, values, valid):
+    scores = jnp.einsum("...qd,...kd->...qk", queries, keys, preferred_element_type=jnp.float32)
+    scores = scores * (1.0 / math.sqrt(queries.shape[-1]))
+    scores = jnp.where(valid, scores, NEGATIVE)
+    best = jnp.max(scores, axis=-1)
+    weights = jnp.exp(scores - best[..., None])
+    summed = jnp.einsum(
+        "...qk,...kd->...qd",
+        weights.astype(jnp.bfloat16),
+        values,
+        preferred_element_type=jnp.float32,
+    )
+    return (summed, best, jnp.sum(weights, axis=-1))
+
+
+SHORT_MAX = 2048
+
+
 def local(
     tokens,
     ln_gain,
@@ -139,18 +169,29 @@
     cache_lengths,
 ):
     n = lax.axis_size("tx") * lax.axis_size("tz")
-    bits = n.bit_length() - 1
     width = kv_weight.shape[1] // 2
     query_cols = q_weight.shape[1]
     heads_here = query_cols // width
     width_model = tokens.shape[-1]
     per_device = tokens.shape[1]
-
-    mine = lax.all_to_all(kv_cache, "dp", split_axis=0, concat_axis=2, tiled=True)
-    inner_all = mine.shape[2]
-    gathered = lax.all_gather(mine, "tz", axis=1, tiled=True)
-    gathered = lax.all_gather(gathered, "tx", axis=1, tiled=True)
-    flat_keys = gathered[0].reshape(-1, 2 * width)
+    requests, blocks_here, inner_here = kv_cache.shape[:3]
+    group = lax.axis_index("dp")
+    inner_all = inner_here * lax.axis_size("dp")
+    longest = jnp.argmax(cache_lengths).astype(jnp.int32)
+    long_length = lax.dynamic_index_in_dim(cache_lengths, longest, 0, keepdims=False)
+    inner_pos = group * inner_here + jnp.arange(inner_here, dtype=jnp.int32)
+
+    long_local = lax.dynamic_index_in_dim(kv_cache, longest, 0, keepdims=False)
+    long_all = gather_rounds(long_local, n)
+    slot_src = layout_source(jnp.arange(n, dtype=jnp.int32), n)
+    long_block = slot_src[:, None] * blocks_here + jnp.arange(blocks_here, dtype=jnp.int32)
+    long_pos = (long_block[:, :, None] * inner_all + inner_pos).reshape(-1)
+    long_keys = long_all.reshape(-1, 2 * width)
+
+    short_blocks = -(-SHORT_MAX // inner_all)
+    short_gath = lax.all_gather(kv_cache, "tz", axis=1, tiled=True)[:, :short_blocks]
+    short_keys = spread_from_first(short_gath, "tx").reshape(requests, -1, 2 * width)
+    short_pos = (jnp.arange(short_blocks, dtype=jnp.int32)[:, None] * inner_all + inner_pos).reshape(-1)
 
     normed = norm_rows(tokens[0], ln_gain, ln_bias)
     piece = gather_rounds(normed, n).reshape(n * per_device, width_model)
@@ -165,7 +206,6 @@
     span = projected.shape[0]
     row = jnp.arange(span, dtype=jnp.int32)
     token_pos = layout_source(row // per_device, n) * per_device + row % per_device
-    group = lax.axis_index("dp")
     own_length = lax.dynamic_index_in_dim(cache_lengths, group, 0, keepdims=False)
     places = own_length + token_pos
     cosine, sine = rotary_tables(places, width)
@@ -183,14 +223,39 @@
     )
     rows = span * heads_here
     query_rows = queries.reshape(rows, width)
-    places_piece = jnp.arange(flat_keys.shape[0], dtype=jnp.int32)
-    valid = (places_piece < own_length)[None, :]
-    state = lax.cond(
-        jnp.int32(0) * inner_all < own_length,
-        lambda carry: fold_keys(carry, query_rows, flat_keys, valid),
-        lambda carry: carry,
-        empty_state(rows, width, ()),
-    )
+
+    q_all = lax.all_gather(query_rows, "dp", axis=0, tiled=False)
+    which = jnp.arange(requests, dtype=jnp.int32)
+    short_valid = (short_pos[None, :] < cache_lengths[:, None]) & (which != longest)[:, None]
+    short_state = partial_state(
+        q_all, short_keys[..., :width], short_keys[..., width:], short_valid[:, None, :]
+    )
+    q_long = lax.dynamic_index_in_dim(q_all, longest, 0, keepdims=False)
+    long_v, long_m, long_s = partial_state(
+        q_long, long_keys[:, :width], long_keys[:, width:], (long_pos < long_length)[None, :]
+    )
+    is_long = which == longest
+    state_all = combine(
+        short_state,
+        (
+            jnp.where(is_long[:, None, None], long_v[None], 0.0),
+            jnp.where(is_long[:, None], long_m[None], NEGATIVE),
+            jnp.where(is_long[:, None], long_s[None], 0.0),
+        ),
+    )
+    packed = jnp.concatenate(
+        [state_all[0], state_all[1][..., None], state_all[2][..., None]], axis=-1
+    )
+    got = lax.all_to_all(packed, "dp", 0, 0, tiled=True)
+    part_v, part_m, part_s = got[..., :width], got[..., width], got[..., width + 1]
+    best = jnp.max(part_m, axis=0)
+    scale = jnp.exp(part_m - best[None])
+    state = (
+        jnp.sum(part_v * scale[..., None], axis=0),
+        best,
+        jnp.sum(part_s * scale, axis=0),
+    )
+
     pos_of_row = jnp.repeat(token_pos, heads_here)
     causal = token_pos[None, :] <= pos_of_row[:, None]
     summed, best, total = absorb(state, query_rows, new_keys, new_values, causal)

time: 330 us -> 272 us (0.82)
  the two profiles are of different devices: /device:TPU:10 before, /device:TPU:4 now
where the time goes in v3:
time: 272 us; the launch traced here: 270 us
  waiting for transfers between devices  98.1 us (36%)
  starting transfers between devices  84.9 us (31%)
  other arithmetic  28.2 us (10%)
  between operations  16.1 us (6%)
  matrix products  15.4 us (6%)
  local copies, waits for them, and re-layouts  15.1 us (6%)
  blocking collectives  12.3 us (5%)
    ppermute x12, starting transfers between devices, gather_rounds(): other = lax.ppermute(buf, TENSOR, [(i, i ^ 1 << b) for i in range(n)])  56.3 us
    ppermute x6, waiting for transfers between devices, scatter_rounds(): lax.ppermute(send.astype(jnp.bfloat16), TENSOR, [(i, i ^ 1 << b) for i in...  43.3 us
    ppermute x12, waiting for transfers between devices, gather_rounds(): other = lax.ppermute(buf, TENSOR, [(i, i ^ 1 << b) for i in range(n)])  28.1 us
    ppermute x6, starting transfers between devices, scatter_rounds(): lax.ppermute(send.astype(jnp.bfloat16), TENSOR, [(i, i ^ 1 << b) for i in...  23.1 us
    ppermute x2, waiting for transfers between devices, spread_from_first(): got = lax.ppermute(x, name, pairs)  18.5 us
    all_gather x1, blocking collectives, local(): q_all = lax.all_gather(query_rows, 'dp', axis=0, tiled=False)  12.3 us
    all_to_all x1, waiting for transfers between devices, local(): got = lax.all_to_all(packed, 'dp', 0, 0, tiled=True)  7.43 us
  transfers between devices with their start and end apart: 22, of which 16 were waited for; matrix products, arithmetic and copies ran while one was open for 13% of the time, Pallas kernels for 0%

profile of v3, /device:TPU:4, one launch (start us, length us, event | category | flops | bytes accessed | tf_op | source)
XLA Modules:
  0.0 270.1 jit_solution(13453803087890826874)
XLA Ops:
  7.3 1.3 iota_reduce_fusion
  11.2 15.7 %collective-permute-start.8 = (bf16[1,8,8,128]{3,2,1,0:T(8,128)(2,1)S(1)}, bf16[1,8,8,128]{3,2,1,0:T(8,128)(2,1)S(1)}, u32[]{:S(2)}, u32[]{:S(2)}) collective-permute-start(bf16[1,8,8,128]{3,2,1,0:T(8,128)(2,1)S(1)} %constant_dynamic-slice_fusion), channel_id=1, source_target_pairs={{0,8},{1,9},{2,10},{3,11},{4,12},{5,13},{6,14},{7,15},{8,0},{9,1},... | collective-permute-start | bytes 49160 | tf_op jit(solution)/shard_map/ppermute | solution.py:106
  29.6 1.9 collective-permute-start
  32.2 1.3 fusion.160
  38.6 6.0 %collective-permute-start.9 = (bf16[2,8,8,128]{3,2,1,0:T(8,128)(2,1)S(1)}, bf16[2,8,8,128]{3,2,1,0:T(8,128)(2,1)S(1)}, u32[]{:S(2)}, u32[]{:S(2)}) collective-permute-start(bf16[2,8,8,128]{3,2,1,0:T(8,128)(2,1)S(1)} %pad_maximum_fusion.14), channel_id=1, source_target_pairs={{0,4},{1,5},{2,6},{3,7},{4,0},{5,1},{6,2},{7,3},{8,12},{9,13},{10,... | collective-permute-start | bytes 98312 | tf_op jit(solution)/shard_map/ppermute | solution.py:106
  45.6 3.8 %collective-permute-start.1 = (bf16[2,2,4544]{2,1,0:T(2,128)(2,1)S(1)}, bf16[2,2,4544]{2,1,0:T(2,128)(2,1)S(1)}, u32[]{:S(2)}, u32[]{:S(2)}) collective-permute-start(bf16[2,2,4544]{2,1,0:T(2,128)(2,1)S(1)} %pad_maximum_fusion.11), channel_id=1, source_target_pairs={{0,4},{1,5},{2,6},{3,7},{4,0},{5,1},{6,2},{7,3},{8,12},{9,13},{10,... | collective-permute-start | bytes 109064 | tf_op jit(solution)/shard_map/ppermute | solution.py:106
  49.9 2.9 %collective-permute-start.10 = (bf16[4,8,8,128]{3,2,1,0:T(8,128)(2,1)S(1)}, bf16[4,8,8,128]{3,2,1,0:T(8,128)(2,1)S(1)}, u32[]{:S(2)}, u32[]{:S(2)}) collective-permute-start(bf16[4,8,8,128]{3,2,1,0:T(8,128)(2,1)S(1)} %pad_maximum_fusion.10), channel_id=1, source_target_pairs={{0,2},{1,3},{2,0},{3,1},{4,6},{5,7},{6,4},{7,5},{8,10},{9,11},{10,... | collective-permute-start | bytes 196616 | tf_op jit(solution)/shard_map/ppermute | solution.py:106
  52.8 2.7 %collective-permute-done.1 = bf16[2,2,4544]{2,1,0:T(2,128)(2,1)S(1)} collective-permute-done((bf16[2,2,4544]{2,1,0:T(2,128)(2,1)S(1)}, bf16[2,2,4544]{2,1,0:T(2,128)(2,1)S(1)}, u32[]{:S(2)}, u32[]{:S(2)}) %collective-permute-start.1) | collective-permute-done | bytes 36384 | tf_op jit(solution)/shard_map/ppermute | solution.py:106
  55.8 5.8 %collective-permute-start.2 = (bf16[4,2,4544]{2,1,0:T(2,128)(2,1)S(1)}, bf16[4,2,4544]{2,1,0:T(2,128)(2,1)S(1)}, u32[]{:S(2)}, u32[]{:S(2)}) collective-permute-start(bf16[4,2,4544]{2,1,0:T(2,128)(2,1)S(1)} %pad_maximum_fusion.9), channel_id=1, source_target_pairs={{0,2},{1,3},{2,0},{3,1},{4,6},{5,7},{6,4},{7,5},{8,10},{9,11},{10,... | collective-permute-start | bytes 218120 | tf_op jit(solution)/shard_map/ppermute | solution.py:106
  61.7 3.9 %collective-permute-start.11 = (bf16[8,8,8,128]{3,2,1,0:T(8,128)(2,1)S(1)}, bf16[8,8,8,128]{3,2,1,0:T(8,128)(2,1)S(1)}, u32[]{:S(2)}, u32[]{:S(2)}) collective-permute-start(bf16[8,8,8,128]{3,2,1,0:T(8,128)(2,1)S(1)} %pad_maximum_fusion.8), channel_id=1, source_target_pairs={{0,1},{1,0},{2,3},{3,2},{4,5},{5,4},{6,7},{7,6},{8,9},{9,8},{10,11... | collective-permute-start | bytes 393224 | tf_op jit(solution)/shard_map/ppermute | solution.py:106
  65.9 3.8 %collective-permute-start.3 = (bf16[8,2,4544]{2,1,0:T(2,128)(2,1)S(1)}, bf16[8,2,4544]{2,1,0:T(2,128)(2,1)S(1)}, u32[]{:S(2)}, u32[]{:S(2)}) collective-permute-start(bf16[8,2,4544]{2,1,0:T(2,128)(2,1)S(1)} %pad_maximum_fusion.7), channel_id=1, source_target_pairs={{0,1},{1,0},{2,3},{3,2},{4,5},{5,4},{6,7},{7,6},{8,9},{9,8},{10,11... | collective-permute-start | bytes 436232 | tf_op jit(solution)/shard_map/ppermute | solution.py:106
  69.8 2.6 collective-permute-done.11
  72.4 1.9 collective-permute-start.12
  75.7 4.9 %collective-permute-start.4 = (bf16[16,2,4544]{2,1,0:T(2,128)(2,1)S(1)}, bf16[16,2,4544]{2,1,0:T(2,128)(2,1)S(1)}, u32[]{:S(2)}, u32[]{:S(2)}) collective-permute-start(bf16[16,2,4544]{2,1,0:T(2,128)(2,1)S(1)} %pad_maximum_fusion.4), channel_id=1, source_target_pairs={{0,32},{1,33},{2,34},{3,35},{4,36},{5,37},{6,38},{7,39},{8,40},{9,... | collective-permute-start | bytes 872456 | tf_op jit(solution)/shard_map/ppermute | solution.py:106
  80.5 4.4 %collective-permute-done.12 = bf16[16,8,8,128]{3,2,1,0:T(8,128)(2,1)S(1)} collective-permute-done((bf16[16,8,8,128]{3,2,1,0:T(8,128)(2,1)S(1)}, bf16[16,8,8,128]{3,2,1,0:T(8,128)(2,1)S(1)}, u32[]{:S(2)}, u32[]{:S(2)}) %collective-permute-start.12) | collective-permute-done | bytes 262176 | tf_op jit(solution)/shard_map/ppermute | solution.py:106
  85.0 2.8 %collective-permute-start.13 = (bf16[32,8,8,128]{3,2,1,0:T(8,128)(2,1)S(1)}, bf16[32,8,8,128]{3,2,1,0:T(8,128)(2,1)S(1)}, u32[]{:S(2)}, u32[]{:S(2)}) collective-permute-start(bf16[32,8,8,128]{3,2,1,0:T(8,128)(2,1)S(1)} %pad_maximum_fusion.3), channel_id=1, source_target_pairs={{0,16},{1,17},{2,18},{3,19},{4,20},{5,21},{6,22},{7,23},{8,24},{9,... | collective-permute-start | bytes 1572872 | tf_op jit(solution)/shard_map/ppermute | solution.py:106
  87.8 3.4 %collective-permute-done.4 = bf16[16,2,4544]{2,1,0:T(2,128)(2,1)S(1)} collective-permute-done((bf16[16,2,4544]{2,1,0:T(2,128)(2,1)S(1)}, bf16[16,2,4544]{2,1,0:T(2,128)(2,1)S(1)}, u32[]{:S(2)}, u32[]{:S(2)}) %collective-permute-start.4) | collective-permute-done | bytes 290848 | tf_op jit(solution)/shard_map/ppermute | solution.py:106
  92.7 2.8 %collective-permute-start.5 = (bf16[32,2,4544]{2,1,0:T(2,128)(2,1)S(1)}, bf16[32,2,4544]{2,1,0:T(2,128)(2,1)S(1)}, u32[]{:S(2)}, u32[]{:S(2)}) collective-permute-start(bf16[32,2,4544]{2,1,0:T(2,128)(2,1)S(1)} %pad_maximum_fusion.2), channel_id=1, source_target_pairs={{0,16},{1,17},{2,18},{3,19},{4,20},{5,21},{6,22},{7,23},{8,24},{9,... | collective-permute-start | bytes 1744904 | tf_op jit(solution)/shard_map/ppermute | solution.py:106
  96.1 5.6 %collective-permute-done.13 = bf16[32,8,8,128]{3,2,1,0:T(8,128)(2,1)S(1)} collective-permute-done((bf16[32,8,8,128]{3,2,1,0:T(8,128)(2,1)S(1)}, bf16[32,8,8,128]{3,2,1,0:T(8,128)(2,1)S(1)}, u32[]{:S(2)}, u32[]{:S(2)}) %collective-permute-start.13) | collective-permute-done | bytes 524320 | tf_op jit(solution)/shard_map/ppermute | solution.py:106
  102.9 8.4 %collective-permute-done.5 = bf16[32,2,4544]{2,1,0:T(2,128)(2,1)S(1)} collective-permute-done((bf16[32,2,4544]{2,1,0:T(2,128)(2,1)S(1)}, bf16[32,2,4544]{2,1,0:T(2,128)(2,1)S(1)}, u32[]{:S(2)}, u32[]{:S(2)}) %collective-permute-start.5) | collective-permute-done | bytes 581664 | tf_op jit(solution)/shard_map/ppermute | solution.py:106
  112.6 2.6 pad_maximum_fusion
  115.1 2.0 reshape.553
  117.7 12.3 %all-gather = bf16[1024,64]{0,1:T(8,128)(2,1)S(1)} all-gather(bf16[128,64]{0,1:T(8,128)(2,1)S(1)} %fusion.85), channel_id=2, replica_groups=mesh['dp'=8,'tx'=4,'tz'=16] {'dp'}, dimensions={0}, use_global_device_ids=true | all-gather | bytes 147456 | tf_op jit(solution)/shard_map/all_gather | solution.py:227
  134.3 1.3 slice_negate_fusion
  135.6 2.3 fusion.9
  137.9 1.9 broadcast_select_fusion.6
  139.8 1.5 collective-permute-start.7
  142.3 5.2 %fusion.39 = f32[128,4544]{0,1:T(8,128)} fusion(bf16[142,4544]{1,0:T(8,128)(2,1)S(1)} %copy-done, bf16[128,4544]{1,0:T(8,128)(2,1)} %copy-done.1, bf16[4544,142]{0,1:T(8,128)(2,1)} %param.16), kind=kOutput, calls=%fused_computation.102 | convolution fusion | flops 331548416 | bytes 6070784 | tf_op jit(solution)/shard_map/dot_general | solution.py:263
  147.5 18.5 %collective-permute-done.7 = bf16[8,32,8,128]{3,2,1,0:T(8,128)(2,1)} collective-permute-done((bf16[8,32,8,128]{3,2,1,0:T(8,128)(2,1)}, bf16[8,32,8,128]{3,2,1,0:T(8,128)(2,1)}, u32[]{:S(2)}, u32[]{:S(2)}) %collective-permute-start.7) | collective-permute-done | bytes 524320 | tf_op jit(solution)/shard_map/ppermute | solution.py:135
  169.7 3.4 %all-to-all-start = ((f32[8,128,66]{1,2,0:T(8,128)}), f32[8,128,66]{1,2,0:T(8,128)S(1)}, u32[]{:S(2)}, u32[]{:S(2)}) async-start(f32[8,128,66]{1,2,0:T(8,128)} %pad_maximum_fusion.5), calls=%async_computation | async-start | bytes 589824 | tf_op jit(solution)/shard_map/all_to_all | solution.py:249
  173.5 7.4 %all-to-all-done = f32[8,128,66]{1,2,0:T(8,128)S(1)} async-done(((f32[8,128,66]{1,2,0:T(8,128)}), f32[8,128,66]{1,2,0:T(8,128)S(1)}, u32[]{:S(2)}, u32[]{:S(2)}) %all-to-all-start) | async-done | bytes 270368 | tf_op jit(solution)/shard_map/all_to_all | solution.py:249
  181.1 3.7 %convolution_add_fusion = f32[128,4544]{0,1:T(8,128)} fusion(f32[128,4544]{0,1:T(8,128)} %fusion.39, bf16[64,4544]{1,0:T(8,128)(2,1)S(1)} %copy-done.5, f32[128,128]{0,1:T(8,128)S(1)} %get-tuple-element.53, f32[128]{0:T(128)S(1)} %get-tuple-element.52, f32[128,64]{0,1:T(8,128)S(1)} %fusion.22, f32[128,128]{0,1:T(8,128)S(1)} %copy-done.8, ...), kind=kOutput, calls=%fused_computation | convolution fusion | flops 77201408 | bytes 5359616 | tf_op jit(solution)/shard_map/dot_general | solution.py:263
  184.8 3.1 %copy.27 = f32[128,4544]{1,0:T(8,128)} copy(f32[128,4544]{0,1:T(8,128)} %convolution_add_fusion) | data formatting | bytes 4653056 | tf_op jit(solution)/shard_map/add | solution.py:263
  187.8 3.7 %reshape_reshape.3 = f32[2,2,2,2,2,2,2,4544]{7,6,5,4,3,2,1,0:T(2,128)} reshape(f32[128,4544]{1,0:T(8,128)} %copy.27) | data formatting | bytes 4653056 | tf_op jit(solution)/shard_map/reshape;reshape | solution.py:117
  191.5 1.7 fusion.16
  193.2 2.1 collective-permute-start.14
  195.3 14.5 %collective-permute-done.14 = bf16[2,2,2,2,2,2,4544]{6,5,4,3,2,1,0:T(2,128)(2,1)S(1)} collective-permute-done((bf16[2,2,2,2,2,2,4544]{6,5,4,3,2,1,0:T(2,128)(2,1)S(1)}, bf16[2,2,2,2,2,2,4544]{6,5,4,3,2,1,0:T(2,128)(2,1)S(1)}, u32[]{:S(2)}, u32[]{:S(2)}) %collective-permute-start.14) | collective-permute-done | bytes 581664 | tf_op jit(solution)/shard_map/ppermute | solution.py:122
  209.8 1.9 bitcast_add_fusion
  211.9 1.9 collective-permute-start.15
  213.8 8.9 %collective-permute-done.15 = bf16[2,2,2,2,2,4544]{5,4,3,2,1,0:T(2,128)(2,1)S(1)} collective-permute-done((bf16[2,2,2,2,2,4544]{5,4,3,2,1,0:T(2,128)(2,1)S(1)}, bf16[2,2,2,2,2,4544]{5,4,3,2,1,0:T(2,128)(2,1)S(1)}, u32[]{:S(2)}, u32[]{:S(2)}) %collective-permute-start.15) | collective-permute-done | bytes 290848 | tf_op jit(solution)/shard_map/ppermute | solution.py:122
  223.2 2.3 collective-permute-start.16
  225.5 4.7 %collective-permute-done.16 = bf16[2,2,2,2,4544]{4,3,2,1,0:T(2,128)(2,1)S(1)} collective-permute-done((bf16[2,2,2,2,4544]{4,3,2,1,0:T(2,128)(2,1)S(1)}, bf16[2,2,2,2,4544]{4,3,2,1,0:T(2,128)(2,1)S(1)}, u32[]{:S(2)}, u32[]{:S(2)}) %collective-permute-start.16) | collective-permute-done | bytes 145440 | tf_op jit(solution)/shard_map/ppermute | solution.py:122
  230.5 2.6 collective-permute-start.17
  233.1 5.1 %collective-permute-done.17 = bf16[2,2,2,4544]{3,2,1,0:T(2,128)(2,1)S(1)} collective-permute-done((bf16[2,2,2,4544]{3,2,1,0:T(2,128)(2,1)S(1)}, bf16[2,2,2,4544]{3,2,1,0:T(2,128)(2,1)S(1)}, u32[]{:S(2)}, u32[]{:S(2)}) %collective-permute-start.17) | collective-permute-done | bytes 72736 | tf_op jit(solution)/shard_map/ppermute | solution.py:122
  238.4 3.1 %collective-permute-start.18 = (bf16[2,2,4544]{2,1,0:T(2,128)(2,1)S(1)}, bf16[2,2,4544]{2,1,0:T(2,128)(2,1)S(1)}, u32[]{:S(2)}, u32[]{:S(2)}) collective-permute-start(bf16[2,2,4544]{2,1,0:T(2,128)(2,1)S(1)} %fusion.48), channel_id=1, source_target_pairs={{0,4},{1,5},{2,6},{3,7},{4,0},{5,1},{6,2},{7,3},{8,12},{9,13},{10,... | collective-permute-start | bytes 109064 | tf_op jit(solution)/shard_map/ppermute | solution.py:122
  241.5 6.7 %collective-permute-done.18 = bf16[2,2,4544]{2,1,0:T(2,128)(2,1)S(1)} collective-permute-done((bf16[2,2,4544]{2,1,0:T(2,128)(2,1)S(1)}, bf16[2,2,4544]{2,1,0:T(2,128)(2,1)S(1)}, u32[]{:S(2)}, u32[]{:S(2)}) %collective-permute-start.18) | collective-permute-done | bytes 36384 | tf_op jit(solution)/shard_map/ppermute | solution.py:122
  248.3 11.1 %collective-permute-start.19 = (bf16[2,4544]{1,0:T(2,128)(2,1)S(1)}, bf16[2,4544]{1,0:T(2,128)(2,1)S(1)}, u32[]{:S(2)}, u32[]{:S(2)}) collective-permute-start(bf16[2,4544]{1,0:T(2,128)(2,1)S(1)} %fusion.90), channel_id=1, source_target_pairs={{0,8},{1,9},{2,10},{3,11},{4,12},{5,13},{6,14},{7,15},{8,0},{9,1},... | collective-permute-start | bytes 54536 | tf_op jit(solution)/shard_map/ppermute | solution.py:122
  259.3 3.3 %collective-permute-done.19 = bf16[2,4544]{1,0:T(2,128)(2,1)S(1)} collective-permute-done((bf16[2,4544]{1,0:T(2,128)(2,1)S(1)}, bf16[2,4544]{1,0:T(2,128)(2,1)S(1)}, u32[]{:S(2)}, u32[]{:S(2)}) %collective-permute-start.19) | collective-permute-done | bytes 18208 | tf_op jit(solution)/shard_map/ppermute | solution.py:122
  (139 shorter events, 29.2 us)
Async XLA Ops:
  6.5 135.7 %copy-start = (bf16[142,4544]{1,0:T(8,128)(2,1)S(1)}, bf16[142,4544]{1,0:T(8,128)(2,1)}, u32[]{:S(2)}) copy-start(bf16[142,4544]{1,0:T(8,128)(2,1)} %param.17) | copy-start | bytes 3871492
  6.5 125.8 %all-gather.3.cloned.1.call-start = ((), (), s32[]{:S(2)}) async-start(), calls=%async_computation.1 | async-start | bytes 2228224 | tf_op jit(solution)/shard_map/all_gather | solution.py:192
  11.2 26.7 %collective-permute-start.8 = (bf16[1,8,8,128]{3,2,1,0:T(8,128)(2,1)S(1)}, bf16[1,8,8,128]{3,2,1,0:T(8,128)(2,1)S(1)}, u32[]{:S(2)}, u32[]{:S(2)}) collective-permute-start(bf16[1,8,8,128]{3,2,1,0:T(8,128)(2,1)S(1)} %constant_dynamic-slice_fusion), channel_id=1, source_target_pairs={{0,8},{1,9},{2,10},{3,11},{4,12},{5,13},{6,14},{7,15},{8,0},{9,1},... | collective-permute-start | bytes 49160 | tf_op jit(solution)/shard_map/ppermute | solution.py:106
  29.6 15.0 %collective-permute-start = (bf16[1,2,4544]{2,1,0:T(2,128)(2,1)S(1)}, bf16[1,2,4544]{2,1,0:T(2,128)(2,1)S(1)}, u32[]{:S(2)}, u32[]{:S(2)}) collective-permute-start(bf16[1,2,4544]{2,1,0:T(2,128)(2,1)S(1)} %fusion.47), channel_id=1, source_target_pairs={{0,8},{1,9},{2,10},{3,11},{4,12},{5,13},{6,14},{7,15},{8,0},{9,1},... | collective-permute-start | bytes 54536 | tf_op jit(solution)/shard_map/ppermute | solution.py:106
  34.9 82.7 %copy-start.12 = (f32[128,32]{0,1:T(8,128)}, f32[128,32]{0,1:T(8,128)S(1)}, u32[]{:S(2)}) copy-start(f32[128,32]{0,1:T(8,128)S(1)} %get-tuple-element.44) | copy-start | bytes 49156
  35.0 82.7 %copy-start.14 = (f32[128,32]{0,1:T(8,128)}, f32[128,32]{0,1:T(8,128)S(1)}, u32[]{:S(2)}) copy-start(f32[128,32]{0,1:T(8,128)S(1)} %get-tuple-element.45) | copy-start | bytes 49156
  38.6 11.3 %collective-permute-start.9 = (bf16[2,8,8,128]{3,2,1,0:T(8,128)(2,1)S(1)}, bf16[2,8,8,128]{3,2,1,0:T(8,128)(2,1)S(1)}, u32[]{:S(2)}, u32[]{:S(2)}) collective-permute-start(bf16[2,8,8,128]{3,2,1,0:T(8,128)(2,1)S(1)} %pad_maximum_fusion.14), channel_id=1, source_target_pairs={{0,4},{1,5},{2,6},{3,7},{4,0},{5,1},{6,2},{7,3},{8,12},{9,13},{10,... | collective-permute-start | bytes 98312 | tf_op jit(solution)/shard_map/ppermute | solution.py:106
  45.6 10.0 %collective-permute-start.1 = (bf16[2,2,4544]{2,1,0:T(2,128)(2,1)S(1)}, bf16[2,2,4544]{2,1,0:T(2,128)(2,1)S(1)}, u32[]{:S(2)}, u32[]{:S(2)}) collective-permute-start(bf16[2,2,4544]{2,1,0:T(2,128)(2,1)S(1)} %pad_maximum_fusion.11), channel_id=1, source_target_pairs={{0,4},{1,5},{2,6},{3,7},{4,0},{5,1},{6,2},{7,3},{8,12},{9,13},{10,... | collective-permute-start | bytes 109064 | tf_op jit(solution)/shard_map/ppermute | solution.py:106
  49.9 11.7 %collective-permute-start.10 = (bf16[4,8,8,128]{3,2,1,0:T(8,128)(2,1)S(1)}, bf16[4,8,8,128]{3,2,1,0:T(8,128)(2,1)S(1)}, u32[]{:S(2)}, u32[]{:S(2)}) collective-permute-start(bf16[4,8,8,128]{3,2,1,0:T(8,128)(2,1)S(1)} %pad_maximum_fusion.10), channel_id=1, source_target_pairs={{0,2},{1,3},{2,0},{3,1},{4,6},{5,7},{6,4},{7,5},{8,10},{9,11},{10,... | collective-permute-start | bytes 196616 | tf_op jit(solution)/shard_map/ppermute | solution.py:106
  55.8 9.8 %collective-permute-start.2 = (bf16[4,2,4544]{2,1,0:T(2,128)(2,1)S(1)}, bf16[4,2,4544]{2,1,0:T(2,128)(2,1)S(1)}, u32[]{:S(2)}, u32[]{:S(2)}) collective-permute-start(bf16[4,2,4544]{2,1,0:T(2,128)(2,1)S(1)} %pad_maximum_fusion.9), channel_id=1, source_target_pairs={{0,2},{1,3},{2,0},{3,1},{4,6},{5,7},{6,4},{7,5},{8,10},{9,11},{10,... | collective-permute-start | bytes 218120 | tf_op jit(solution)/shard_map/ppermute | solution.py:106
  61.7 10.7 %collective-permute-start.11 = (bf16[8,8,8,128]{3,2,1,0:T(8,128)(2,1)S(1)}, bf16[8,8,8,128]{3,2,1,0:T(8,128)(2,1)S(1)}, u32[]{:S(2)}, u32[]{:S(2)}) collective-permute-start(bf16[8,8,8,128]{3,2,1,0:T(8,128)(2,1)S(1)} %pad_maximum_fusion.8), channel_id=1, source_target_pairs={{0,1},{1,0},{2,3},{3,2},{4,5},{5,4},{6,7},{7,6},{8,9},{9,8},{10,11... | collective-permute-start | bytes 393224 | tf_op jit(solution)/shard_map/ppermute | solution.py:106
  65.9 9.0 %collective-permute-start.3 = (bf16[8,2,4544]{2,1,0:T(2,128)(2,1)S(1)}, bf16[8,2,4544]{2,1,0:T(2,128)(2,1)S(1)}, u32[]{:S(2)}, u32[]{:S(2)}) collective-permute-start(bf16[8,2,4544]{2,1,0:T(2,128)(2,1)S(1)} %pad_maximum_fusion.7), channel_id=1, source_target_pairs={{0,1},{1,0},{2,3},{3,2},{4,5},{5,4},{6,7},{7,6},{8,9},{9,8},{10,11... | collective-permute-start | bytes 436232 | tf_op jit(solution)/shard_map/ppermute | solution.py:106
  72.4 12.5 %collective-permute-start.12 = (bf16[16,8,8,128]{3,2,1,0:T(8,128)(2,1)S(1)}, bf16[16,8,8,128]{3,2,1,0:T(8,128)(2,1)S(1)}, u32[]{:S(2)}, u32[]{:S(2)}) collective-permute-start(bf16[16,8,8,128]{3,2,1,0:T(8,128)(2,1)S(1)} %pad_maximum_fusion.6), channel_id=1, source_target_pairs={{0,32},{1,33},{2,34},{3,35},{4,36},{5,37},{6,38},{7,39},{8,40},{9,... | collective-permute-start | bytes 786440 | tf_op jit(solution)/shard_map/ppermute | solution.py:106
  75.7 15.6 %collective-permute-start.4 = (bf16[16,2,4544]{2,1,0:T(2,128)(2,1)S(1)}, bf16[16,2,4544]{2,1,0:T(2,128)(2,1)S(1)}, u32[]{:S(2)}, u32[]{:S(2)}) collective-permute-start(bf16[16,2,4544]{2,1,0:T(2,128)(2,1)S(1)} %pad_maximum_fusion.4), channel_id=1, source_target_pairs={{0,32},{1,33},{2,34},{3,35},{4,36},{5,37},{6,38},{7,39},{8,40},{9,... | collective-permute-start | bytes 872456 | tf_op jit(solution)/shard_map/ppermute | solution.py:106
  85.0 10.4 %copy-start.22 = (s32[8]{0:T(128)S(1)}, s32[8]{0:T(128)}, u32[]{:S(2)}) copy-start(s32[8]{0:T(128)} %param.19) | copy-start | bytes 100
  85.0 16.7 %collective-permute-start.13 = (bf16[32,8,8,128]{3,2,1,0:T(8,128)(2,1)S(1)}, bf16[32,8,8,128]{3,2,1,0:T(8,128)(2,1)S(1)}, u32[]{:S(2)}, u32[]{:S(2)}) collective-permute-start(bf16[32,8,8,128]{3,2,1,0:T(8,128)(2,1)S(1)} %pad_maximum_fusion.3), channel_id=1, source_target_pairs={{0,16},{1,17},{2,18},{3,19},{4,20},{5,21},{6,22},{7,23},{8,24},{9,... | collective-permute-start | bytes 1572872 | tf_op jit(solution)/shard_map/ppermute | solution.py:106
  92.7 18.6 %collective-permute-start.5 = (bf16[32,2,4544]{2,1,0:T(2,128)(2,1)S(1)}, bf16[32,2,4544]{2,1,0:T(2,128)(2,1)S(1)}, u32[]{:S(2)}, u32[]{:S(2)}) collective-permute-start(bf16[32,2,4544]{2,1,0:T(2,128)(2,1)S(1)} %pad_maximum_fusion.2), channel_id=1, source_target_pairs={{0,16},{1,17},{2,18},{3,19},{4,20},{5,21},{6,22},{7,23},{8,24},{9,... | collective-permute-start | bytes 1744904 | tf_op jit(solution)/shard_map/ppermute | solution.py:106
  115.1 2.0 copy-start.6
  117.1 14.1 %copy-start.1 = (bf16[128,4544]{1,0:T(8,128)(2,1)}, bf16[128,4544]{1,0:T(8,128)(2,1)S(1)}, u32[]{:S(2)}) copy-start(bf16[128,4544]{1,0:T(8,128)(2,1)S(1)} %reshape.553) | copy-start | bytes 3489796
  117.1 12.9 %copy-start.4 = (bf16[4544,128]{1,0:T(8,128)(2,1)S(1)}, bf16[4544,128]{1,0:T(8,128)(2,1)}, u32[]{:S(2)}) copy-start(bf16[4544,128]{1,0:T(8,128)(2,1)} %param.14) | copy-start | bytes 3489796
  117.7 13.5 %copy-start.10 = (bf16[128,64]{0,1:T(8,128)(2,1)}, bf16[128,64]{0,1:T(8,128)(2,1)S(1)}, u32[]{:S(2)}) copy-start(bf16[128,64]{0,1:T(8,128)(2,1)S(1)} %fusion.85) | copy-start | bytes 49156
  130.0 1.2 copy-start.2
  130.0 1.2 copy-start.16
  132.4 3.2 %copy-start.3 = (bf16[64,8,8,128]{3,2,1,0:T(8,128)(2,1)S(1)}, bf16[64,8,8,128]{3,2,1,0:T(8,128)(2,1)}, u32[]{:S(2)}) copy-start(bf16[64,8,8,128]{3,2,1,0:T(8,128)(2,1)} %pad_maximum_fusion.1) | copy-start | bytes 3145732
  133.6 4.4 %collective-permute-start.6 = (bf16[8,32,8,128]{3,2,1,0:T(8,128)(2,1)S(1)}, bf16[8,32,8,128]{3,2,1,0:T(8,128)(2,1)S(1)}, u32[]{:S(2)}, u32[]{:S(2)}) collective-permute-start(bf16[8,32,8,128]{3,2,1,0:T(8,128)(2,1)S(1)} %slice.61), channel_id=1, source_target_pairs={{0,16},{1,17},{2,18},{3,19},{4,20},{5,21},{6,22},{7,23},{8,24},{9,... | collective-permute-start | bytes 1572872 | tf_op jit(solution)/shard_map/ppermute | solution.py:135
  137.9 3.4 %copy-start.19 = (f32[128]{0:T(128)S(1)}, f32[128]{0:T(128)}, u32[]{:S(2)}) copy-start(f32[128]{0:T(128)} %get-tuple-element.50) | copy-start | bytes 1540
  139.8 26.2 %collective-permute-start.7 = (bf16[8,32,8,128]{3,2,1,0:T(8,128)(2,1)}, bf16[8,32,8,128]{3,2,1,0:T(8,128)(2,1)}, u32[]{:S(2)}, u32[]{:S(2)}) collective-permute-start(bf16[8,32,8,128]{3,2,1,0:T(8,128)(2,1)} %broadcast_select_fusion.6), channel_id=1, source_target_pairs={{0,48},{16,32},{1,49},{17,33},{2,50},{18,34},{3,51},{19,35},{4,52}... | collective-permute-start | bytes 1572872 | tf_op jit(solution)/shard_map/ppermute | solution.py:135
  147.5 19.6 %copy-start.21 = (pred[8,256]{1,0:T(8,128)(4,1)S(1)}, pred[8,256]{1,0:T(8,128)(4,1)}, u32[]{:S(2)}) copy-start(pred[8,256]{1,0:T(8,128)(4,1)} %compare_and_fusion) | copy-start | bytes 6148
  147.5 20.1 %copy-start.20 = (f32[128]{0:T(128)S(1)}, f32[128]{0:T(128)}, u32[]{:S(2)}) copy-start(f32[128]{0:T(128)} %get-tuple-element.50) | copy-start | bytes 1540
  147.5 20.1 %copy-start.23 = (pred[8]{0:T(512)(128)(4,1)S(1)}, pred[8]{0:T(512)(128)(4,1)}, u32[]{:S(2)}) copy-start(pred[8]{0:T(512)(128)(4,1)} %iota_compare_fusion) | copy-start | bytes 28
  167.1 0.9 copy-start.9
  167.6 1.2 copy-start.24
  168.0 5.1 %copy-start.8 = (f32[128,128]{0,1:T(8,128)S(1)}, f32[128,128]{0,1:T(8,128)}, u32[]{:S(2)}) copy-start(f32[128,128]{0,1:T(8,128)} %fusion.167) | copy-start | bytes 196612
  168.1 5.1 %copy-start.11 = (bf16[128,64]{0,1:T(8,128)(2,1)S(1)}, bf16[128,64]{0,1:T(8,128)(2,1)}, u32[]{:S(2)}) copy-start(bf16[128,64]{0,1:T(8,128)(2,1)} %copy-done.10) | copy-start | bytes 49156
  168.1 5.1 %copy-start.13 = (f32[128,32]{0,1:T(8,128)S(1)}, f32[128,32]{0,1:T(8,128)}, u32[]{:S(2)}) copy-start(f32[128,32]{0,1:T(8,128)} %copy-done.12) | copy-start | bytes 49156
  168.1 5.1 %copy-start.15 = (f32[128,32]{0,1:T(8,128)S(1)}, f32[128,32]{0,1:T(8,128)}, u32[]{:S(2)}) copy-start(f32[128,32]{0,1:T(8,128)} %copy-done.14) | copy-start | bytes 49156
  168.1 5.1 %copy-start.17 = (f32[128,32]{0,1:T(8,128)S(1)}, f32[128,32]{0,1:T(8,128)}, u32[]{:S(2)}) copy-start(f32[128,32]{0,1:T(8,128)} %get-tuple-element.32) | copy-start | bytes 49156
  168.1 5.1 %copy-start.18 = (f32[128,32]{0,1:T(8,128)S(1)}, f32[128,32]{0,1:T(8,128)}, u32[]{:S(2)}) copy-start(f32[128,32]{0,1:T(8,128)} %get-tuple-element.33) | copy-start | bytes 49156
  168.1 5.1 %copy-start.25 = (s32[128]{0:T(128)S(1)}, s32[128]{0:T(128)}, u32[]{:S(2)}) copy-start(s32[128]{0:T(128)} %get-tuple-element.54) | copy-start | bytes 1540
  168.9 12.2 %copy-start.5 = (bf16[64,4544]{1,0:T(8,128)(2,1)S(1)}, bf16[64,4544]{1,0:T(8,128)(2,1)}, u32[]{:S(2)}) copy-start(bf16[64,4544]{1,0:T(8,128)(2,1)} %param.15) | copy-start | bytes 1744900
  169.7 11.2 %all-to-all-start = ((f32[8,128,66]{1,2,0:T(8,128)}), f32[8,128,66]{1,2,0:T(8,128)S(1)}, u32[]{:S(2)}, u32[]{:S(2)}) async-start(f32[8,128,66]{1,2,0:T(8,128)} %pad_maximum_fusion.5), calls=%async_computation | async-start | bytes 589824 | tf_op jit(solution)/shard_map/all_to_all | solution.py:249
  193.2 16.6 %collective-permute-start.14 = (bf16[2,2,2,2,2,2,4544]{6,5,4,3,2,1,0:T(2,128)(2,1)S(1)}, bf16[2,2,2,2,2,2,4544]{6,5,4,3,2,1,0:T(2,128)(2,1)S(1)}, u32[]{:S(2)}, u32[]{:S(2)}) collective-permute-start(bf16[2,2,2,2,2,2,4544]{6,5,4,3,2,1,0:T(2,128)(2,1)S(1)} %fusion.16), channel_id=1, source_target_pairs={{0,16},{1,17},{2,18},{3,19},{4,20},{5,21},{6,22},{7,23},{8,24},{9,... | collective-permute-start | bytes 1744904 | tf_op jit(solution)/shard_map/ppermute | solution.py:122
  211.9 10.9 %collective-permute-start.15 = (bf16[2,2,2,2,2,4544]{5,4,3,2,1,0:T(2,128)(2,1)S(1)}, bf16[2,2,2,2,2,4544]{5,4,3,2,1,0:T(2,128)(2,1)S(1)}, u32[]{:S(2)}, u32[]{:S(2)}) collective-permute-start(bf16[2,2,2,2,2,4544]{5,4,3,2,1,0:T(2,128)(2,1)S(1)} %fusion.21), channel_id=1, source_target_pairs={{0,32},{1,33},{2,34},{3,35},{4,36},{5,37},{6,38},{7,39},{8,40},{9,... | collective-permute-start | bytes 872456 | tf_op jit(solution)/shard_map/ppermute | solution.py:122
  213.8 48.8 %copy-start.7 = (bf16[1,2,4544]{2,1,0:T(2,128)(2,1)S(1)}, bf16[1,2,4544]{2,1,0:T(2,128)(2,1)}, u32[]{:S(2)}) copy-start(bf16[1,2,4544]{2,1,0:T(2,128)(2,1)} %param.10) | copy-start | bytes 54532
  223.2 7.0 %collective-permute-start.16 = (bf16[2,2,2,2,4544]{4,3,2,1,0:T(2,128)(2,1)S(1)}, bf16[2,2,2,2,4544]{4,3,2,1,0:T(2,128)(2,1)S(1)}, u32[]{:S(2)}, u32[]{:S(2)}) collective-permute-start(bf16[2,2,2,2,4544]{4,3,2,1,0:T(2,128)(2,1)S(1)} %fusion.23), channel_id=1, source_target_pairs={{0,1},{1,0},{2,3},{3,2},{4,5},{5,4},{6,7},{7,6},{8,9},{9,8},{10,11... | collective-permute-start | bytes 436232 | tf_op jit(solution)/shard_map/ppermute | solution.py:122
  230.5 7.8 %collective-permute-start.17 = (bf16[2,2,2,4544]{3,2,1,0:T(2,128)(2,1)S(1)}, bf16[2,2,2,4544]{3,2,1,0:T(2,128)(2,1)S(1)}, u32[]{:S(2)}, u32[]{:S(2)}) collective-permute-start(bf16[2,2,2,4544]{3,2,1,0:T(2,128)(2,1)S(1)} %fusion.27), channel_id=1, source_target_pairs={{0,2},{1,3},{2,0},{3,1},{4,6},{5,7},{6,4},{7,5},{8,10},{9,11},{10,... | collective-permute-start | bytes 218120 | tf_op jit(solution)/shard_map/ppermute | solution.py:122
  238.4 9.8 %collective-permute-start.18 = (bf16[2,2,4544]{2,1,0:T(2,128)(2,1)S(1)}, bf16[2,2,4544]{2,1,0:T(2,128)(2,1)S(1)}, u32[]{:S(2)}, u32[]{:S(2)}) collective-permute-start(bf16[2,2,4544]{2,1,0:T(2,128)(2,1)S(1)} %fusion.48), channel_id=1, source_target_pairs={{0,4},{1,5},{2,6},{3,7},{4,0},{5,1},{6,2},{7,3},{8,12},{9,13},{10,... | collective-permute-start | bytes 109064 | tf_op jit(solution)/shard_map/ppermute | solution.py:122
  248.3 14.4 %collective-permute-start.19 = (bf16[2,4544]{1,0:T(2,128)(2,1)S(1)}, bf16[2,4544]{1,0:T(2,128)(2,1)S(1)}, u32[]{:S(2)}, u32[]{:S(2)}) collective-permute-start(bf16[2,4544]{1,0:T(2,128)(2,1)S(1)} %fusion.90), channel_id=1, source_target_pairs={{0,8},{1,9},{2,10},{3,11},{4,12},{5,13},{6,14},{7,15},{8,0},{9,1},... | collective-permute-start | bytes 54536 | tf_op jit(solution)/shard_map/ppermute | solution.py:122
Sparse Core Ops, SparseCore 0:
  9.4 81.0 all-gather.2

commit v4 on v3

--- a/solution.py
+++ b/solution.py
@@ -154,6 +154,41 @@
 
 
 SHORT_MAX = 2048
+
+
+def z_rounds(piece):
+    size = lax.axis_size("tz")
+    me = lax.axis_index("tz")
+    buf = piece[None]
+    for b in reversed(range(size.bit_length() - 1)):
+        other = lax.ppermute(buf, "tz", [(i, i ^ (1 << b)) for i in range(size)])
+        low = ((me >> b) & 1) == 0
+        buf = jnp.concatenate(
+            [jnp.where(low, buf, other), jnp.where(low, other, buf)], axis=0
+        )
+    return buf
+
+
+def gather_tensor(piece):
+    nx = lax.axis_size("tx")
+    buf = z_rounds(piece)
+    wide = jnp.broadcast_to(buf[None], (nx,) + buf.shape)
+    return lax.all_to_all(wide, "tx", 0, 0, tiled=True).reshape((-1,) + piece.shape)
+
+
+def slot_source(index):
+    nz = lax.axis_size("tz")
+    return (index // nz) * nz + bit_reversed(index % nz, nz.bit_length() - 1)
+
+
+def scatter_tensor(partial):
+    nx, nz = lax.axis_size("tx"), lax.axis_size("tz")
+    bits = nz.bit_length() - 1
+    buf = partial.reshape((nx, nz) + partial.shape[1:]).astype(jnp.bfloat16)
+    over_x = lax.all_to_all(buf, "tx", 0, 0, tiled=True).astype(jnp.float32).sum(0)
+    order = [int(format(c, f"0{bits}b")[::-1], 2) if bits else 0 for c in range(nz)]
+    ready = jnp.take(over_x, jnp.array(order, dtype=jnp.int32), axis=0).astype(jnp.bfloat16)
+    return lax.all_to_all(ready, "tz", 0, 0, tiled=True).astype(jnp.float32).sum(0)
 
 
 def local(
@@ -182,8 +217,11 @@
     inner_pos = group * inner_here + jnp.arange(inner_here, dtype=jnp.int32)
 
     long_local = lax.dynamic_index_in_dim(kv_cache, longest, 0, keepdims=False)
-    long_all = gather_rounds(long_local, n)
-    slot_src = layout_source(jnp.arange(n, dtype=jnp.int32), n)
+    normed = norm_rows(tokens[0], ln_gain, ln_bias)
+    both = gather_tensor(jnp.concatenate([normed.reshape(-1), long_local.reshape(-1)]))
+    token_cut = normed.size
+    long_all = both[:, token_cut:].reshape((n,) + long_local.shape)
+    slot_src = slot_source(jnp.arange(n, dtype=jnp.int32))
     long_block = slot_src[:, None] * blocks_here + jnp.arange(blocks_here, dtype=jnp.int32)
     long_pos = (long_block[:, :, None] * inner_all + inner_pos).reshape(-1)
     long_keys = long_all.reshape(-1, 2 * width)
@@ -193,8 +231,7 @@
     short_keys = spread_from_first(short_gath, "tx").reshape(requests, -1, 2 * width)
     short_pos = (jnp.arange(short_blocks, dtype=jnp.int32)[:, None] * inner_all + inner_pos).reshape(-1)
 
-    normed = norm_rows(tokens[0], ln_gain, ln_bias)
-    piece = gather_rounds(normed, n).reshape(n * per_device, width_model)
+    piece = both[:, :token_cut].reshape(n * per_device, width_model)
     projected = jnp.concatenate(
         [
             jnp.dot(piece, q_weight, preferred_element_type=jnp.float32),
@@ -205,7 +242,7 @@
     )
     span = projected.shape[0]
     row = jnp.arange(span, dtype=jnp.int32)
-    token_pos = layout_source(row // per_device, n) * per_device + row % per_device
+    token_pos = slot_source(row // per_device) * per_device + row % per_device
     own_length = lax.dynamic_index_in_dim(cache_lengths, group, 0, keepdims=False)
     places = own_length + token_pos
     cosine, sine = rotary_tables(places, width)
@@ -263,7 +300,7 @@
     partial = jnp.dot(attn, dense_weight, preferred_element_type=jnp.float32) + jnp.dot(
         hidden, down_weight, preferred_element_type=jnp.float32
     )
-    layer_rows = scatter_rounds(partial.reshape(n, per_device, width_model), n)
+    layer_rows = scatter_tensor(partial.reshape(n, per_device, width_model))
     return (tokens[0].astype(jnp.float32) + layer_rows).astype(jnp.bfloat16)[None]
 
 

time: 272 us -> 236 us (0.87)
  the two profiles are of different devices: /device:TPU:4 before, /device:TPU:64 now
where the time goes in v4:
time: 236 us; the launch traced here: 235 us
  waiting for transfers between devices  71.5 us (30%)
  starting transfers between devices  52.4 us (22%)
  blocking collectives  39.4 us (17%)
  other arithmetic  20.6 us (9%)
  local copies, waits for them, and re-layouts  18.8 us (8%)
  matrix products  16.2 us (7%)
  between operations  15.9 us (7%)
    ppermute x4, starting transfers between devices, z_rounds(): other = lax.ppermute(buf, 'tz', [(i, i ^ 1 << b) for i in range(size)])  31.9 us
    all_to_all x1, blocking collectives, scatter_tensor(): lax.all_to_all(ready, 'tz', 0, 0, tiled=True).astype(jnp.float32).sum(0)  27.2 us
    all_gather x1, waiting for transfers between devices, local(): lax.all_gather(kv_cache, 'tz', axis=1, tiled=True)[:, :short_blocks]  16.9 us
    all_to_all x1, waiting for transfers between devices, scatter_tensor(): lax.all_to_all(buf, 'tx', 0, 0, tiled=True).astype(jnp.float32).sum(0)  16.1 us
    ppermute x4, waiting for transfers between devices, z_rounds(): other = lax.ppermute(buf, 'tz', [(i, i ^ 1 << b) for i in range(size)])  14 us
    all_to_all x1, waiting for transfers between devices, gather_tensor(): lax.all_to_all(wide, 'tx', 0, 0, tiled=True).reshape((-1,) + piece.shape)  13.9 us
    all_gather x1, blocking collectives, local(): q_all = lax.all_gather(query_rows, 'dp', axis=0, tiled=False)  12.1 us
    all_to_all x1, waiting for transfers between devices, local(): got = lax.all_to_all(packed, 'dp', 0, 0, tiled=True)  7.51 us
  transfers between devices with their start and end apart: 10, of which 9 were waited for; matrix products, arithmetic and copies ran while one was open for 13% of the time, Pallas kernels for 0%

profile of v4, /device:TPU:64, one launch (start us, length us, event | category | flops | bytes accessed | tf_op | source)
XLA Modules:
  0.0 234.7 jit_solution(17665344807848158370)
XLA Ops:
  6.5 1.0 convert_reduce_fusion.2
  8.3 1.3 iota_reduce_fusion
  10.9 0.9 fusion.38
  15.4 13.9 %collective-permute-start = (bf16[1,17280]{1,0:T(2,128)(2,1)S(1)}, bf16[1,17280]{1,0:T(2,128)(2,1)S(1)}, u32[]{:S(2)}, u32[]{:S(2)}) collective-permute-start(bf16[1,17280]{1,0:T(2,128)(2,1)S(1)} %broadcast_in_dim.147), channel_id=1, source_target_pairs={{0,8},{1,9},{2,10},{3,11},{4,12},{5,13},{6,14},{7,15},{8,0},{9,1},... | collective-permute-start | bytes 103688 | tf_op jit(solution)/shard_map/ppermute | solution.py:164
  29.3 3.2 %collective-permute-done = bf16[1,17280]{1,0:T(2,128)(2,1)S(1)} collective-permute-done((bf16[1,17280]{1,0:T(2,128)(2,1)S(1)}, bf16[1,17280]{1,0:T(2,128)(2,1)S(1)}, u32[]{:S(2)}, u32[]{:S(2)}) %collective-permute-start) | collective-permute-done | bytes 34592 | tf_op jit(solution)/shard_map/ppermute | solution.py:164
  32.8 10.1 %collective-permute-start.1 = (bf16[2,17280]{1,0:T(2,128)(2,1)S(1)}, bf16[2,17280]{1,0:T(2,128)(2,1)S(1)}, u32[]{:S(2)}, u32[]{:S(2)}) collective-permute-start(bf16[2,17280]{1,0:T(2,128)(2,1)S(1)} %pad_maximum_fusion.4), channel_id=1, source_target_pairs={{0,4},{1,5},{2,6},{3,7},{4,0},{5,1},{6,2},{7,3},{8,12},{9,13},{10,... | collective-permute-start | bytes 207368 | tf_op jit(solution)/shard_map/ppermute | solution.py:164
  42.9 3.1 %collective-permute-done.1 = bf16[2,17280]{1,0:T(2,128)(2,1)S(1)} collective-permute-done((bf16[2,17280]{1,0:T(2,128)(2,1)S(1)}, bf16[2,17280]{1,0:T(2,128)(2,1)S(1)}, u32[]{:S(2)}, u32[]{:S(2)}) %collective-permute-start.1) | collective-permute-done | bytes 69152 | tf_op jit(solution)/shard_map/ppermute | solution.py:164
  46.4 4.4 %collective-permute-start.2 = (bf16[4,17280]{1,0:T(4,128)(2,1)S(1)}, bf16[4,17280]{1,0:T(4,128)(2,1)S(1)}, u32[]{:S(2)}, u32[]{:S(2)}) collective-permute-start(bf16[4,17280]{1,0:T(4,128)(2,1)S(1)} %pad_maximum_fusion.3), channel_id=1, source_target_pairs={{0,2},{1,3},{2,0},{3,1},{4,6},{5,7},{6,4},{7,5},{8,10},{9,11},{10,... | collective-permute-start | bytes 414728 | tf_op jit(solution)/shard_map/ppermute | solution.py:164
  50.8 3.5 %collective-permute-done.2 = bf16[4,17280]{1,0:T(4,128)(2,1)S(1)} collective-permute-done((bf16[4,17280]{1,0:T(4,128)(2,1)S(1)}, bf16[4,17280]{1,0:T(4,128)(2,1)S(1)}, u32[]{:S(2)}, u32[]{:S(2)}) %collective-permute-start.2) | collective-permute-done | bytes 138272 | tf_op jit(solution)/shard_map/ppermute | solution.py:164
  54.7 3.5 %collective-permute-start.3 = (bf16[8,17280]{1,0:T(8,128)(2,1)S(1)}, bf16[8,17280]{1,0:T(8,128)(2,1)S(1)}, u32[]{:S(2)}, u32[]{:S(2)}) collective-permute-start(bf16[8,17280]{1,0:T(8,128)(2,1)S(1)} %pad_maximum_fusion.2), channel_id=1, source_target_pairs={{0,1},{1,0},{2,3},{3,2},{4,5},{5,4},{6,7},{7,6},{8,9},{9,8},{10,11... | collective-permute-start | bytes 829448 | tf_op jit(solution)/shard_map/ppermute | solution.py:164
  58.9 4.2 %collective-permute-done.3 = bf16[8,17280]{1,0:T(8,128)(2,1)S(1)} collective-permute-done((bf16[8,17280]{1,0:T(8,128)(2,1)S(1)}, bf16[8,17280]{1,0:T(8,128)(2,1)S(1)}, u32[]{:S(2)}, u32[]{:S(2)}) %collective-permute-start.3) | collective-permute-done | bytes 276512 | tf_op jit(solution)/shard_map/ppermute | solution.py:164
  63.4 1.5 broadcast_in_dim.148
  64.9 4.3 %all-to-all-start = ((bf16[4,16,17280]{2,1,0:T(8,128)(2,1)}), bf16[4,16,17280]{2,1,0:T(8,128)(2,1)S(1)}, u32[]{:S(2)}, u32[]{:S(2)}) async-start(bf16[4,16,17280]{2,1,0:T(8,128)(2,1)} %broadcast_in_dim.148), calls=%async_computation | async-start | bytes 4423680 | tf_op jit(solution)/shard_map/all_to_all | solution.py:176
  69.3 1.4 add_compare_fusion
  70.7 1.6 lt.86
  74.3 1.2 iota_compare_fusion
  75.6 1.1 fusion.91
  76.7 1.3 compare_and_fusion
  78.8 13.9 %all-to-all-done = bf16[4,16,17280]{2,1,0:T(8,128)(2,1)S(1)} async-done(((bf16[4,16,17280]{2,1,0:T(8,128)(2,1)}), bf16[4,16,17280]{2,1,0:T(8,128)(2,1)S(1)}, u32[]{:S(2)}, u32[]{:S(2)}) %all-to-all-start) | async-done | bytes 2211872 | tf_op jit(solution)/shard_map/all_to_all | solution.py:176
  92.7 1.1 slice.69
  93.8 1.1 slice.75
  94.9 1.9 reshape.589
  96.9 1.3 reshape_reshape.4
  98.2 1.7 fusion.139
  99.9 12.1 %all-gather = bf16[1024,64]{0,1:T(8,128)(2,1)S(1)} all-gather(bf16[128,64]{0,1:T(8,128)(2,1)S(1)} %fusion.75), channel_id=2, replica_groups=mesh['dp'=8,'tx'=4,'tz'=16] {'dp'}, dimensions={0}, use_global_device_ids=true | all-gather | bytes 147456 | tf_op jit(solution)/shard_map/all_gather | solution.py:264
  112.1 1.2 fusion.140
  113.3 1.1 fusion.135
  114.5 16.9 %all-gather.3.cloned.1.call-done = bf16[8,128,8,128]{3,2,1,0:T(8,128)(2,1)} async-done(((bf16[8,8,8,128]{3,2,1,0:T(8,128)(2,1)}), bf16[8,128,8,128]{3,2,1,0:T(8,128)(2,1)}) %all-gather.3.cloned.1.call-update) | async-done | bytes 2097168 | tf_op jit(solution)/shard_map/all_gather | solution.py:230
  131.4 1.2 slice.72
  132.6 3.4 %collective-permute-start.4 = (bf16[8,32,8,128]{3,2,1,0:T(8,128)(2,1)S(1)}, bf16[8,32,8,128]{3,2,1,0:T(8,128)(2,1)S(1)}, u32[]{:S(2)}, u32[]{:S(2)}) collective-permute-start(bf16[8,32,8,128]{3,2,1,0:T(8,128)(2,1)S(1)} %slice.72), channel_id=1, source_target_pairs={{0,16},{1,17},{2,18},{3,19},{4,20},{5,21},{6,22},{7,23},{8,24},{9,... | collective-permute-start | bytes 1572872 | tf_op jit(solution)/shard_map/ppermute | solution.py:135
  136.0 1.4 slice_negate_fusion
  137.4 2.3 fusion.10
  139.7 3.0 %collective-permute-done.4 = bf16[8,32,8,128]{3,2,1,0:T(8,128)(2,1)S(1)} collective-permute-done((bf16[8,32,8,128]{3,2,1,0:T(8,128)(2,1)S(1)}, bf16[8,32,8,128]{3,2,1,0:T(8,128)(2,1)S(1)}, u32[]{:S(2)}, u32[]{:S(2)}) %collective-permute-start.4) | collective-permute-done | bytes 524320 | tf_op jit(solution)/shard_map/ppermute | solution.py:135
  142.7 1.9 broadcast_select_fusion
  144.6 2.1 collective-permute-start.5
  146.7 1.0 fusion.2
  147.7 5.2 %fusion.34 = f32[128,4544]{0,1:T(8,128)} fusion(bf16[142,4544]{1,0:T(8,128)(2,1)S(1)} %copy-done, bf16[128,4544]{1,0:T(8,128)(2,1)} %copy-done.1, bf16[4544,142]{0,1:T(8,128)(2,1)} %param.17), kind=kOutput, calls=%fused_computation.71 | convolution fusion | flops 331548416 | bytes 6070784 | tf_op jit(solution)/shard_map/dot_general | solution.py:300
  152.9 1.1 select_bitcast_fusion
  156.6 4.3 %all-to-all-start.1 = ((f32[8,128,66]{1,2,0:T(8,128)}), f32[8,128,66]{1,2,0:T(8,128)S(1)}, u32[]{:S(2)}, u32[]{:S(2)}) async-start(f32[8,128,66]{1,2,0:T(8,128)} %pad_maximum_fusion.1), calls=%async_computation.1 | async-start | bytes 589824 | tf_op jit(solution)/shard_map/all_to_all | solution.py:286
  161.2 7.5 %all-to-all-done.1 = f32[8,128,66]{1,2,0:T(8,128)S(1)} async-done(((f32[8,128,66]{1,2,0:T(8,128)}), f32[8,128,66]{1,2,0:T(8,128)S(1)}, u32[]{:S(2)}, u32[]{:S(2)}) %all-to-all-start.1) | async-done | bytes 270368 | tf_op jit(solution)/shard_map/all_to_all | solution.py:286
  168.8 3.3 %fusion = bf16[128,4544]{0,1:T(8,128)(2,1)} fusion(f32[128,4544]{0,1:T(8,128)} %fusion.34, bf16[64,4544]{1,0:T(8,128)(2,1)S(1)} %copy-done.6, f32[128,128]{0,1:T(8,128)S(1)} %get-tuple-element.37, f32[128]{0:T(128)S(1)} %get-tuple-element.36, f32[128,64]{0,1:T(8,128)S(1)} %fusion.21, f32[128,128]{0,1:T(8,128)S(1)} %copy-done.8, ...), kind=kOutput, calls=%fused_computation.2 | convolution fusion | flops 77783040 | bytes 4196352 | tf_op jit(solution)/shard_map/dot_general | solution.py:300
  172.1 1.6 copy.52
  173.7 1.3 convert_element_type.81
  175.0 6.4 %all-to-all-start.2 = ((bf16[4,16,2,4544]{3,2,1,0:T(2,128)(2,1)}), bf16[4,16,2,4544]{3,2,1,0:T(2,128)(2,1)S(1)}, u32[]{:S(2)}, u32[]{:S(2)}) async-start(bf16[4,16,2,4544]{3,2,1,0:T(2,128)(2,1)} %convert_element_type.81), calls=%async_computation.2 | async-start | bytes 2359296 | tf_op jit(solution)/shard_map/all_to_all | solution.py:188
  181.4 16.1 %all-to-all-done.2 = bf16[4,16,2,4544]{3,2,1,0:T(2,128)(2,1)S(1)} async-done(((bf16[4,16,2,4544]{3,2,1,0:T(2,128)(2,1)}), bf16[4,16,2,4544]{3,2,1,0:T(2,128)(2,1)S(1)}, u32[]{:S(2)}, u32[]{:S(2)}) %all-to-all-start.2) | async-done | bytes 1163296 | tf_op jit(solution)/shard_map/all_to_all | solution.py:188
  197.5 1.2 convert_reduce_fusion
  198.7 1.1 gather_fusion
  199.8 27.2 %all_to_all.20 = bf16[16,2,4544]{2,1,0:T(2,128)(2,1)S(1)} all-to-all(bf16[16,2,4544]{2,1,0:T(2,128)(2,1)S(1)} %gather_fusion), channel_id=1, replica_groups=mesh['dp'=8,'tx'=4,'tz'=16] {'tz'}, dimensions={0} | all-to-all | bytes 581632 | tf_op jit(solution)/shard_map/all_to_all | solution.py:191
  (112 shorter events, 12.2 us)
Async XLA Ops:
  6.5 141.1 %copy-start = (bf16[142,4544]{1,0:T(8,128)(2,1)S(1)}, bf16[142,4544]{1,0:T(8,128)(2,1)}, u32[]{:S(2)}) copy-start(bf16[142,4544]{1,0:T(8,128)(2,1)} %param.18) | copy-start | bytes 3871492
  6.5 124.9 %all-gather.3.cloned.1.call-start = ((), (), s32[]{:S(2)}) async-start(), calls=%async_computation.4 | async-start | bytes 2228224 | tf_op jit(solution)/shard_map/all_gather | solution.py:230
  15.3 42.9 %copy-start.22 = (s32[8]{0:T(128)S(1)}, s32[8]{0:T(128)}, u32[]{:S(2)}) copy-start(s32[8]{0:T(128)} %param.20) | copy-start | bytes 100
  15.4 17.1 %collective-permute-start = (bf16[1,17280]{1,0:T(2,128)(2,1)S(1)}, bf16[1,17280]{1,0:T(2,128)(2,1)S(1)}, u32[]{:S(2)}, u32[]{:S(2)}) collective-permute-start(bf16[1,17280]{1,0:T(2,128)(2,1)S(1)} %broadcast_in_dim.147), channel_id=1, source_target_pairs={{0,8},{1,9},{2,10},{3,11},{4,12},{5,13},{6,14},{7,15},{8,0},{9,1},... | collective-permute-start | bytes 103688 | tf_op jit(solution)/shard_map/ppermute | solution.py:164
  32.8 13.2 %collective-permute-start.1 = (bf16[2,17280]{1,0:T(2,128)(2,1)S(1)}, bf16[2,17280]{1,0:T(2,128)(2,1)S(1)}, u32[]{:S(2)}, u32[]{:S(2)}) collective-permute-start(bf16[2,17280]{1,0:T(2,128)(2,1)S(1)} %pad_maximum_fusion.4), channel_id=1, source_target_pairs={{0,4},{1,5},{2,6},{3,7},{4,0},{5,1},{6,2},{7,3},{8,12},{9,13},{10,... | collective-permute-start | bytes 207368 | tf_op jit(solution)/shard_map/ppermute | solution.py:164
  46.4 7.9 %collective-permute-start.2 = (bf16[4,17280]{1,0:T(4,128)(2,1)S(1)}, bf16[4,17280]{1,0:T(4,128)(2,1)S(1)}, u32[]{:S(2)}, u32[]{:S(2)}) collective-permute-start(bf16[4,17280]{1,0:T(4,128)(2,1)S(1)} %pad_maximum_fusion.3), channel_id=1, source_target_pairs={{0,2},{1,3},{2,0},{3,1},{4,6},{5,7},{6,4},{7,5},{8,10},{9,11},{10,... | collective-permute-start | bytes 414728 | tf_op jit(solution)/shard_map/ppermute | solution.py:164
  54.7 8.4 %collective-permute-start.3 = (bf16[8,17280]{1,0:T(8,128)(2,1)S(1)}, bf16[8,17280]{1,0:T(8,128)(2,1)S(1)}, u32[]{:S(2)}, u32[]{:S(2)}) collective-permute-start(bf16[8,17280]{1,0:T(8,128)(2,1)S(1)} %pad_maximum_fusion.2), channel_id=1, source_target_pairs={{0,1},{1,0},{2,3},{3,2},{4,5},{5,4},{6,7},{7,6},{8,9},{9,8},{10,11... | collective-permute-start | bytes 829448 | tf_op jit(solution)/shard_map/ppermute | solution.py:164
  58.9 10.4 %copy-start.24 = (s32[8]{0:T(128)}, s32[8]{0:T(128)S(1)}, u32[]{:S(2)}) copy-start(s32[8]{0:T(128)S(1)} %iota_add_fusion) | copy-start | bytes 100
  64.9 27.8 %all-to-all-start = ((bf16[4,16,17280]{2,1,0:T(8,128)(2,1)}), bf16[4,16,17280]{2,1,0:T(8,128)(2,1)S(1)}, u32[]{:S(2)}, u32[]{:S(2)}) async-start(bf16[4,16,17280]{2,1,0:T(8,128)(2,1)} %broadcast_in_dim.148), calls=%async_computation | async-start | bytes 4423680 | tf_op jit(solution)/shard_map/all_to_all | solution.py:176
  94.9 1.9 copy-start.4
  96.8 15.3 %copy-start.1 = (bf16[128,4544]{1,0:T(8,128)(2,1)}, bf16[128,4544]{1,0:T(8,128)(2,1)S(1)}, u32[]{:S(2)}) copy-start(bf16[128,4544]{1,0:T(8,128)(2,1)S(1)} %reshape.589) | copy-start | bytes 3489796
  98.2 1.7 copy-start.12
  98.2 1.7 copy-start.14
  98.2 13.9 %copy-start.5 = (bf16[4544,128]{1,0:T(8,128)(2,1)S(1)}, bf16[4544,128]{1,0:T(8,128)(2,1)}, u32[]{:S(2)}) copy-start(bf16[4544,128]{1,0:T(8,128)(2,1)} %param.15) | copy-start | bytes 3489796
  99.9 12.2 %copy-start.10 = (bf16[128,64]{0,1:T(8,128)(2,1)}, bf16[128,64]{0,1:T(8,128)(2,1)S(1)}, u32[]{:S(2)}) copy-start(bf16[128,64]{0,1:T(8,128)(2,1)S(1)} %fusion.75) | copy-start | bytes 49156
  112.1 1.3 copy-start.2
  112.1 1.3 copy-start.16
  131.4 6.0 %copy-start.3 = (bf16[4096,128]{1,0:T(8,128)(2,1)S(1)}, bf16[4096,128]{1,0:T(8,128)(2,1)}, u32[]{:S(2)}) copy-start(bf16[4096,128]{1,0:T(8,128)(2,1)} %reshape_reshape.4) | copy-start | bytes 3145732
  132.6 10.1 %collective-permute-start.4 = (bf16[8,32,8,128]{3,2,1,0:T(8,128)(2,1)S(1)}, bf16[8,32,8,128]{3,2,1,0:T(8,128)(2,1)S(1)}, u32[]{:S(2)}, u32[]{:S(2)}) collective-permute-start(bf16[8,32,8,128]{3,2,1,0:T(8,128)(2,1)S(1)} %slice.72), channel_id=1, source_target_pairs={{0,16},{1,17},{2,18},{3,19},{4,20},{5,21},{6,22},{7,23},{8,24},{9,... | collective-permute-start | bytes 1572872 | tf_op jit(solution)/shard_map/ppermute | solution.py:135
  139.7 6.9 %copy-start.19 = (f32[128]{0:T(128)S(1)}, f32[128]{0:T(128)}, u32[]{:S(2)}) copy-start(f32[128]{0:T(128)} %get-tuple-element.34) | copy-start | bytes 1540
  144.6 8.3 %collective-permute-start.5 = (bf16[8,32,8,128]{3,2,1,0:T(8,128)(2,1)}, bf16[8,32,8,128]{3,2,1,0:T(8,128)(2,1)}, u32[]{:S(2)}, u32[]{:S(2)}) collective-permute-start(bf16[8,32,8,128]{3,2,1,0:T(8,128)(2,1)} %broadcast_select_fusion), channel_id=1, source_target_pairs={{0,48},{16,32},{1,49},{17,33},{2,50},{18,34},{3,51},{19,35},{4,52}... | collective-permute-start | bytes 1572872 | tf_op jit(solution)/shard_map/ppermute | solution.py:135
  152.8 1.2 copy-start.21
  152.8 1.6 copy-start.20
  152.8 1.6 copy-start.23
  154.0 0.9 copy-start.9
  154.5 1.2 copy-start.25
  154.9 6.0 %copy-start.8 = (f32[128,128]{0,1:T(8,128)S(1)}, f32[128,128]{0,1:T(8,128)}, u32[]{:S(2)}) copy-start(f32[128,128]{0,1:T(8,128)} %fusion.140) | copy-start | bytes 196612
  154.9 5.9 %copy-start.11 = (bf16[128,64]{0,1:T(8,128)(2,1)S(1)}, bf16[128,64]{0,1:T(8,128)(2,1)}, u32[]{:S(2)}) copy-start(bf16[128,64]{0,1:T(8,128)(2,1)} %copy-done.10) | copy-start | bytes 49156
  154.9 5.9 %copy-start.13 = (f32[128,32]{0,1:T(8,128)S(1)}, f32[128,32]{0,1:T(8,128)}, u32[]{:S(2)}) copy-start(f32[128,32]{0,1:T(8,128)} %get-tuple-element.28) | copy-start | bytes 49156
  154.9 5.9 %copy-start.15 = (f32[128,32]{0,1:T(8,128)S(1)}, f32[128,32]{0,1:T(8,128)}, u32[]{:S(2)}) copy-start(f32[128,32]{0,1:T(8,128)} %get-tuple-element.29) | copy-start | bytes 49156
  155.0 5.9 %copy-start.17 = (f32[128,32]{0,1:T(8,128)S(1)}, f32[128,32]{0,1:T(8,128)}, u32[]{:S(2)}) copy-start(f32[128,32]{0,1:T(8,128)} %get-tuple-element.20) | copy-start | bytes 49156
  155.0 5.9 %copy-start.18 = (f32[128,32]{0,1:T(8,128)S(1)}, f32[128,32]{0,1:T(8,128)}, u32[]{:S(2)}) copy-start(f32[128,32]{0,1:T(8,128)} %get-tuple-element.21) | copy-start | bytes 49156
  155.0 5.9 %copy-start.27 = (s32[128]{0:T(128)S(1)}, s32[128]{0:T(128)}, u32[]{:S(2)}) copy-start(s32[128]{0:T(128)} %get-tuple-element.38) | copy-start | bytes 1540
  155.7 13.1 %copy-start.6 = (bf16[64,4544]{1,0:T(8,128)(2,1)S(1)}, bf16[64,4544]{1,0:T(8,128)(2,1)}, u32[]{:S(2)}) copy-start(bf16[64,4544]{1,0:T(8,128)(2,1)} %param.16) | copy-start | bytes 1744900
  156.6 12.1 %all-to-all-start.1 = ((f32[8,128,66]{1,2,0:T(8,128)}), f32[8,128,66]{1,2,0:T(8,128)S(1)}, u32[]{:S(2)}, u32[]{:S(2)}) async-start(f32[8,128,66]{1,2,0:T(8,128)} %pad_maximum_fusion.1), calls=%async_computation.1 | async-start | bytes 589824 | tf_op jit(solution)/shard_map/all_to_all | solution.py:286
  175.0 6.4 %copy-start.26 = (s32[16]{0:T(128)S(1)}, s32[16]{0:T(128)}, u32[]{:S(2)}) copy-start(s32[16]{0:T(128)} %constant.238) | copy-start | bytes 196
  175.0 22.5 %all-to-all-start.2 = ((bf16[4,16,2,4544]{3,2,1,0:T(2,128)(2,1)}), bf16[4,16,2,4544]{3,2,1,0:T(2,128)(2,1)S(1)}, u32[]{:S(2)}, u32[]{:S(2)}) async-start(bf16[4,16,2,4544]{3,2,1,0:T(2,128)(2,1)} %convert_element_type.81), calls=%async_computation.2 | async-start | bytes 2359296 | tf_op jit(solution)/shard_map/all_to_all | solution.py:188
  181.4 45.7 %copy-start.7 = (bf16[1,2,4544]{2,1,0:T(2,128)(2,1)S(1)}, bf16[1,2,4544]{2,1,0:T(2,128)(2,1)}, u32[]{:S(2)}) copy-start(bf16[1,2,4544]{2,1,0:T(2,128)(2,1)} %param.11) | copy-start | bytes 54532
Sparse Core Ops, SparseCore 0:
  58.4 73.0 all-gather.2

commit v5 on v4

--- a/solution.py
+++ b/solution.py
@@ -228,7 +228,6 @@
 
     short_blocks = -(-SHORT_MAX // inner_all)
     short_gath = lax.all_gather(kv_cache, "tz", axis=1, tiled=True)[:, :short_blocks]
-    short_keys = spread_from_first(short_gath, "tx").reshape(requests, -1, 2 * width)
     short_pos = (jnp.arange(short_blocks, dtype=jnp.int32)[:, None] * inner_all + inner_pos).reshape(-1)
 
     piece = both[:, :token_cut].reshape(n * per_device, width_model)
@@ -262,14 +261,19 @@
     query_rows = queries.reshape(rows, width)
 
     q_all = lax.all_gather(query_rows, "dp", axis=0, tiled=False)
+    q_long = lax.dynamic_index_in_dim(q_all, longest, 0, keepdims=False)
+    long_v, long_m, long_s = partial_state(
+        q_long, long_keys[:, :width], long_keys[:, width:], (long_pos < long_length)[None, :]
+    )
+    down_part = jnp.dot(hidden, down_weight, preferred_element_type=jnp.float32)
+    short_gath, long_v, long_m, long_s, down_part = lax.optimization_barrier(
+        (short_gath, long_v, long_m, long_s, down_part)
+    )
+    short_keys = spread_from_first(short_gath, "tx").reshape(requests, -1, 2 * width)
     which = jnp.arange(requests, dtype=jnp.int32)
     short_valid = (short_pos[None, :] < cache_lengths[:, None]) & (which != longest)[:, None]
     short_state = partial_state(
         q_all, short_keys[..., :width], short_keys[..., width:], short_valid[:, None, :]
-    )
-    q_long = lax.dynamic_index_in_dim(q_all, longest, 0, keepdims=False)
-    long_v, long_m, long_s = partial_state(
-        q_long, long_keys[:, :width], long_keys[:, width:], (long_pos < long_length)[None, :]
     )
     is_long = which == longest
     state_all = combine(
@@ -297,9 +301,7 @@
     causal = token_pos[None, :] <= pos_of_row[:, None]
     summed, best, total = absorb(state, query_rows, new_keys, new_values, causal)
     attn = (summed / total[:, None]).astype(jnp.bfloat16)
-    partial = jnp.dot(attn, dense_weight, preferred_element_type=jnp.float32) + jnp.dot(
-        hidden, down_weight, preferred_element_type=jnp.float32
-    )
+    partial = jnp.dot(attn, dense_weight, preferred_element_type=jnp.float32) + down_part
     layer_rows = scatter_tensor(partial.reshape(n, per_device, width_model))
     return (tokens[0].astype(jnp.float32) + layer_rows).astype(jnp.bfloat16)[None]
 

time: 236 us -> 234 us (level)
  other arithmetic: 20.6 us -> 15.5 us
    all_gather x1, waiting for transfers between devices: 16.9 us -> 10.3 us  [local(): lax.all_gather(kv_cache, 'tz', axis=1, tiled=True)[:, :short_blocks]]
    ppermute x2, waiting for transfers between devices: 3 us -> 8.04 us  [spread_from_first(): got = lax.ppermute(x, name, pairs)]
    all_to_all x1, waiting for transfers between devices: 13.9 us -> 16.8 us  [gather_tensor(): lax.all_to_all(wide, 'tx', 0, 0, tiled=True).reshape((-1,) + piece.shape)]
  transfers between devices with their start and end apart: 10 -> 10, of which waited for: 9 -> 10; matrix products, arithmetic and copies ran while one was open for 13% -> 12% of each run, Pallas kernels for 0% -> 0%
where the time goes in v5:
time: 234 us; the launch traced here: 233 us
  waiting for transfers between devices  73.5 us (31%)
  starting transfers between devices  53.6 us (23%)
  blocking collectives  39.5 us (17%)
  local copies, waits for them, and re-layouts  19.4 us (8%)
  between operations  15.9 us (7%)
  other arithmetic  15.5 us (7%)
  matrix products  15.1 us (6%)
    ppermute x4, starting transfers between devices, z_rounds(): other = lax.ppermute(buf, 'tz', [(i, i ^ 1 << b) for i in range(size)])  31.9 us
    all_to_all x1, blocking collectives, scatter_tensor(): lax.all_to_all(ready, 'tz', 0, 0, tiled=True).astype(jnp.float32).sum(0)  27.4 us
    all_to_all x1, waiting for transfers between devices, gather_tensor(): lax.all_to_all(wide, 'tx', 0, 0, tiled=True).reshape((-1,) + piece.shape)  16.8 us
    all_to_all x1, waiting for transfers between devices, scatter_tensor(): lax.all_to_all(buf, 'tx', 0, 0, tiled=True).astype(jnp.float32).sum(0)  16.1 us
    ppermute x4, waiting for transfers between devices, z_rounds(): other = lax.ppermute(buf, 'tz', [(i, i ^ 1 << b) for i in range(size)])  14.7 us
    all_gather x1, blocking collectives, local(): q_all = lax.all_gather(query_rows, 'dp', axis=0, tiled=False)  12.1 us
    all_gather x1, waiting for transfers between devices, local(): lax.all_gather(kv_cache, 'tz', axis=1, tiled=True)[:, :short_blocks]  10.3 us
    ppermute x2, waiting for transfers between devices, spread_from_first(): got = lax.ppermute(x, name, pairs)  8.04 us
  transfers between devices with their start and end apart: 10, of which 10 were waited for; matrix products, arithmetic and copies ran while one was open for 12% of the time, Pallas kernels for 0%

profile of v5, /device:TPU:64, one launch (start us, length us, event | category | flops | bytes accessed | tf_op | source)
XLA Modules:
  0.0 232.6 jit_solution(17383636290066094947)
XLA Ops:
  6.5 1.0 convert_reduce_fusion.2
  7.5 0.8 reshape.592
  8.3 1.4 iota_reduce_fusion
  10.9 0.7 add.273
  12.6 0.9 fusion.38
  15.4 13.9 %collective-permute-start = (bf16[1,17280]{1,0:T(2,128)(2,1)S(1)}, bf16[1,17280]{1,0:T(2,128)(2,1)S(1)}, u32[]{:S(2)}, u32[]{:S(2)}) collective-permute-start(bf16[1,17280]{1,0:T(2,128)(2,1)S(1)} %broadcast_in_dim.147), channel_id=1, source_target_pairs={{0,8},{1,9},{2,10},{3,11},{4,12},{5,13},{6,14},{7,15},{8,0},{9,1},... | collective-permute-start | bytes 103688 | tf_op jit(solution)/shard_map/ppermute | solution.py:164
  29.3 3.2 %collective-permute-done = bf16[1,17280]{1,0:T(2,128)(2,1)S(1)} collective-permute-done((bf16[1,17280]{1,0:T(2,128)(2,1)S(1)}, bf16[1,17280]{1,0:T(2,128)(2,1)S(1)}, u32[]{:S(2)}, u32[]{:S(2)}) %collective-permute-start) | collective-permute-done | bytes 34592 | tf_op jit(solution)/shard_map/ppermute | solution.py:164
  32.8 10.1 %collective-permute-start.1 = (bf16[2,17280]{1,0:T(2,128)(2,1)S(1)}, bf16[2,17280]{1,0:T(2,128)(2,1)S(1)}, u32[]{:S(2)}, u32[]{:S(2)}) collective-permute-start(bf16[2,17280]{1,0:T(2,128)(2,1)S(1)} %pad_maximum_fusion.4), channel_id=1, source_target_pairs={{0,4},{1,5},{2,6},{3,7},{4,0},{5,1},{6,2},{7,3},{8,12},{9,13},{10,... | collective-permute-start | bytes 207368 | tf_op jit(solution)/shard_map/ppermute | solution.py:164
  42.9 3.1 %collective-permute-done.1 = bf16[2,17280]{1,0:T(2,128)(2,1)S(1)} collective-permute-done((bf16[2,17280]{1,0:T(2,128)(2,1)S(1)}, bf16[2,17280]{1,0:T(2,128)(2,1)S(1)}, u32[]{:S(2)}, u32[]{:S(2)}) %collective-permute-start.1) | collective-permute-done | bytes 69152 | tf_op jit(solution)/shard_map/ppermute | solution.py:164
  46.4 4.4 %collective-permute-start.2 = (bf16[4,17280]{1,0:T(4,128)(2,1)S(1)}, bf16[4,17280]{1,0:T(4,128)(2,1)S(1)}, u32[]{:S(2)}, u32[]{:S(2)}) collective-permute-start(bf16[4,17280]{1,0:T(4,128)(2,1)S(1)} %pad_maximum_fusion.3), channel_id=1, source_target_pairs={{0,2},{1,3},{2,0},{3,1},{4,6},{5,7},{6,4},{7,5},{8,10},{9,11},{10,... | collective-permute-start | bytes 414728 | tf_op jit(solution)/shard_map/ppermute | solution.py:164
  50.8 3.5 %collective-permute-done.2 = bf16[4,17280]{1,0:T(4,128)(2,1)S(1)} collective-permute-done((bf16[4,17280]{1,0:T(4,128)(2,1)S(1)}, bf16[4,17280]{1,0:T(4,128)(2,1)S(1)}, u32[]{:S(2)}, u32[]{:S(2)}) %collective-permute-start.2) | collective-permute-done | bytes 138272 | tf_op jit(solution)/shard_map/ppermute | solution.py:164
  54.7 3.5 %collective-permute-start.3 = (bf16[8,17280]{1,0:T(8,128)(2,1)S(1)}, bf16[8,17280]{1,0:T(8,128)(2,1)S(1)}, u32[]{:S(2)}, u32[]{:S(2)}) collective-permute-start(bf16[8,17280]{1,0:T(8,128)(2,1)S(1)} %pad_maximum_fusion.2), channel_id=1, source_target_pairs={{0,1},{1,0},{2,3},{3,2},{4,5},{5,4},{6,7},{7,6},{8,9},{9,8},{10,11... | collective-permute-start | bytes 829448 | tf_op jit(solution)/shard_map/ppermute | solution.py:164
  58.2 4.9 %collective-permute-done.3 = bf16[8,17280]{1,0:T(8,128)(2,1)S(1)} collective-permute-done((bf16[8,17280]{1,0:T(8,128)(2,1)S(1)}, bf16[8,17280]{1,0:T(8,128)(2,1)S(1)}, u32[]{:S(2)}, u32[]{:S(2)}) %collective-permute-start.3) | collective-permute-done | bytes 276512 | tf_op jit(solution)/shard_map/ppermute | solution.py:164
  63.4 1.5 broadcast_in_dim.148
  64.9 4.5 %all-to-all-start = ((bf16[4,16,17280]{2,1,0:T(8,128)(2,1)}), bf16[4,16,17280]{2,1,0:T(8,128)(2,1)S(1)}, u32[]{:S(2)}, u32[]{:S(2)}) async-start(bf16[4,16,17280]{2,1,0:T(8,128)(2,1)} %broadcast_in_dim.148), calls=%async_computation | async-start | bytes 4423680 | tf_op jit(solution)/shard_map/all_to_all | solution.py:176
  70.5 1.4 add_compare_fusion
  72.0 1.6 lt.86
  74.1 1.2 fusion.91
  75.3 0.7 multiply_sine_fusion
  76.0 16.8 %all-to-all-done = bf16[4,16,17280]{2,1,0:T(8,128)(2,1)S(1)} async-done(((bf16[4,16,17280]{2,1,0:T(8,128)(2,1)}), bf16[4,16,17280]{2,1,0:T(8,128)(2,1)S(1)}, u32[]{:S(2)}, u32[]{:S(2)}) %all-to-all-start) | async-done | bytes 2211872 | tf_op jit(solution)/shard_map/all_to_all | solution.py:176
  92.9 1.1 slice.73
  93.9 1.1 slice.69
  95.0 1.6 reshape_reshape.4
  96.6 1.8 reshape.589
  98.5 1.6 fusion.139
  100.1 12.1 %all-gather = bf16[1024,64]{0,1:T(8,128)(2,1)S(1)} all-gather(bf16[128,64]{0,1:T(8,128)(2,1)S(1)} %fusion.75), channel_id=2, replica_groups=mesh['dp'=8,'tx'=4,'tz'=16] {'dp'}, dimensions={0}, use_global_device_ids=true | all-gather | bytes 147456 | tf_op jit(solution)/shard_map/all_gather | solution.py:263
  113.5 1.0 fusion.2
  114.6 1.7 fusion.10
  116.2 4.8 %fusion.34 = f32[128,4544]{0,1:T(8,128)} fusion(bf16[142,4544]{1,0:T(8,128)(2,1)S(1)} %copy-done, bf16[128,4544]{1,0:T(8,128)(2,1)S(1)} %reshape.589, bf16[4544,142]{0,1:T(8,128)(2,1)} %param.17), kind=kOutput, calls=%fused_computation.71 | convolution fusion | flops 331548416 | bytes 6070784 | tf_op jit(solution)/shard_map/dot_general | solution.py:268
  121.1 10.3 %all-gather.3.cloned.1.call-done = bf16[8,128,8,128]{3,2,1,0:T(8,128)(2,1)} async-done(((bf16[8,8,8,128]{3,2,1,0:T(8,128)(2,1)}), bf16[8,128,8,128]{3,2,1,0:T(8,128)(2,1)}) %all-gather.3.cloned.1.call-update) | async-done | bytes 2097168 | tf_op jit(solution)/shard_map/all_gather | solution.py:230
  131.4 1.1 slice.72
  132.4 4.2 %collective-permute-start.4 = (bf16[8,32,8,128]{3,2,1,0:T(8,128)(2,1)S(1)}, bf16[8,32,8,128]{3,2,1,0:T(8,128)(2,1)}, u32[]{:S(2)}, u32[]{:S(2)}) collective-permute-start(bf16[8,32,8,128]{3,2,1,0:T(8,128)(2,1)S(1)} %slice.72), channel_id=1, source_target_pairs={{0,16},{1,17},{2,18},{3,19},{4,20},{5,21},{6,22},{7,23},{8,24},{9,... | collective-permute-start | bytes 1572872 | tf_op jit(solution)/shard_map/ppermute | solution.py:135
  138.1 4.4 %collective-permute-done.4 = bf16[8,32,8,128]{3,2,1,0:T(8,128)(2,1)} collective-permute-done((bf16[8,32,8,128]{3,2,1,0:T(8,128)(2,1)S(1)}, bf16[8,32,8,128]{3,2,1,0:T(8,128)(2,1)}, u32[]{:S(2)}, u32[]{:S(2)}) %collective-permute-start.4) | collective-permute-done | bytes 524320 | tf_op jit(solution)/shard_map/ppermute | solution.py:135
  142.6 1.3 collective-permute-start.5
  143.9 1.2 iota_compare_fusion
  145.1 1.8 fusion.140
  147.0 3.6 %collective-permute-done.5 = bf16[8,32,8,128]{3,2,1,0:T(8,128)(2,1)S(1)} collective-permute-done((bf16[8,32,8,128]{3,2,1,0:T(8,128)(2,1)S(1)}, bf16[8,32,8,128]{3,2,1,0:T(8,128)(2,1)S(1)}, u32[]{:S(2)}, u32[]{:S(2)}) %collective-permute-start.5) | collective-permute-done | bytes 524320 | tf_op jit(solution)/shard_map/ppermute | solution.py:135
  151.8 0.8 fusion.5
  153.3 4.2 %all-to-all-start.1 = ((f32[8,128,66]{1,2,0:T(8,128)}), f32[8,128,66]{1,2,0:T(8,128)S(1)}, u32[]{:S(2)}, u32[]{:S(2)}) async-start(f32[8,128,66]{1,2,0:T(8,128)} %pad_maximum_fusion.1), calls=%async_computation.1 | async-start | bytes 589824 | tf_op jit(solution)/shard_map/all_to_all | solution.py:290
  157.8 7.5 %all-to-all-done.1 = f32[8,128,66]{1,2,0:T(8,128)S(1)} async-done(((f32[8,128,66]{1,2,0:T(8,128)}), f32[8,128,66]{1,2,0:T(8,128)S(1)}, u32[]{:S(2)}, u32[]{:S(2)}) %all-to-all-start.1) | async-done | bytes 270368 | tf_op jit(solution)/shard_map/all_to_all | solution.py:290
  165.4 3.3 %fusion = bf16[128,4544]{0,1:T(8,128)(2,1)} fusion(f32[128,4544]{0,1:T(8,128)} %fusion.34, bf16[64,4544]{1,0:T(8,128)(2,1)S(1)} %copy-done.3, f32[128,128]{0,1:T(8,128)S(1)} %get-tuple-element.47, f32[128]{0:T(128)S(1)} %get-tuple-element.46, f32[128,64]{0,1:T(8,128)S(1)} %fusion.21, f32[128,128]{0,1:T(8,128)S(1)} %copy-done.6, ...), kind=kOutput, calls=%fused_computation.2 | convolution fusion | flops 77783040 | bytes 4196352 | tf_op jit(solution)/shard_map/dot_general | solution.py:304
  168.7 1.6 copy.52
  170.3 1.3 convert_element_type.81
  171.6 7.5 %all-to-all-start.2 = ((bf16[4,16,2,4544]{3,2,1,0:T(2,128)(2,1)}), bf16[4,16,2,4544]{3,2,1,0:T(2,128)(2,1)S(1)}, u32[]{:S(2)}, u32[]{:S(2)}) async-start(bf16[4,16,2,4544]{3,2,1,0:T(2,128)(2,1)} %convert_element_type.81), calls=%async_computation.2 | async-start | bytes 2359296 | tf_op jit(solution)/shard_map/all_to_all | solution.py:188
  179.2 16.1 %all-to-all-done.2 = bf16[4,16,2,4544]{3,2,1,0:T(2,128)(2,1)S(1)} async-done(((bf16[4,16,2,4544]{3,2,1,0:T(2,128)(2,1)}), bf16[4,16,2,4544]{3,2,1,0:T(2,128)(2,1)S(1)}, u32[]{:S(2)}, u32[]{:S(2)}) %all-to-all-start.2) | async-done | bytes 1163296 | tf_op jit(solution)/shard_map/all_to_all | solution.py:188
  195.3 1.2 convert_reduce_fusion
  196.4 1.1 gather_fusion
  197.6 27.4 %all_to_all.20 = bf16[16,2,4544]{2,1,0:T(2,128)(2,1)S(1)} all-to-all(bf16[16,2,4544]{2,1,0:T(2,128)(2,1)S(1)} %gather_fusion), channel_id=1, replica_groups=mesh['dp'=8,'tx'=4,'tz'=16] {'tz'}, dimensions={0} | all-to-all | bytes 581632 | tf_op jit(solution)/shard_map/all_to_all | solution.py:191
  (110 shorter events, 10.9 us)
Async XLA Ops:
  6.5 109.7 %copy-start = (bf16[142,4544]{1,0:T(8,128)(2,1)S(1)}, bf16[142,4544]{1,0:T(8,128)(2,1)}, u32[]{:S(2)}) copy-start(bf16[142,4544]{1,0:T(8,128)(2,1)} %param.18) | copy-start | bytes 3871492
  6.5 124.8 %all-gather.3.cloned.1.call-start = ((), (), s32[]{:S(2)}) async-start(), calls=%async_computation.4 | async-start | bytes 2228224 | tf_op jit(solution)/shard_map/all_gather | solution.py:230
  15.4 17.1 %collective-permute-start = (bf16[1,17280]{1,0:T(2,128)(2,1)S(1)}, bf16[1,17280]{1,0:T(2,128)(2,1)S(1)}, u32[]{:S(2)}, u32[]{:S(2)}) collective-permute-start(bf16[1,17280]{1,0:T(2,128)(2,1)S(1)} %broadcast_in_dim.147), channel_id=1, source_target_pairs={{0,8},{1,9},{2,10},{3,11},{4,12},{5,13},{6,14},{7,15},{8,0},{9,1},... | collective-permute-start | bytes 103688 | tf_op jit(solution)/shard_map/ppermute | solution.py:164
  32.8 13.2 %collective-permute-start.1 = (bf16[2,17280]{1,0:T(2,128)(2,1)S(1)}, bf16[2,17280]{1,0:T(2,128)(2,1)S(1)}, u32[]{:S(2)}, u32[]{:S(2)}) collective-permute-start(bf16[2,17280]{1,0:T(2,128)(2,1)S(1)} %pad_maximum_fusion.4), channel_id=1, source_target_pairs={{0,4},{1,5},{2,6},{3,7},{4,0},{5,1},{6,2},{7,3},{8,12},{9,13},{10,... | collective-permute-start | bytes 207368 | tf_op jit(solution)/shard_map/ppermute | solution.py:164
  46.4 7.9 %collective-permute-start.2 = (bf16[4,17280]{1,0:T(4,128)(2,1)S(1)}, bf16[4,17280]{1,0:T(4,128)(2,1)S(1)}, u32[]{:S(2)}, u32[]{:S(2)}) collective-permute-start(bf16[4,17280]{1,0:T(4,128)(2,1)S(1)} %pad_maximum_fusion.3), channel_id=1, source_target_pairs={{0,2},{1,3},{2,0},{3,1},{4,6},{5,7},{6,4},{7,5},{8,10},{9,11},{10,... | collective-permute-start | bytes 414728 | tf_op jit(solution)/shard_map/ppermute | solution.py:164
  54.7 8.4 %collective-permute-start.3 = (bf16[8,17280]{1,0:T(8,128)(2,1)S(1)}, bf16[8,17280]{1,0:T(8,128)(2,1)S(1)}, u32[]{:S(2)}, u32[]{:S(2)}) collective-permute-start(bf16[8,17280]{1,0:T(8,128)(2,1)S(1)} %pad_maximum_fusion.2), channel_id=1, source_target_pairs={{0,1},{1,0},{2,3},{3,2},{4,5},{5,4},{6,7},{7,6},{8,9},{9,8},{10,11... | collective-permute-start | bytes 829448 | tf_op jit(solution)/shard_map/ppermute | solution.py:164
  64.9 4.5 %copy-start.18 = (s32[8]{0:T(128)S(1)}, s32[8]{0:T(128)}, u32[]{:S(2)}) copy-start(s32[8]{0:T(128)} %param.20) | copy-start | bytes 100
  64.9 28.0 %all-to-all-start = ((bf16[4,16,17280]{2,1,0:T(8,128)(2,1)}), bf16[4,16,17280]{2,1,0:T(8,128)(2,1)S(1)}, u32[]{:S(2)}, u32[]{:S(2)}) async-start(bf16[4,16,17280]{2,1,0:T(8,128)(2,1)} %broadcast_in_dim.148), calls=%async_computation | async-start | bytes 4423680 | tf_op jit(solution)/shard_map/all_to_all | solution.py:176
  70.0 0.5 copy-start.21
  98.5 1.6 copy-start.10
  98.5 1.6 copy-start.12
  98.5 14.5 %copy-start.14 = (pred[4096]{0:T(1024)(128)(4,1)S(1)}, pred[4096]{0:T(1024)(128)(4,1)}, u32[]{:S(2)}) copy-start(pred[4096]{0:T(1024)(128)(4,1)} %lt.86) | copy-start | bytes 12292
  100.1 12.2 %copy-start.8 = (bf16[128,64]{0,1:T(8,128)(2,1)}, bf16[128,64]{0,1:T(8,128)(2,1)S(1)}, u32[]{:S(2)}) copy-start(bf16[128,64]{0,1:T(8,128)(2,1)S(1)} %fusion.75) | copy-start | bytes 49156
  112.3 0.7 copy-start.1
  113.5 1.0 copy-start.15
  116.2 20.4 %copy-start.22 = (s32[8]{0:T(128)S(1)}, s32[8]{0:T(128)}, u32[]{:S(2)}) copy-start(s32[8]{0:T(128)} %copy-done.21) | copy-start | bytes 100
  116.2 20.4 %copy-start.25 = (s32[32]{0:T(128)S(1)}, s32[32]{0:T(128)}, u32[]{:S(2)}) copy-start(s32[32]{0:T(128)} %iota_multiply_fusion) | copy-start | bytes 388
  116.2 21.2 %copy-start.19 = (s32[8]{0:T(128)S(1)}, s32[8]{0:T(128)}, u32[]{:S(2)}) copy-start(s32[8]{0:T(128)} %param.20) | copy-start | bytes 100
  132.4 10.1 %collective-permute-start.4 = (bf16[8,32,8,128]{3,2,1,0:T(8,128)(2,1)S(1)}, bf16[8,32,8,128]{3,2,1,0:T(8,128)(2,1)}, u32[]{:S(2)}, u32[]{:S(2)}) collective-permute-start(bf16[8,32,8,128]{3,2,1,0:T(8,128)(2,1)S(1)} %slice.72), channel_id=1, source_target_pairs={{0,16},{1,17},{2,18},{3,19},{4,20},{5,21},{6,22},{7,23},{8,24},{9,... | collective-permute-start | bytes 1572872 | tf_op jit(solution)/shard_map/ppermute | solution.py:135
  142.6 8.0 %collective-permute-start.5 = (bf16[8,32,8,128]{3,2,1,0:T(8,128)(2,1)S(1)}, bf16[8,32,8,128]{3,2,1,0:T(8,128)(2,1)S(1)}, u32[]{:S(2)}, u32[]{:S(2)}) collective-permute-start(bf16[8,32,8,128]{3,2,1,0:T(8,128)(2,1)S(1)} %broadcast_select_fusion), channel_id=1, source_target_pairs={{0,48},{16,32},{1,49},{17,33},{2,50},{18,34},{3,51},{19,35},{4,52}... | collective-permute-start | bytes 1572872 | tf_op jit(solution)/shard_map/ppermute | solution.py:135
  146.9 4.2 %copy-start.5 = (f32[128,128]{0,1:T(8,128)}, f32[128,128]{0,1:T(8,128)S(1)}, u32[]{:S(2)}) copy-start(f32[128,128]{0,1:T(8,128)S(1)} %fusion.140) | copy-start | bytes 196612
  146.9 3.7 %copy-start.2 = (bf16[1024,64]{0,1:T(8,128)(2,1)S(1)}, bf16[1024,64]{0,1:T(8,128)(2,1)}, u32[]{:S(2)}) copy-start(bf16[1024,64]{0,1:T(8,128)(2,1)} %copy-done.1) | copy-start | bytes 393220
  146.9 3.7 %copy-start.17 = (pred[8,256]{1,0:T(8,128)(4,1)S(1)}, pred[8,256]{1,0:T(8,128)(4,1)}, u32[]{:S(2)}) copy-start(pred[8,256]{1,0:T(8,128)(4,1)} %compare_and_fusion) | copy-start | bytes 6148
  150.7 0.9 copy-start.16
  150.7 0.9 copy-start.20
  150.7 0.9 copy-start.23
  150.7 1.0 copy-start.7
  151.7 5.7 %copy-start.6 = (f32[128,128]{0,1:T(8,128)S(1)}, f32[128,128]{0,1:T(8,128)}, u32[]{:S(2)}) copy-start(f32[128,128]{0,1:T(8,128)} %copy-done.5) | copy-start | bytes 196612
  151.7 5.7 %copy-start.9 = (bf16[128,64]{0,1:T(8,128)(2,1)S(1)}, bf16[128,64]{0,1:T(8,128)(2,1)}, u32[]{:S(2)}) copy-start(bf16[128,64]{0,1:T(8,128)(2,1)} %copy-done.8) | copy-start | bytes 49156
  151.8 5.7 %copy-start.11 = (f32[128,32]{0,1:T(8,128)S(1)}, f32[128,32]{0,1:T(8,128)}, u32[]{:S(2)}) copy-start(f32[128,32]{0,1:T(8,128)} %get-tuple-element.38) | copy-start | bytes 49156
  151.8 5.7 %copy-start.13 = (f32[128,32]{0,1:T(8,128)S(1)}, f32[128,32]{0,1:T(8,128)}, u32[]{:S(2)}) copy-start(f32[128,32]{0,1:T(8,128)} %get-tuple-element.39) | copy-start | bytes 49156
  151.8 5.7 %copy-start.26 = (s32[128]{0:T(128)S(1)}, s32[128]{0:T(128)}, u32[]{:S(2)}) copy-start(s32[128]{0:T(128)} %get-tuple-element.48) | copy-start | bytes 1540
  152.5 12.9 %copy-start.3 = (bf16[64,4544]{1,0:T(8,128)(2,1)S(1)}, bf16[64,4544]{1,0:T(8,128)(2,1)}, u32[]{:S(2)}) copy-start(bf16[64,4544]{1,0:T(8,128)(2,1)} %param.16) | copy-start | bytes 1744900
  153.3 12.0 %all-to-all-start.1 = ((f32[8,128,66]{1,2,0:T(8,128)}), f32[8,128,66]{1,2,0:T(8,128)S(1)}, u32[]{:S(2)}, u32[]{:S(2)}) async-start(f32[8,128,66]{1,2,0:T(8,128)} %pad_maximum_fusion.1), calls=%async_computation.1 | async-start | bytes 589824 | tf_op jit(solution)/shard_map/all_to_all | solution.py:290
  171.6 7.6 %copy-start.24 = (s32[16]{0:T(128)S(1)}, s32[16]{0:T(128)}, u32[]{:S(2)}) copy-start(s32[16]{0:T(128)} %constant.238) | copy-start | bytes 196
  171.6 23.6 %all-to-all-start.2 = ((bf16[4,16,2,4544]{3,2,1,0:T(2,128)(2,1)}), bf16[4,16,2,4544]{3,2,1,0:T(2,128)(2,1)S(1)}, u32[]{:S(2)}, u32[]{:S(2)}) async-start(bf16[4,16,2,4544]{3,2,1,0:T(2,128)(2,1)} %convert_element_type.81), calls=%async_computation.2 | async-start | bytes 2359296 | tf_op jit(solution)/shard_map/all_to_all | solution.py:188
  179.2 45.9 %copy-start.4 = (bf16[1,2,4544]{2,1,0:T(2,128)(2,1)S(1)}, bf16[1,2,4544]{2,1,0:T(2,128)(2,1)}, u32[]{:S(2)}) copy-start(bf16[1,2,4544]{2,1,0:T(2,128)(2,1)} %param.11) | copy-start | bytes 54532
Sparse Core Ops, SparseCore 0:
  58.4 72.9 all-gather.2

commit v6 on v5

--- a/solution.py
+++ b/solution.py
@@ -156,16 +156,38 @@
 SHORT_MAX = 2048
 
 
+def z_groups(size):
+    groups, b = [], size.bit_length() - 1
+    while b > 0:
+        lo = max(b - 2, 0)
+        groups.append((lo, b - lo))
+        b = lo
+    return groups
+
+
+def z_source(slot, size):
+    out, offset = 0, 0
+    for lo, width in z_groups(size):
+        out |= ((slot >> offset) & ((1 << width) - 1)) << lo
+        offset += width
+    return out
+
+
 def z_rounds(piece):
     size = lax.axis_size("tz")
     me = lax.axis_index("tz")
     buf = piece[None]
-    for b in reversed(range(size.bit_length() - 1)):
-        other = lax.ppermute(buf, "tz", [(i, i ^ (1 << b)) for i in range(size)])
-        low = ((me >> b) & 1) == 0
-        buf = jnp.concatenate(
-            [jnp.where(low, buf, other), jnp.where(low, other, buf)], axis=0
-        )
+    for lo, width in z_groups(size):
+        radix = 1 << width
+        mine = (me >> lo) & (radix - 1)
+        got = [buf] + [
+            lax.ppermute(buf, "tz", [(i, i ^ (k << lo)) for i in range(size)])
+            for k in range(1, radix)
+        ]
+        stacked = jnp.stack(got)
+        buf = jnp.stack(
+            [lax.dynamic_index_in_dim(stacked, v ^ mine, 0, keepdims=False) for v in range(radix)]
+        ).reshape((-1,) + piece.shape)
     return buf
 
 
@@ -178,7 +200,8 @@
 
 def slot_source(index):
     nz = lax.axis_size("tz")
-    return (index // nz) * nz + bit_reversed(index % nz, nz.bit_length() - 1)
+    table = jnp.array([z_source(s, nz) for s in range(nz)], dtype=jnp.int32)
+    return (index // nz) * nz + table[index % nz]
 
 
 def scatter_tensor(partial):
@@ -186,7 +209,7 @@
     bits = nz.bit_length() - 1
     buf = partial.reshape((nx, nz) + partial.shape[1:]).astype(jnp.bfloat16)
     over_x = lax.all_to_all(buf, "tx", 0, 0, tiled=True).astype(jnp.float32).sum(0)
-    order = [int(format(c, f"0{bits}b")[::-1], 2) if bits else 0 for c in range(nz)]
+    order = [next(s for s in range(nz) if z_source(s, nz) == c) for c in range(nz)]
     ready = jnp.take(over_x, jnp.array(order, dtype=jnp.int32), axis=0).astype(jnp.bfloat16)
     return lax.all_to_all(ready, "tz", 0, 0, tiled=True).astype(jnp.float32).sum(0)
 

time: 234 us -> 240 us (1.026)
  waiting for transfers between devices: 73.5 us -> 79.3 us
    all_gather x1, waiting for transfers between devices: 10.3 us -> 0.01 us  [local(): lax.all_gather(kv_cache, 'tz', axis=1, tiled=True)[:, :short_blocks]]
    ppermute x2, waiting for transfers between devices: 8.04 us -> 17.7 us  [spread_from_first(): got = lax.ppermute(x, name, pairs)]
    ppermute x4 -> x6, waiting for transfers between devices: 14.7 us -> 18.7 us  [z_rounds(): lax.ppermute(buf, 'tz', [(i, i ^ k << lo) for i in range(size)])]
    all_to_all x1, waiting for transfers between devices: 16.8 us -> 19.4 us  [gather_tensor(): lax.all_to_all(wide, 'tx', 0, 0, tiled=True).reshape((-1,) + piece.shape)]
    ppermute x4 -> x6, starting transfers between devices: 31.9 us -> 31.5 us  [z_rounds(): lax.ppermute(buf, 'tz', [(i, i ^ k << lo) for i in range(size)])]
  transfers between devices with their start and end apart: 10 -> 12, of which waited for: 10 -> 9; matrix products, arithmetic and copies ran while one was open for 12% -> 12% of each run, Pallas kernels for 0% -> 0%
where the time goes in v6:
time: 240 us; the launch traced here: 239 us
  waiting for transfers between devices  79.3 us (33%)
  starting transfers between devices  52.3 us (22%)
  blocking collectives  41.2 us (17%)
  local copies, waits for them, and re-layouts  20.4 us (8%)
  other arithmetic  16.3 us (7%)
  between operations  16 us (7%)
  matrix products  13.5 us (6%)
    ppermute x6, starting transfers between devices, z_rounds(): lax.ppermute(buf, 'tz', [(i, i ^ k << lo) for i in range(size)])  31.5 us
    all_to_all x1, blocking collectives, scatter_tensor(): lax.all_to_all(ready, 'tz', 0, 0, tiled=True).astype(jnp.float32).sum(0)  29.1 us
    all_to_all x1, waiting for transfers between devices, gather_tensor(): lax.all_to_all(wide, 'tx', 0, 0, tiled=True).reshape((-1,) + piece.shape)  19.4 us
    ppermute x6, waiting for transfers between devices, z_rounds(): lax.ppermute(buf, 'tz', [(i, i ^ k << lo) for i in range(size)])  18.7 us
    ppermute x2, waiting for transfers between devices, spread_from_first(): got = lax.ppermute(x, name, pairs)  17.7 us
    all_to_all x1, waiting for transfers between devices, scatter_tensor(): lax.all_to_all(buf, 'tx', 0, 0, tiled=True).astype(jnp.float32).sum(0)  16.1 us
    all_gather x1, blocking collectives, local(): q_all = lax.all_gather(query_rows, 'dp', axis=0, tiled=False)  12.1 us
    all_to_all x1, starting transfers between devices, scatter_tensor(): lax.all_to_all(buf, 'tx', 0, 0, tiled=True).astype(jnp.float32).sum(0)  7.52 us
  transfers between devices with their start and end apart: 12, of which 9 were waited for; matrix products, arithmetic and copies ran while one was open for 12% of the time, Pallas kernels for 0%

profile of v6, /device:TPU:64, one launch (start us, length us, event | category | flops | bytes accessed | tf_op | source)
XLA Modules:
  0.0 239.1 jit_solution(6501775348407289438)
XLA Ops:
  6.5 1.0 convert_reduce_fusion.2
  7.5 0.8 reshape.626
  8.3 1.4 iota_reduce_fusion
  11.1 0.7 add.316
  12.8 0.9 fusion.38
  15.6 10.9 %collective-permute-start.2 = (bf16[1,17280]{1,0:T(2,128)(2,1)S(1)}, bf16[1,17280]{1,0:T(2,128)(2,1)S(1)}, u32[]{:S(2)}, u32[]{:S(2)}) collective-permute-start(bf16[1,17280]{1,0:T(2,128)(2,1)S(1)} %broadcast_in_dim.150), channel_id=1, source_target_pairs={{0,12},{1,13},{2,14},{3,15},{4,8},{5,9},{6,10},{7,11},{8,4},{9,5},... | collective-permute-start | bytes 103688 | tf_op jit(solution)/shard_map/ppermute | solution.py:184
  26.5 5.4 %collective-permute-start.1 = (bf16[1,17280]{1,0:T(2,128)(2,1)S(1)}, bf16[1,17280]{1,0:T(2,128)(2,1)S(1)}, u32[]{:S(2)}, u32[]{:S(2)}) collective-permute-start(bf16[1,17280]{1,0:T(2,128)(2,1)S(1)} %broadcast_in_dim.150), channel_id=1, source_target_pairs={{0,8},{1,9},{2,10},{3,11},{4,12},{5,13},{6,14},{7,15},{8,0},{9,1},... | collective-permute-start | bytes 103688 | tf_op jit(solution)/shard_map/ppermute | solution.py:184
  32.0 3.8 %collective-permute-start = (bf16[1,17280]{1,0:T(2,128)(2,1)S(1)}, bf16[1,17280]{1,0:T(2,128)(2,1)S(1)}, u32[]{:S(2)}, u32[]{:S(2)}) collective-permute-start(bf16[1,17280]{1,0:T(2,128)(2,1)S(1)} %broadcast_in_dim.150), channel_id=1, source_target_pairs={{0,4},{1,5},{2,6},{3,7},{4,0},{5,1},{6,2},{7,3},{8,12},{9,13},{10,... | collective-permute-start | bytes 103688 | tf_op jit(solution)/shard_map/ppermute | solution.py:184
  35.9 8.4 %collective-permute-done.1 = bf16[1,17280]{1,0:T(2,128)(2,1)S(1)} collective-permute-done((bf16[1,17280]{1,0:T(2,128)(2,1)S(1)}, bf16[1,17280]{1,0:T(2,128)(2,1)S(1)}, u32[]{:S(2)}, u32[]{:S(2)}) %collective-permute-start.1) | collective-permute-done | bytes 34592 | tf_op jit(solution)/shard_map/ppermute | solution.py:184
  44.3 1.2 collective-permute-done
  46.5 4.2 %collective-permute-start.5 = (bf16[4,17280]{1,0:T(4,128)(2,1)S(1)}, bf16[4,17280]{1,0:T(4,128)(2,1)S(1)}, u32[]{:S(2)}, u32[]{:S(2)}) collective-permute-start(bf16[4,17280]{1,0:T(4,128)(2,1)S(1)} %fusion.156), channel_id=1, source_target_pairs={{0,3},{1,2},{2,1},{3,0},{4,7},{5,6},{6,5},{7,4},{8,11},{9,10},{10,... | collective-permute-start | bytes 414728 | tf_op jit(solution)/shard_map/ppermute | solution.py:184
  50.7 3.9 %collective-permute-start.4 = (bf16[4,17280]{1,0:T(4,128)(2,1)S(1)}, bf16[4,17280]{1,0:T(4,128)(2,1)S(1)}, u32[]{:S(2)}, u32[]{:S(2)}) collective-permute-start(bf16[4,17280]{1,0:T(4,128)(2,1)S(1)} %fusion.156), channel_id=1, source_target_pairs={{0,2},{1,3},{2,0},{3,1},{4,6},{5,7},{6,4},{7,5},{8,10},{9,11},{10,... | collective-permute-start | bytes 414728 | tf_op jit(solution)/shard_map/ppermute | solution.py:184
  54.6 3.4 %collective-permute-start.3 = (bf16[4,17280]{1,0:T(4,128)(2,1)S(1)}, bf16[4,17280]{1,0:T(4,128)(2,1)S(1)}, u32[]{:S(2)}, u32[]{:S(2)}) collective-permute-start(bf16[4,17280]{1,0:T(4,128)(2,1)S(1)} %fusion.156), channel_id=1, source_target_pairs={{0,1},{1,0},{2,3},{3,2},{4,5},{5,4},{6,7},{7,6},{8,9},{9,8},{10,11... | collective-permute-start | bytes 414728 | tf_op jit(solution)/shard_map/ppermute | solution.py:184
  58.3 4.6 %collective-permute-done.5 = bf16[4,17280]{1,0:T(4,128)(2,1)S(1)} collective-permute-done((bf16[4,17280]{1,0:T(4,128)(2,1)S(1)}, bf16[4,17280]{1,0:T(4,128)(2,1)S(1)}, u32[]{:S(2)}, u32[]{:S(2)}) %collective-permute-start.5) | collective-permute-done | bytes 138272 | tf_op jit(solution)/shard_map/ppermute | solution.py:184
  62.9 4.4 %collective-permute-done.4 = bf16[4,17280]{1,0:T(4,128)(2,1)S(1)} collective-permute-done((bf16[4,17280]{1,0:T(4,128)(2,1)S(1)}, bf16[4,17280]{1,0:T(4,128)(2,1)S(1)}, u32[]{:S(2)}, u32[]{:S(2)}) %collective-permute-start.4) | collective-permute-done | bytes 138272 | tf_op jit(solution)/shard_map/ppermute | solution.py:184
  68.6 1.5 broadcast_in_dim.152
  70.1 4.5 %all-to-all-start = ((bf16[4,16,17280]{2,1,0:T(8,128)(2,1)}), bf16[4,16,17280]{2,1,0:T(8,128)(2,1)S(1)}, u32[]{:S(2)}, u32[]{:S(2)}) async-start(bf16[4,16,17280]{2,1,0:T(8,128)(2,1)} %broadcast_in_dim.152), calls=%async_computation | async-start | bytes 4423680 | tf_op jit(solution)/shard_map/all_to_all | solution.py:198
  74.7 1.3 gather_fusion
  77.2 1.3 add_compare_fusion
  78.6 1.0 lt.140
  80.1 1.2 fusion.92
  81.3 0.7 multiply_sine_fusion
  82.0 19.4 %all-to-all-done = bf16[4,16,17280]{2,1,0:T(8,128)(2,1)S(1)} async-done(((bf16[4,16,17280]{2,1,0:T(8,128)(2,1)}), bf16[4,16,17280]{2,1,0:T(8,128)(2,1)S(1)}, u32[]{:S(2)}, u32[]{:S(2)}) %all-to-all-start) | async-done | bytes 2211872 | tf_op jit(solution)/shard_map/all_to_all | solution.py:198
  101.4 1.0 slice.92
  102.5 1.1 slice.88
  103.6 2.3 reshape_reshape.4
  105.9 1.9 reshape.623
  108.6 12.1 %all-gather = bf16[1024,64]{0,1:T(8,128)(2,1)S(1)} all-gather(bf16[128,64]{0,1:T(8,128)(2,1)S(1)} %fusion.75), channel_id=2, replica_groups=mesh['dp'=8,'tx'=4,'tz'=16] {'dp'}, dimensions={0}, use_global_device_ids=true | all-gather | bytes 147456 | tf_op jit(solution)/shard_map/all_gather | solution.py:286
  121.8 1.1 fusion.10
  122.8 4.8 %fusion.34 = f32[128,4544]{0,1:T(8,128)} fusion(bf16[142,4544]{1,0:T(8,128)(2,1)S(1)} %copy-done, bf16[128,4544]{1,0:T(8,128)(2,1)S(1)} %reshape.623, bf16[4544,142]{0,1:T(8,128)(2,1)} %param.19), kind=kOutput, calls=%fused_computation.64 | convolution fusion | flops 331548416 | bytes 6070784 | tf_op jit(solution)/shard_map/dot_general | solution.py:291
  127.7 1.1 slice.91
  128.8 3.3 %collective-permute-start.6 = (bf16[8,32,8,128]{3,2,1,0:T(8,128)(2,1)S(1)}, bf16[8,32,8,128]{3,2,1,0:T(8,128)(2,1)}, u32[]{:S(2)}, u32[]{:S(2)}) collective-permute-start(bf16[8,32,8,128]{3,2,1,0:T(8,128)(2,1)S(1)} %slice.91), channel_id=1, source_target_pairs={{0,16},{1,17},{2,18},{3,19},{4,20},{5,21},{6,22},{7,23},{8,24},{9,... | collective-permute-start | bytes 1572872 | tf_op jit(solution)/shard_map/ppermute | solution.py:135
  133.0 9.9 %collective-permute-done.6 = bf16[8,32,8,128]{3,2,1,0:T(8,128)(2,1)} collective-permute-done((bf16[8,32,8,128]{3,2,1,0:T(8,128)(2,1)S(1)}, bf16[8,32,8,128]{3,2,1,0:T(8,128)(2,1)}, u32[]{:S(2)}, u32[]{:S(2)}) %collective-permute-start.6) | collective-permute-done | bytes 524320 | tf_op jit(solution)/shard_map/ppermute | solution.py:135
  142.9 1.1 broadcast_select_fusion
  144.0 2.1 collective-permute-start.7
  146.8 1.8 fusion.145
  148.7 7.7 %collective-permute-done.7 = bf16[8,32,8,128]{3,2,1,0:T(8,128)(2,1)} collective-permute-done((bf16[8,32,8,128]{3,2,1,0:T(8,128)(2,1)S(1)}, bf16[8,32,8,128]{3,2,1,0:T(8,128)(2,1)}, u32[]{:S(2)}, u32[]{:S(2)}) %collective-permute-start.7) | collective-permute-done | bytes 524320 | tf_op jit(solution)/shard_map/ppermute | solution.py:135
  157.5 0.8 fusion.5
  159.0 3.4 %all-to-all-start.1 = ((f32[8,128,66]{1,2,0:T(8,128)}), f32[8,128,66]{1,2,0:T(8,128)S(1)}, u32[]{:S(2)}, u32[]{:S(2)}) async-start(f32[8,128,66]{1,2,0:T(8,128)} %pad_maximum_fusion.2), calls=%async_computation.1 | async-start | bytes 589824 | tf_op jit(solution)/shard_map/all_to_all | solution.py:313
  162.7 7.5 %all-to-all-done.1 = f32[8,128,66]{1,2,0:T(8,128)S(1)} async-done(((f32[8,128,66]{1,2,0:T(8,128)}), f32[8,128,66]{1,2,0:T(8,128)S(1)}, u32[]{:S(2)}, u32[]{:S(2)}) %all-to-all-start.1) | async-done | bytes 270368 | tf_op jit(solution)/shard_map/all_to_all | solution.py:313
  170.3 3.3 %fusion = bf16[128,4544]{0,1:T(8,128)(2,1)} fusion(f32[128,4544]{0,1:T(8,128)} %fusion.34, bf16[64,4544]{1,0:T(8,128)(2,1)S(1)} %copy-done.5, f32[128,128]{0,1:T(8,128)S(1)} %get-tuple-element.47, f32[128]{0:T(128)S(1)} %get-tuple-element.46, f32[128,64]{0,1:T(8,128)S(1)} %fusion.21, f32[128,128]{0,1:T(8,128)S(1)} %fusion.145, ...), kind=kOutput, calls=%fused_computation.3 | convolution fusion | flops 77783040 | bytes 4196352 | tf_op jit(solution)/shard_map/dot_general | solution.py:327
  173.6 1.6 copy.54
  175.2 1.3 convert_element_type.81
  176.5 7.5 %all-to-all-start.2 = ((bf16[4,16,2,4544]{3,2,1,0:T(2,128)(2,1)}), bf16[4,16,2,4544]{3,2,1,0:T(2,128)(2,1)S(1)}, u32[]{:S(2)}, u32[]{:S(2)}) async-start(bf16[4,16,2,4544]{3,2,1,0:T(2,128)(2,1)} %convert_element_type.81), calls=%async_computation.2 | async-start | bytes 2359296 | tf_op jit(solution)/shard_map/all_to_all | solution.py:211
  184.0 16.1 %all-to-all-done.2 = bf16[4,16,2,4544]{3,2,1,0:T(2,128)(2,1)S(1)} async-done(((bf16[4,16,2,4544]{3,2,1,0:T(2,128)(2,1)}), bf16[4,16,2,4544]{3,2,1,0:T(2,128)(2,1)S(1)}, u32[]{:S(2)}, u32[]{:S(2)}) %all-to-all-start.2) | async-done | bytes 1163296 | tf_op jit(solution)/shard_map/all_to_all | solution.py:211
  200.1 1.2 convert_reduce_fusion
  201.3 1.1 gather_fusion.1
  202.4 29.1 %all_to_all.20 = bf16[16,2,4544]{2,1,0:T(2,128)(2,1)S(1)} all-to-all(bf16[16,2,4544]{2,1,0:T(2,128)(2,1)S(1)} %gather_fusion.1), channel_id=1, replica_groups=mesh['dp'=8,'tx'=4,'tz'=16] {'tz'}, dimensions={0} | all-to-all | bytes 581632 | tf_op jit(solution)/shard_map/all_to_all | solution.py:214
  (88 shorter events, 12.9 us)
Async XLA Ops:
  6.5 116.3 %copy-start = (bf16[142,4544]{1,0:T(8,128)(2,1)S(1)}, bf16[142,4544]{1,0:T(8,128)(2,1)}, u32[]{:S(2)}) copy-start(bf16[142,4544]{1,0:T(8,128)(2,1)} %param.20) | copy-start | bytes 3871492
  6.5 121.1 %all-gather.3.cloned.1.call-start = ((), (), s32[]{:S(2)}) async-start(), calls=%async_computation.4 | async-start | bytes 2228224 | tf_op jit(solution)/shard_map/all_gather | solution.py:253
  15.6 20.3 %collective-permute-start.2 = (bf16[1,17280]{1,0:T(2,128)(2,1)S(1)}, bf16[1,17280]{1,0:T(2,128)(2,1)S(1)}, u32[]{:S(2)}, u32[]{:S(2)}) collective-permute-start(bf16[1,17280]{1,0:T(2,128)(2,1)S(1)} %broadcast_in_dim.150), channel_id=1, source_target_pairs={{0,12},{1,13},{2,14},{3,15},{4,8},{5,9},{6,10},{7,11},{8,4},{9,5},... | collective-permute-start | bytes 103688 | tf_op jit(solution)/shard_map/ppermute | solution.py:184
  26.5 17.7 %collective-permute-start.1 = (bf16[1,17280]{1,0:T(2,128)(2,1)S(1)}, bf16[1,17280]{1,0:T(2,128)(2,1)S(1)}, u32[]{:S(2)}, u32[]{:S(2)}) collective-permute-start(bf16[1,17280]{1,0:T(2,128)(2,1)S(1)} %broadcast_in_dim.150), channel_id=1, source_target_pairs={{0,8},{1,9},{2,10},{3,11},{4,12},{5,13},{6,14},{7,15},{8,0},{9,1},... | collective-permute-start | bytes 103688 | tf_op jit(solution)/shard_map/ppermute | solution.py:184
  32.0 13.6 %collective-permute-start = (bf16[1,17280]{1,0:T(2,128)(2,1)S(1)}, bf16[1,17280]{1,0:T(2,128)(2,1)S(1)}, u32[]{:S(2)}, u32[]{:S(2)}) collective-permute-start(bf16[1,17280]{1,0:T(2,128)(2,1)S(1)} %broadcast_in_dim.150), channel_id=1, source_target_pairs={{0,4},{1,5},{2,6},{3,7},{4,0},{5,1},{6,2},{7,3},{8,12},{9,13},{10,... | collective-permute-start | bytes 103688 | tf_op jit(solution)/shard_map/ppermute | solution.py:184
  46.5 16.4 %collective-permute-start.5 = (bf16[4,17280]{1,0:T(4,128)(2,1)S(1)}, bf16[4,17280]{1,0:T(4,128)(2,1)S(1)}, u32[]{:S(2)}, u32[]{:S(2)}) collective-permute-start(bf16[4,17280]{1,0:T(4,128)(2,1)S(1)} %fusion.156), channel_id=1, source_target_pairs={{0,3},{1,2},{2,1},{3,0},{4,7},{5,6},{6,5},{7,4},{8,11},{9,10},{10,... | collective-permute-start | bytes 414728 | tf_op jit(solution)/shard_map/ppermute | solution.py:184
  50.7 16.6 %collective-permute-start.4 = (bf16[4,17280]{1,0:T(4,128)(2,1)S(1)}, bf16[4,17280]{1,0:T(4,128)(2,1)S(1)}, u32[]{:S(2)}, u32[]{:S(2)}) collective-permute-start(bf16[4,17280]{1,0:T(4,128)(2,1)S(1)} %fusion.156), channel_id=1, source_target_pairs={{0,2},{1,3},{2,0},{3,1},{4,6},{5,7},{6,4},{7,5},{8,10},{9,11},{10,... | collective-permute-start | bytes 414728 | tf_op jit(solution)/shard_map/ppermute | solution.py:184
  54.6 12.7 %collective-permute-start.3 = (bf16[4,17280]{1,0:T(4,128)(2,1)S(1)}, bf16[4,17280]{1,0:T(4,128)(2,1)S(1)}, u32[]{:S(2)}, u32[]{:S(2)}) collective-permute-start(bf16[4,17280]{1,0:T(4,128)(2,1)S(1)} %fusion.156), channel_id=1, source_target_pairs={{0,1},{1,0},{2,3},{3,2},{4,5},{5,4},{6,7},{7,6},{8,9},{9,8},{10,11... | collective-permute-start | bytes 414728 | tf_op jit(solution)/shard_map/ppermute | solution.py:184
  70.1 4.5 %copy-start.1 = (s32[16]{0:T(128)S(1)}, s32[16]{0:T(128)}, u32[]{:S(2)}) copy-start(s32[16]{0:T(128)} %constant.240.clone) | copy-start | bytes 196
  70.1 5.8 %copy-start.9 = (s32[8]{0:T(128)S(1)}, s32[8]{0:T(128)}, u32[]{:S(2)}) copy-start(s32[8]{0:T(128)} %param.22) | copy-start | bytes 100
  70.1 31.3 %all-to-all-start = ((bf16[4,16,17280]{2,1,0:T(8,128)(2,1)}), bf16[4,16,17280]{2,1,0:T(8,128)(2,1)S(1)}, u32[]{:S(2)}, u32[]{:S(2)}) async-start(bf16[4,16,17280]{2,1,0:T(8,128)(2,1)} %broadcast_in_dim.152), calls=%async_computation | async-start | bytes 4423680 | tf_op jit(solution)/shard_map/all_to_all | solution.py:198
  105.9 1.9 copy-start.4
  107.8 0.7 copy-start.7
  107.8 0.7 copy-start.8
  107.8 12.9 %copy-start.2 = (bf16[4096,128]{1,0:T(8,128)(2,1)S(1)}, bf16[4096,128]{1,0:T(8,128)(2,1)}, u32[]{:S(2)}) copy-start(bf16[4096,128]{1,0:T(8,128)(2,1)} %reshape_reshape.4) | copy-start | bytes 3145732
  122.8 9.2 %copy-start.10 = (s32[32]{0:T(128)S(1)}, s32[32]{0:T(128)}, u32[]{:S(2)}) copy-start(s32[32]{0:T(128)} %iota_multiply_fusion) | copy-start | bytes 388
  128.7 4.2 %copy-start.3 = (bf16[8,32,8,128]{3,2,1,0:T(8,128)(2,1)}, bf16[8,32,8,128]{3,2,1,0:T(8,128)(2,1)S(1)}, u32[]{:S(2)}) copy-start(bf16[8,32,8,128]{3,2,1,0:T(8,128)(2,1)S(1)} %slice.91) | copy-start | bytes 1572868
  128.8 14.2 %collective-permute-start.6 = (bf16[8,32,8,128]{3,2,1,0:T(8,128)(2,1)S(1)}, bf16[8,32,8,128]{3,2,1,0:T(8,128)(2,1)}, u32[]{:S(2)}, u32[]{:S(2)}) collective-permute-start(bf16[8,32,8,128]{3,2,1,0:T(8,128)(2,1)S(1)} %slice.91), channel_id=1, source_target_pairs={{0,16},{1,17},{2,18},{3,19},{4,20},{5,21},{6,22},{7,23},{8,24},{9,... | collective-permute-start | bytes 1572872 | tf_op jit(solution)/shard_map/ppermute | solution.py:135
  144.0 12.4 %collective-permute-start.7 = (bf16[8,32,8,128]{3,2,1,0:T(8,128)(2,1)S(1)}, bf16[8,32,8,128]{3,2,1,0:T(8,128)(2,1)}, u32[]{:S(2)}, u32[]{:S(2)}) collective-permute-start(bf16[8,32,8,128]{3,2,1,0:T(8,128)(2,1)S(1)} %broadcast_select_fusion), channel_id=1, source_target_pairs={{0,48},{16,32},{1,49},{17,33},{2,50},{18,34},{3,51},{19,35},{4,52}... | collective-permute-start | bytes 1572872 | tf_op jit(solution)/shard_map/ppermute | solution.py:135
  157.5 4.9 %copy-start.11 = (s32[128]{0:T(128)S(1)}, s32[128]{0:T(128)}, u32[]{:S(2)}) copy-start(s32[128]{0:T(128)} %get-tuple-element.48) | copy-start | bytes 1540
  158.3 12.1 %copy-start.5 = (bf16[64,4544]{1,0:T(8,128)(2,1)S(1)}, bf16[64,4544]{1,0:T(8,128)(2,1)}, u32[]{:S(2)}) copy-start(bf16[64,4544]{1,0:T(8,128)(2,1)} %param.18) | copy-start | bytes 1744900
  159.0 11.2 %all-to-all-start.1 = ((f32[8,128,66]{1,2,0:T(8,128)}), f32[8,128,66]{1,2,0:T(8,128)S(1)}, u32[]{:S(2)}, u32[]{:S(2)}) async-start(f32[8,128,66]{1,2,0:T(8,128)} %pad_maximum_fusion.2), calls=%async_computation.1 | async-start | bytes 589824 | tf_op jit(solution)/shard_map/all_to_all | solution.py:313
  176.5 23.6 %all-to-all-start.2 = ((bf16[4,16,2,4544]{3,2,1,0:T(2,128)(2,1)}), bf16[4,16,2,4544]{3,2,1,0:T(2,128)(2,1)S(1)}, u32[]{:S(2)}, u32[]{:S(2)}) async-start(bf16[4,16,2,4544]{3,2,1,0:T(2,128)(2,1)} %convert_element_type.81), calls=%async_computation.2 | async-start | bytes 2359296 | tf_op jit(solution)/shard_map/all_to_all | solution.py:211
  184.0 47.6 %copy-start.6 = (bf16[1,2,4544]{2,1,0:T(2,128)(2,1)S(1)}, bf16[1,2,4544]{2,1,0:T(2,128)(2,1)}, u32[]{:S(2)}) copy-start(bf16[1,2,4544]{2,1,0:T(2,128)(2,1)} %param.13) | copy-start | bytes 54532
Sparse Core Ops, SparseCore 0:
  35.9 77.1 all-gather.2

commit v7 on v5

--- a/solution.py
+++ b/solution.py
@@ -174,6 +174,12 @@
     buf = z_rounds(piece)
     wide = jnp.broadcast_to(buf[None], (nx,) + buf.shape)
     return lax.all_to_all(wide, "tx", 0, 0, tiled=True).reshape((-1,) + piece.shape)
+
+
+def x_spread(buf):
+    nx = lax.axis_size("tx")
+    wide = jnp.broadcast_to(buf[None], (nx,) + buf.shape)
+    return lax.all_to_all(wide, "tx", 0, 0, tiled=True).reshape((-1,) + buf.shape[2:])
 
 
 def slot_source(index):
@@ -218,9 +224,11 @@
 
     long_local = lax.dynamic_index_in_dim(kv_cache, longest, 0, keepdims=False)
     normed = norm_rows(tokens[0], ln_gain, ln_bias)
-    both = gather_tensor(jnp.concatenate([normed.reshape(-1), long_local.reshape(-1)]))
+    both = z_rounds(jnp.concatenate([normed.reshape(-1), long_local.reshape(-1)]))
     token_cut = normed.size
-    long_all = both[:, token_cut:].reshape((n,) + long_local.shape)
+    token_all = x_spread(both[:, :token_cut])
+    token_all, long_half = lax.optimization_barrier((token_all, both[:, token_cut:]))
+    long_all = x_spread(long_half).reshape((n,) + long_local.shape)
     slot_src = slot_source(jnp.arange(n, dtype=jnp.int32))
     long_block = slot_src[:, None] * blocks_here + jnp.arange(blocks_here, dtype=jnp.int32)
     long_pos = (long_block[:, :, None] * inner_all + inner_pos).reshape(-1)
@@ -230,7 +238,7 @@
     short_gath = lax.all_gather(kv_cache, "tz", axis=1, tiled=True)[:, :short_blocks]
     short_pos = (jnp.arange(short_blocks, dtype=jnp.int32)[:, None] * inner_all + inner_pos).reshape(-1)
 
-    piece = both[:, :token_cut].reshape(n * per_device, width_model)
+    piece = token_all.reshape(n * per_device, width_model)
     projected = jnp.concatenate(
         [
             jnp.dot(piece, q_weight, preferred_element_type=jnp.float32),

time: 234 us -> 245 us (1.047)
  waiting for transfers between devices: 73.5 us -> 77.4 us
  blocking collectives: 39.5 us -> 43.2 us
    all_gather x1, waiting for transfers between devices: 10.3 us -> 0.01 us  [local(): lax.all_gather(kv_cache, 'tz', axis=1, tiled=True)[:, :short_blocks]]
    ppermute x2, waiting for transfers between devices: 8.04 us -> 16 us  [spread_from_first(): got = lax.ppermute(x, name, pairs)]
    ppermute x4, waiting for transfers between devices: 14.7 us -> 22.6 us  [z_rounds(): other = lax.ppermute(buf, 'tz', [(i, i ^ 1 << b) for i in range(size)])]
    all_to_all x1, blocking collectives: 27.4 us -> 31.9 us  [scatter_tensor(): lax.all_to_all(ready, 'tz', 0, 0, tiled=True).astype(jnp.float32).sum(0)]
    all_to_all x1 -> x2, starting transfers between devices: 4.45 us -> 7.8 us  [x_spread(): lax.all_to_all(wide, 'tx', 0, 0, tiled=True).reshape((-1,) + buf.shape[2:])]
    reshape x1 -> x2, local copies, waits for them, and re-layouts: 1.85 us -> 4.94 us  [the longest x1 2.81 us: x_spread(): lax.all_to_all(wide, 'tx', 0, 0, tiled=True).reshape((-1,) + buf.shape[2:])]
    all_to_all x1 -> x2, waiting for transfers between devices: 16.8 us -> 14.5 us  [x_spread(): lax.all_to_all(wide, 'tx', 0, 0, tiled=True).reshape((-1,) + buf.shape[2:])]
  transfers between devices with their start and end apart: 10 -> 11, of which waited for: 10 -> 9; matrix products, arithmetic and copies ran while one was open for 12% -> 15% of each run, Pallas kernels for 0% -> 0%
where the time goes in v7:
time: 245 us; the launch traced here: 243 us
  waiting for transfers between devices  77.4 us (32%)
  starting transfers between devices  54.9 us (22%)
  blocking collectives  43.2 us (18%)
  local copies, waits for them, and re-layouts  21.6 us (9%)
  between operations  15.9 us (6%)
  other arithmetic  15.5 us (6%)
  matrix products  14.8 us (6%)
    all_to_all x1, blocking collectives, scatter_tensor(): lax.all_to_all(ready, 'tz', 0, 0, tiled=True).astype(jnp.float32).sum(0)  31.9 us
    ppermute x4, starting transfers between devices, z_rounds(): other = lax.ppermute(buf, 'tz', [(i, i ^ 1 << b) for i in range(size)])  29.7 us
    ppermute x4, waiting for transfers between devices, z_rounds(): other = lax.ppermute(buf, 'tz', [(i, i ^ 1 << b) for i in range(size)])  22.6 us
    all_to_all x1, waiting for transfers between devices, scatter_tensor(): lax.all_to_all(buf, 'tx', 0, 0, tiled=True).astype(jnp.float32).sum(0)  16.1 us
    ppermute x2, waiting for transfers between devices, spread_from_first(): got = lax.ppermute(x, name, pairs)  16 us
    all_to_all x2, waiting for transfers between devices, x_spread(): lax.all_to_all(wide, 'tx', 0, 0, tiled=True).reshape((-1,) + buf.shape[2:])  14.5 us
    all_gather x1, blocking collectives, local(): q_all = lax.all_gather(query_rows, 'dp', axis=0, tiled=False)  11.3 us
    all_to_all x2, starting transfers between devices, x_spread(): lax.all_to_all(wide, 'tx', 0, 0, tiled=True).reshape((-1,) + buf.shape[2:])  7.8 us
  transfers between devices with their start and end apart: 11, of which 9 were waited for; matrix products, arithmetic and copies ran while one was open for 15% of the time, Pallas kernels for 0%

profile of v7, /device:TPU:64, one launch (start us, length us, event | category | flops | bytes accessed | tf_op | source)
XLA Modules:
  0.0 243.3 jit_solution(1502850672744337550)
XLA Ops:
  7.3 0.9 convert_reduce_fusion.2
  8.1 0.8 reshape.593
  8.9 1.3 iota_reduce_fusion
  14.5 0.9 fusion.39
  15.9 13.9 %collective-permute-start = (bf16[1,17280]{1,0:T(2,128)(2,1)S(1)}, bf16[1,17280]{1,0:T(2,128)(2,1)S(1)}, u32[]{:S(2)}, u32[]{:S(2)}) collective-permute-start(bf16[1,17280]{1,0:T(2,128)(2,1)S(1)} %broadcast_in_dim.153), channel_id=1, source_target_pairs={{0,8},{1,9},{2,10},{3,11},{4,12},{5,13},{6,14},{7,15},{8,0},{9,1},... | collective-permute-start | bytes 103688 | tf_op jit(solution)/shard_map/ppermute | solution.py:164
  30.0 1.4 fusion.134
  31.4 5.3 %collective-permute-done = bf16[1,17280]{1,0:T(2,128)(2,1)S(1)} collective-permute-done((bf16[1,17280]{1,0:T(2,128)(2,1)S(1)}, bf16[1,17280]{1,0:T(2,128)(2,1)S(1)}, u32[]{:S(2)}, u32[]{:S(2)}) %collective-permute-start) | collective-permute-done | bytes 34592 | tf_op jit(solution)/shard_map/ppermute | solution.py:164
  37.0 7.0 %collective-permute-start.1 = (bf16[2,17280]{1,0:T(2,128)(2,1)S(1)}, bf16[2,17280]{1,0:T(2,128)(2,1)S(1)}, u32[]{:S(2)}, u32[]{:S(2)}) collective-permute-start(bf16[2,17280]{1,0:T(2,128)(2,1)S(1)} %pad_maximum_fusion.4), channel_id=1, source_target_pairs={{0,4},{1,5},{2,6},{3,7},{4,0},{5,1},{6,2},{7,3},{8,12},{9,13},{10,... | collective-permute-start | bytes 207368 | tf_op jit(solution)/shard_map/ppermute | solution.py:164
  44.0 0.8 add_compare_fusion
  44.8 4.5 %collective-permute-done.1 = bf16[2,17280]{1,0:T(2,128)(2,1)S(1)} collective-permute-done((bf16[2,17280]{1,0:T(2,128)(2,1)S(1)}, bf16[2,17280]{1,0:T(2,128)(2,1)S(1)}, u32[]{:S(2)}, u32[]{:S(2)}) %collective-permute-start.1) | collective-permute-done | bytes 69152 | tf_op jit(solution)/shard_map/ppermute | solution.py:164
  49.7 4.4 %collective-permute-start.2 = (bf16[4,17280]{1,0:T(4,128)(2,1)S(1)}, bf16[4,17280]{1,0:T(4,128)(2,1)S(1)}, u32[]{:S(2)}, u32[]{:S(2)}) collective-permute-start(bf16[4,17280]{1,0:T(4,128)(2,1)S(1)} %pad_maximum_fusion.3), channel_id=1, source_target_pairs={{0,2},{1,3},{2,0},{3,1},{4,6},{5,7},{6,4},{7,5},{8,10},{9,11},{10,... | collective-permute-start | bytes 414728 | tf_op jit(solution)/shard_map/ppermute | solution.py:164
  54.1 1.2 fusion.92
  55.3 3.9 %collective-permute-done.2 = bf16[4,17280]{1,0:T(4,128)(2,1)S(1)} collective-permute-done((bf16[4,17280]{1,0:T(4,128)(2,1)S(1)}, bf16[4,17280]{1,0:T(4,128)(2,1)S(1)}, u32[]{:S(2)}, u32[]{:S(2)}) %collective-permute-start.2) | collective-permute-done | bytes 138272 | tf_op jit(solution)/shard_map/ppermute | solution.py:164
  59.5 4.4 %collective-permute-start.3 = (bf16[8,17280]{1,0:T(8,128)(2,1)S(1)}, bf16[8,17280]{1,0:T(8,128)(2,1)S(1)}, u32[]{:S(2)}, u32[]{:S(2)}) collective-permute-start(bf16[8,17280]{1,0:T(8,128)(2,1)S(1)} %pad_maximum_fusion.1), channel_id=1, source_target_pairs={{0,1},{1,0},{2,3},{3,2},{4,5},{5,4},{6,7},{7,6},{8,9},{9,8},{10,11... | collective-permute-start | bytes 829448 | tf_op jit(solution)/shard_map/ppermute | solution.py:164
  64.5 0.8 lt.86
  65.4 8.9 %collective-permute-done.3 = bf16[8,17280]{1,0:T(8,128)(2,1)S(1)} collective-permute-done((bf16[8,17280]{1,0:T(8,128)(2,1)S(1)}, bf16[8,17280]{1,0:T(8,128)(2,1)S(1)}, u32[]{:S(2)}, u32[]{:S(2)}) %collective-permute-start.3) | collective-permute-done | bytes 276512 | tf_op jit(solution)/shard_map/ppermute | solution.py:164
  74.6 1.1 broadcast_in_dim.154
  75.7 3.5 %all-to-all-start = ((bf16[4,16,9088]{2,1,0:T(8,128)(2,1)}), bf16[4,16,9088]{2,1,0:T(8,128)(2,1)S(1)}, u32[]{:S(2)}, u32[]{:S(2)}) async-start(bf16[4,16,9088]{2,1,0:T(8,128)(2,1)} %broadcast_in_dim.154), calls=%async_computation | async-start | bytes 2326528 | tf_op jit(solution)/shard_map/all_to_all | solution.py:182
  79.2 14.5 %all-to-all-done = bf16[4,16,9088]{2,1,0:T(8,128)(2,1)S(1)} async-done(((bf16[4,16,9088]{2,1,0:T(8,128)(2,1)}), bf16[4,16,9088]{2,1,0:T(8,128)(2,1)S(1)}, u32[]{:S(2)}, u32[]{:S(2)}) %all-to-all-start) | async-done | bytes 1163296 | tf_op jit(solution)/shard_map/all_to_all | solution.py:182
  93.7 2.8 %reshape.589 = bf16[581632]{0:T(1024)(128)(2,1)} reshape(bf16[4,16,9088]{2,1,0:T(8,128)(2,1)S(1)} %all-to-all-done) | data formatting | bytes 2326528 | tf_op jit(solution)/shard_map/reshape | solution.py:182
  96.5 1.1 broadcast_in_dim.156
  97.6 4.3 %all-to-all-start.1 = ((bf16[4,16,8192]{2,1,0:T(8,128)(2,1)}), bf16[4,16,8192]{2,1,0:T(8,128)(2,1)}, u32[]{:S(2)}, u32[]{:S(2)}) async-start(bf16[4,16,8192]{2,1,0:T(8,128)(2,1)} %broadcast_in_dim.156), calls=%async_computation.1 | async-start | bytes 2097152 | tf_op jit(solution)/shard_map/all_to_all | solution.py:182
  101.9 2.1 reshape.590
  105.2 11.3 %all-gather = bf16[1024,64]{0,1:T(8,128)(2,1)S(1)} all-gather(bf16[128,64]{0,1:T(8,128)(2,1)S(1)} %fusion.76), channel_id=2, replica_groups=mesh['dp'=8,'tx'=4,'tz'=16] {'dp'}, dimensions={0}, use_global_device_ids=true | all-gather | bytes 147456 | tf_op jit(solution)/shard_map/all_gather | solution.py:271
  117.8 4.8 %fusion.35 = f32[128,4544]{0,1:T(8,128)} fusion(bf16[142,4544]{1,0:T(8,128)(2,1)S(1)} %copy-done, bf16[128,4544]{1,0:T(8,128)(2,1)S(1)} %reshape.590, bf16[4544,142]{0,1:T(8,128)(2,1)} %param.17), kind=kOutput, calls=%fused_computation.74 | convolution fusion | flops 331548416 | bytes 6070784 | tf_op jit(solution)/shard_map/dot_general | solution.py:276
  122.6 1.6 reshape_reshape_reshape.3
  124.2 1.3 fusion.135
  125.5 1.0 fusion.2
  126.5 1.7 fusion.10
  128.1 1.1 slice.73
  129.2 4.7 %collective-permute-start.4 = (bf16[8,32,8,128]{3,2,1,0:T(8,128)(2,1)S(1)}, bf16[8,32,8,128]{3,2,1,0:T(8,128)(2,1)}, u32[]{:S(2)}, u32[]{:S(2)}) collective-permute-start(bf16[8,32,8,128]{3,2,1,0:T(8,128)(2,1)S(1)} %slice.73), channel_id=1, source_target_pairs={{0,16},{1,17},{2,18},{3,19},{4,20},{5,21},{6,22},{7,23},{8,24},{9,... | collective-permute-start | bytes 1572872 | tf_op jit(solution)/shard_map/ppermute | solution.py:135
  135.3 1.3 compare_and_fusion
  136.6 8.1 %collective-permute-done.4 = bf16[8,32,8,128]{3,2,1,0:T(8,128)(2,1)} collective-permute-done((bf16[8,32,8,128]{3,2,1,0:T(8,128)(2,1)S(1)}, bf16[8,32,8,128]{3,2,1,0:T(8,128)(2,1)}, u32[]{:S(2)}, u32[]{:S(2)}) %collective-permute-start.4) | collective-permute-done | bytes 524320 | tf_op jit(solution)/shard_map/ppermute | solution.py:135
  144.8 1.5 collective-permute-start.5
  146.3 1.1 iota_compare_fusion
  147.5 1.8 fusion.141
  149.3 7.9 %collective-permute-done.5 = bf16[8,32,8,128]{3,2,1,0:T(8,128)(2,1)S(1)} collective-permute-done((bf16[8,32,8,128]{3,2,1,0:T(8,128)(2,1)S(1)}, bf16[8,32,8,128]{3,2,1,0:T(8,128)(2,1)S(1)}, u32[]{:S(2)}, u32[]{:S(2)}) %collective-permute-start.5) | collective-permute-done | bytes 524320 | tf_op jit(solution)/shard_map/ppermute | solution.py:135
  158.4 0.8 fusion.5
  159.9 3.7 %all-to-all-start.2 = ((f32[8,128,66]{1,2,0:T(8,128)}), f32[8,128,66]{1,2,0:T(8,128)S(1)}, u32[]{:S(2)}, u32[]{:S(2)}) async-start(f32[8,128,66]{1,2,0:T(8,128)} %pad_maximum_fusion), calls=%async_computation.2 | async-start | bytes 589824 | tf_op jit(solution)/shard_map/all_to_all | solution.py:298
  163.9 7.5 %all-to-all-done.2 = f32[8,128,66]{1,2,0:T(8,128)S(1)} async-done(((f32[8,128,66]{1,2,0:T(8,128)}), f32[8,128,66]{1,2,0:T(8,128)S(1)}, u32[]{:S(2)}, u32[]{:S(2)}) %all-to-all-start.2) | async-done | bytes 270368 | tf_op jit(solution)/shard_map/all_to_all | solution.py:298
  171.6 3.3 %fusion = bf16[128,4544]{0,1:T(8,128)(2,1)} fusion(f32[128,4544]{0,1:T(8,128)} %fusion.35, bf16[64,4544]{1,0:T(8,128)(2,1)S(1)} %copy-done.4, f32[128,128]{0,1:T(8,128)S(1)} %get-tuple-element.51, f32[128]{0:T(128)S(1)} %get-tuple-element.50, f32[128,64]{0,1:T(8,128)S(1)} %fusion.22, f32[128,128]{0,1:T(8,128)S(1)} %copy-done.7, ...), kind=kOutput, calls=%fused_computation.2 | convolution fusion | flops 77783040 | bytes 4196352 | tf_op jit(solution)/shard_map/dot_general | solution.py:312
  174.9 1.6 copy.52
  176.5 1.3 convert_element_type.81
  177.8 7.5 %all-to-all-start.3 = ((bf16[4,16,2,4544]{3,2,1,0:T(2,128)(2,1)}), bf16[4,16,2,4544]{3,2,1,0:T(2,128)(2,1)S(1)}, u32[]{:S(2)}, u32[]{:S(2)}) async-start(bf16[4,16,2,4544]{3,2,1,0:T(2,128)(2,1)} %convert_element_type.81), calls=%async_computation.3 | async-start | bytes 2359296 | tf_op jit(solution)/shard_map/all_to_all | solution.py:194
  185.4 16.1 %all-to-all-done.3 = bf16[4,16,2,4544]{3,2,1,0:T(2,128)(2,1)S(1)} async-done(((bf16[4,16,2,4544]{3,2,1,0:T(2,128)(2,1)}), bf16[4,16,2,4544]{3,2,1,0:T(2,128)(2,1)S(1)}, u32[]{:S(2)}, u32[]{:S(2)}) %all-to-all-start.3) | async-done | bytes 1163296 | tf_op jit(solution)/shard_map/all_to_all | solution.py:194
  201.4 1.2 convert_reduce_fusion
  202.6 1.1 gather_fusion
  203.7 31.9 %all_to_all.25 = bf16[16,2,4544]{2,1,0:T(2,128)(2,1)S(1)} all-to-all(bf16[16,2,4544]{2,1,0:T(2,128)(2,1)S(1)} %gather_fusion), channel_id=1, replica_groups=mesh['dp'=8,'tx'=4,'tz'=16] {'tz'}, dimensions={0} | all-to-all | bytes 581632 | tf_op jit(solution)/shard_map/all_to_all | solution.py:197
  (105 shorter events, 12.6 us)
Async XLA Ops:
  6.5 111.3 %copy-start = (bf16[142,4544]{1,0:T(8,128)(2,1)S(1)}, bf16[142,4544]{1,0:T(8,128)(2,1)}, u32[]{:S(2)}) copy-start(bf16[142,4544]{1,0:T(8,128)(2,1)} %param.18) | copy-start | bytes 3871492
  6.5 121.6 %all-gather.3.cloned.1.call-start = ((), (), s32[]{:S(2)}) async-start(), calls=%async_computation.5 | async-start | bytes 2228224 | tf_op jit(solution)/shard_map/all_gather | solution.py:238
  15.9 20.8 %collective-permute-start = (bf16[1,17280]{1,0:T(2,128)(2,1)S(1)}, bf16[1,17280]{1,0:T(2,128)(2,1)S(1)}, u32[]{:S(2)}, u32[]{:S(2)}) collective-permute-start(bf16[1,17280]{1,0:T(2,128)(2,1)S(1)} %broadcast_in_dim.153), channel_id=1, source_target_pairs={{0,8},{1,9},{2,10},{3,11},{4,12},{5,13},{6,14},{7,15},{8,0},{9,1},... | collective-permute-start | bytes 103688 | tf_op jit(solution)/shard_map/ppermute | solution.py:164
  30.0 14.9 %copy-start.19 = (s32[8]{0:T(128)}, s32[8]{0:T(128)S(1)}, u32[]{:S(2)}) copy-start(s32[8]{0:T(128)S(1)} %iota_add_fusion) | copy-start | bytes 100
  37.0 12.3 %collective-permute-start.1 = (bf16[2,17280]{1,0:T(2,128)(2,1)S(1)}, bf16[2,17280]{1,0:T(2,128)(2,1)S(1)}, u32[]{:S(2)}, u32[]{:S(2)}) collective-permute-start(bf16[2,17280]{1,0:T(2,128)(2,1)S(1)} %pad_maximum_fusion.4), channel_id=1, source_target_pairs={{0,4},{1,5},{2,6},{3,7},{4,0},{5,1},{6,2},{7,3},{8,12},{9,13},{10,... | collective-permute-start | bytes 207368 | tf_op jit(solution)/shard_map/ppermute | solution.py:164
  49.7 9.5 %collective-permute-start.2 = (bf16[4,17280]{1,0:T(4,128)(2,1)S(1)}, bf16[4,17280]{1,0:T(4,128)(2,1)S(1)}, u32[]{:S(2)}, u32[]{:S(2)}) collective-permute-start(bf16[4,17280]{1,0:T(4,128)(2,1)S(1)} %pad_maximum_fusion.3), channel_id=1, source_target_pairs={{0,2},{1,3},{2,0},{3,1},{4,6},{5,7},{6,4},{7,5},{8,10},{9,11},{10,... | collective-permute-start | bytes 414728 | tf_op jit(solution)/shard_map/ppermute | solution.py:164
  59.5 14.8 %collective-permute-start.3 = (bf16[8,17280]{1,0:T(8,128)(2,1)S(1)}, bf16[8,17280]{1,0:T(8,128)(2,1)S(1)}, u32[]{:S(2)}, u32[]{:S(2)}) collective-permute-start(bf16[8,17280]{1,0:T(8,128)(2,1)S(1)} %pad_maximum_fusion.1), channel_id=1, source_target_pairs={{0,1},{1,0},{2,3},{3,2},{4,5},{5,4},{6,7},{7,6},{8,9},{9,8},{10,11... | collective-permute-start | bytes 829448 | tf_op jit(solution)/shard_map/ppermute | solution.py:164
  65.4 39.2 %copy-start.11 = (f32[128,32]{0,1:T(8,128)}, f32[128,32]{0,1:T(8,128)S(1)}, u32[]{:S(2)}) copy-start(f32[128,32]{0,1:T(8,128)S(1)} %get-tuple-element.42) | copy-start | bytes 49156
  65.4 39.2 %copy-start.13 = (f32[128,32]{0,1:T(8,128)}, f32[128,32]{0,1:T(8,128)S(1)}, u32[]{:S(2)}) copy-start(f32[128,32]{0,1:T(8,128)S(1)} %get-tuple-element.43) | copy-start | bytes 49156
  75.7 18.1 %all-to-all-start = ((bf16[4,16,9088]{2,1,0:T(8,128)(2,1)}), bf16[4,16,9088]{2,1,0:T(8,128)(2,1)S(1)}, u32[]{:S(2)}, u32[]{:S(2)}) async-start(bf16[4,16,9088]{2,1,0:T(8,128)(2,1)} %broadcast_in_dim.154), calls=%async_computation | async-start | bytes 2326528 | tf_op jit(solution)/shard_map/all_to_all | solution.py:182
  97.6 25.0 %all-to-all-start.1 = ((bf16[4,16,8192]{2,1,0:T(8,128)(2,1)}), bf16[4,16,8192]{2,1,0:T(8,128)(2,1)}, u32[]{:S(2)}, u32[]{:S(2)}) async-start(bf16[4,16,8192]{2,1,0:T(8,128)(2,1)} %broadcast_in_dim.156), calls=%async_computation.1 | async-start | bytes 2097152 | tf_op jit(solution)/shard_map/all_to_all | solution.py:182
  101.9 2.1 copy-start.3
  104.6 0.6 copy-start.9
  116.5 0.7 copy-start.1
  125.5 1.0 copy-start.15
  129.2 15.6 %collective-permute-start.4 = (bf16[8,32,8,128]{3,2,1,0:T(8,128)(2,1)S(1)}, bf16[8,32,8,128]{3,2,1,0:T(8,128)(2,1)}, u32[]{:S(2)}, u32[]{:S(2)}) collective-permute-start(bf16[8,32,8,128]{3,2,1,0:T(8,128)(2,1)S(1)} %slice.73), channel_id=1, source_target_pairs={{0,16},{1,17},{2,18},{3,19},{4,20},{5,21},{6,22},{7,23},{8,24},{9,... | collective-permute-start | bytes 1572872 | tf_op jit(solution)/shard_map/ppermute | solution.py:135
  144.8 12.4 %collective-permute-start.5 = (bf16[8,32,8,128]{3,2,1,0:T(8,128)(2,1)S(1)}, bf16[8,32,8,128]{3,2,1,0:T(8,128)(2,1)S(1)}, u32[]{:S(2)}, u32[]{:S(2)}) collective-permute-start(bf16[8,32,8,128]{3,2,1,0:T(8,128)(2,1)S(1)} %broadcast_select_fusion), channel_id=1, source_target_pairs={{0,48},{16,32},{1,49},{17,33},{2,50},{18,34},{3,51},{19,35},{4,52}... | collective-permute-start | bytes 1572872 | tf_op jit(solution)/shard_map/ppermute | solution.py:135
  149.3 8.5 %copy-start.6 = (f32[128,128]{0,1:T(8,128)}, f32[128,128]{0,1:T(8,128)S(1)}, u32[]{:S(2)}) copy-start(f32[128,128]{0,1:T(8,128)S(1)} %fusion.141) | copy-start | bytes 196612
  149.3 8.0 %copy-start.2 = (bf16[1024,64]{0,1:T(8,128)(2,1)S(1)}, bf16[1024,64]{0,1:T(8,128)(2,1)}, u32[]{:S(2)}) copy-start(bf16[1024,64]{0,1:T(8,128)(2,1)} %copy-done.1) | copy-start | bytes 393220
  149.3 8.0 %copy-start.17 = (pred[8,256]{1,0:T(8,128)(4,1)S(1)}, pred[8,256]{1,0:T(8,128)(4,1)}, u32[]{:S(2)}) copy-start(pred[8,256]{1,0:T(8,128)(4,1)} %compare_and_fusion) | copy-start | bytes 6148
  157.3 0.9 copy-start.16
  157.3 0.9 copy-start.18
  157.3 0.9 copy-start.20
  157.3 1.0 copy-start.8
  158.4 5.2 %copy-start.7 = (f32[128,128]{0,1:T(8,128)S(1)}, f32[128,128]{0,1:T(8,128)}, u32[]{:S(2)}) copy-start(f32[128,128]{0,1:T(8,128)} %copy-done.6) | copy-start | bytes 196612
  158.4 5.2 %copy-start.10 = (bf16[128,64]{0,1:T(8,128)(2,1)S(1)}, bf16[128,64]{0,1:T(8,128)(2,1)}, u32[]{:S(2)}) copy-start(bf16[128,64]{0,1:T(8,128)(2,1)} %copy-done.9) | copy-start | bytes 49156
  158.4 5.2 %copy-start.12 = (f32[128,32]{0,1:T(8,128)S(1)}, f32[128,32]{0,1:T(8,128)}, u32[]{:S(2)}) copy-start(f32[128,32]{0,1:T(8,128)} %copy-done.11) | copy-start | bytes 49156
  158.4 5.2 %copy-start.14 = (f32[128,32]{0,1:T(8,128)S(1)}, f32[128,32]{0,1:T(8,128)}, u32[]{:S(2)}) copy-start(f32[128,32]{0,1:T(8,128)} %copy-done.13) | copy-start | bytes 49156
  158.4 5.2 %copy-start.22 = (s32[128]{0:T(128)S(1)}, s32[128]{0:T(128)}, u32[]{:S(2)}) copy-start(s32[128]{0:T(128)} %get-tuple-element.52) | copy-start | bytes 1540
  159.2 12.4 %copy-start.4 = (bf16[64,4544]{1,0:T(8,128)(2,1)S(1)}, bf16[64,4544]{1,0:T(8,128)(2,1)}, u32[]{:S(2)}) copy-start(bf16[64,4544]{1,0:T(8,128)(2,1)} %param.16) | copy-start | bytes 1744900
  159.9 11.5 %all-to-all-start.2 = ((f32[8,128,66]{1,2,0:T(8,128)}), f32[8,128,66]{1,2,0:T(8,128)S(1)}, u32[]{:S(2)}, u32[]{:S(2)}) async-start(f32[8,128,66]{1,2,0:T(8,128)} %pad_maximum_fusion), calls=%async_computation.2 | async-start | bytes 589824 | tf_op jit(solution)/shard_map/all_to_all | solution.py:298
  177.8 7.6 %copy-start.21 = (s32[16]{0:T(128)S(1)}, s32[16]{0:T(128)}, u32[]{:S(2)}) copy-start(s32[16]{0:T(128)} %constant.238) | copy-start | bytes 196
  177.8 23.6 %all-to-all-start.3 = ((bf16[4,16,2,4544]{3,2,1,0:T(2,128)(2,1)}), bf16[4,16,2,4544]{3,2,1,0:T(2,128)(2,1)S(1)}, u32[]{:S(2)}, u32[]{:S(2)}) async-start(bf16[4,16,2,4544]{3,2,1,0:T(2,128)(2,1)} %convert_element_type.81), calls=%async_computation.3 | async-start | bytes 2359296 | tf_op jit(solution)/shard_map/all_to_all | solution.py:194
  185.3 50.5 %copy-start.5 = (bf16[1,2,4544]{2,1,0:T(2,128)(2,1)S(1)}, bf16[1,2,4544]{2,1,0:T(2,128)(2,1)}, u32[]{:S(2)}) copy-start(bf16[1,2,4544]{2,1,0:T(2,128)(2,1)} %param.11) | copy-start | bytes 54532
Sparse Core Ops, SparseCore 0:
  9.4 81.9 all-gather.2

commit v8 on v7

--- a/solution.py
+++ b/solution.py
@@ -221,11 +221,14 @@
     longest = jnp.argmax(cache_lengths).astype(jnp.int32)
     long_length = lax.dynamic_index_in_dim(cache_lengths, longest, 0, keepdims=False)
     inner_pos = group * inner_here + jnp.arange(inner_here, dtype=jnp.int32)
+    short_blocks = -(-SHORT_MAX // inner_all)
 
     long_local = lax.dynamic_index_in_dim(kv_cache, longest, 0, keepdims=False)
     normed = norm_rows(tokens[0], ln_gain, ln_bias)
     both = z_rounds(jnp.concatenate([normed.reshape(-1), long_local.reshape(-1)]))
     token_cut = normed.size
+    both, cache_here = lax.optimization_barrier((both, kv_cache))
+    short_gath = lax.all_gather(cache_here, "tz", axis=1, tiled=True)[:, :short_blocks]
     token_all = x_spread(both[:, :token_cut])
     token_all, long_half = lax.optimization_barrier((token_all, both[:, token_cut:]))
     long_all = x_spread(long_half).reshape((n,) + long_local.shape)
@@ -234,8 +237,6 @@
     long_pos = (long_block[:, :, None] * inner_all + inner_pos).reshape(-1)
     long_keys = long_all.reshape(-1, 2 * width)
 
-    short_blocks = -(-SHORT_MAX // inner_all)
-    short_gath = lax.all_gather(kv_cache, "tz", axis=1, tiled=True)[:, :short_blocks]
     short_pos = (jnp.arange(short_blocks, dtype=jnp.int32)[:, None] * inner_all + inner_pos).reshape(-1)
 
     piece = token_all.reshape(n * per_device, width_model)

time: 245 us -> 240 us (0.980)
  waiting for transfers between devices: 77.4 us -> 73.1 us
  blocking collectives: 43.2 us -> 38.9 us
  starting transfers between devices: 54.9 us -> 58.6 us
    all_gather x1, waiting for transfers between devices: 0.01 us -> 20.1 us  [local(): lax.all_gather(cache_here, 'tz', axis=1, tiled=True)[:, :short_blocks]]
    ppermute x2, waiting for transfers between devices: 16 us -> 6.51 us  [spread_from_first(): got = lax.ppermute(x, name, pairs)]
    ppermute x4, waiting for transfers between devices: 22.6 us -> 14.7 us  [z_rounds(): other = lax.ppermute(buf, 'tz', [(i, i ^ 1 << b) for i in range(size)])]
    all_to_all x2, waiting for transfers between devices: 14.5 us -> 8.22 us  [x_spread(): lax.all_to_all(wide, 'tx', 0, 0, tiled=True).reshape((-1,) + buf.shape[2:])]
    all_to_all x1, blocking collectives: 31.9 us -> 26.8 us  [scatter_tensor(): lax.all_to_all(ready, 'tz', 0, 0, tiled=True).astype(jnp.float32).sum(0)]
  transfers between devices with their start and end apart: 11 -> 11, of which waited for: 9 -> 10; matrix products, arithmetic and copies ran while one was open for 15% -> 12% of each run, Pallas kernels for 0% -> 0%
where the time goes in v8:
time: 240 us; the launch traced here: 239 us
  waiting for transfers between devices  73.1 us (30%)
  starting transfers between devices  58.6 us (24%)
  blocking collectives  38.9 us (16%)
  local copies, waits for them, and re-layouts  21.5 us (9%)
  between operations  16 us (7%)
  other arithmetic  15.7 us (7%)
  matrix products  14.8 us (6%)
    ppermute x4, starting transfers between devices, z_rounds(): other = lax.ppermute(buf, 'tz', [(i, i ^ 1 << b) for i in range(size)])  31.9 us
    all_to_all x1, blocking collectives, scatter_tensor(): lax.all_to_all(ready, 'tz', 0, 0, tiled=True).astype(jnp.float32).sum(0)  26.8 us
    all_gather x1, waiting for transfers between devices, local(): lax.all_gather(cache_here, 'tz', axis=1, tiled=True)[:, :short_blocks]  20.1 us
    all_to_all x1, waiting for transfers between devices, scatter_tensor(): lax.all_to_all(buf, 'tx', 0, 0, tiled=True).astype(jnp.float32).sum(0)  16.1 us
    ppermute x4, waiting for transfers between devices, z_rounds(): other = lax.ppermute(buf, 'tz', [(i, i ^ 1 << b) for i in range(size)])  14.7 us
    all_gather x1, blocking collectives, local(): q_all = lax.all_gather(query_rows, 'dp', axis=0, tiled=False)  12.1 us
    all_to_all x2, starting transfers between devices, x_spread(): lax.all_to_all(wide, 'tx', 0, 0, tiled=True).reshape((-1,) + buf.shape[2:])  8.59 us
    all_to_all x2, waiting for transfers between devices, x_spread(): lax.all_to_all(wide, 'tx', 0, 0, tiled=True).reshape((-1,) + buf.shape[2:])  8.22 us
  transfers between devices with their start and end apart: 11, of which 10 were waited for; matrix products, arithmetic and copies ran while one was open for 12% of the time, Pallas kernels for 0%

profile of v8, /device:TPU:64, one launch (start us, length us, event | category | flops | bytes accessed | tf_op | source)
XLA Modules:
  0.0 238.6 jit_solution(3491469602888795642)
XLA Ops:
  6.5 1.0 convert_reduce_fusion.2
  7.5 0.8 reshape.593
  8.3 1.3 iota_reduce_fusion
  12.6 0.9 fusion.38
  15.4 13.9 %collective-permute-start = (bf16[1,17280]{1,0:T(2,128)(2,1)S(1)}, bf16[1,17280]{1,0:T(2,128)(2,1)S(1)}, u32[]{:S(2)}, u32[]{:S(2)}) collective-permute-start(bf16[1,17280]{1,0:T(2,128)(2,1)S(1)} %broadcast_in_dim.153), channel_id=1, source_target_pairs={{0,8},{1,9},{2,10},{3,11},{4,12},{5,13},{6,14},{7,15},{8,0},{9,1},... | collective-permute-start | bytes 103688 | tf_op jit(solution)/shard_map/ppermute | solution.py:164
  29.3 3.2 %collective-permute-done = bf16[1,17280]{1,0:T(2,128)(2,1)S(1)} collective-permute-done((bf16[1,17280]{1,0:T(2,128)(2,1)S(1)}, bf16[1,17280]{1,0:T(2,128)(2,1)S(1)}, u32[]{:S(2)}, u32[]{:S(2)}) %collective-permute-start) | collective-permute-done | bytes 34592 | tf_op jit(solution)/shard_map/ppermute | solution.py:164
  32.8 10.1 %collective-permute-start.1 = (bf16[2,17280]{1,0:T(2,128)(2,1)S(1)}, bf16[2,17280]{1,0:T(2,128)(2,1)S(1)}, u32[]{:S(2)}, u32[]{:S(2)}) collective-permute-start(bf16[2,17280]{1,0:T(2,128)(2,1)S(1)} %pad_maximum_fusion.4), channel_id=1, source_target_pairs={{0,4},{1,5},{2,6},{3,7},{4,0},{5,1},{6,2},{7,3},{8,12},{9,13},{10,... | collective-permute-start | bytes 207368 | tf_op jit(solution)/shard_map/ppermute | solution.py:164
  42.9 3.1 %collective-permute-done.1 = bf16[2,17280]{1,0:T(2,128)(2,1)S(1)} collective-permute-done((bf16[2,17280]{1,0:T(2,128)(2,1)S(1)}, bf16[2,17280]{1,0:T(2,128)(2,1)S(1)}, u32[]{:S(2)}, u32[]{:S(2)}) %collective-permute-start.1) | collective-permute-done | bytes 69152 | tf_op jit(solution)/shard_map/ppermute | solution.py:164
  46.4 4.4 %collective-permute-start.2 = (bf16[4,17280]{1,0:T(4,128)(2,1)S(1)}, bf16[4,17280]{1,0:T(4,128)(2,1)S(1)}, u32[]{:S(2)}, u32[]{:S(2)}) collective-permute-start(bf16[4,17280]{1,0:T(4,128)(2,1)S(1)} %pad_maximum_fusion.3), channel_id=1, source_target_pairs={{0,2},{1,3},{2,0},{3,1},{4,6},{5,7},{6,4},{7,5},{8,10},{9,11},{10,... | collective-permute-start | bytes 414728 | tf_op jit(solution)/shard_map/ppermute | solution.py:164
  50.8 3.5 %collective-permute-done.2 = bf16[4,17280]{1,0:T(4,128)(2,1)S(1)} collective-permute-done((bf16[4,17280]{1,0:T(4,128)(2,1)S(1)}, bf16[4,17280]{1,0:T(4,128)(2,1)S(1)}, u32[]{:S(2)}, u32[]{:S(2)}) %collective-permute-start.2) | collective-permute-done | bytes 138272 | tf_op jit(solution)/shard_map/ppermute | solution.py:164
  54.7 3.5 %collective-permute-start.3 = (bf16[8,17280]{1,0:T(8,128)(2,1)S(1)}, bf16[8,17280]{1,0:T(8,128)(2,1)S(1)}, u32[]{:S(2)}, u32[]{:S(2)}) collective-permute-start(bf16[8,17280]{1,0:T(8,128)(2,1)S(1)} %pad_maximum_fusion.2), channel_id=1, source_target_pairs={{0,1},{1,0},{2,3},{3,2},{4,5},{5,4},{6,7},{7,6},{8,9},{9,8},{10,11... | collective-permute-start | bytes 829448 | tf_op jit(solution)/shard_map/ppermute | solution.py:164
  58.2 4.9 %collective-permute-done.3 = bf16[8,17280]{1,0:T(8,128)(2,1)S(1)} collective-permute-done((bf16[8,17280]{1,0:T(8,128)(2,1)S(1)}, bf16[8,17280]{1,0:T(8,128)(2,1)S(1)}, u32[]{:S(2)}, u32[]{:S(2)}) %collective-permute-start.3) | collective-permute-done | bytes 276512 | tf_op jit(solution)/shard_map/ppermute | solution.py:164
  64.3 1.1 broadcast_in_dim.154
  65.4 4.3 %all-to-all-start = ((bf16[4,16,9088]{2,1,0:T(8,128)(2,1)}), bf16[4,16,9088]{2,1,0:T(8,128)(2,1)S(1)}, u32[]{:S(2)}, u32[]{:S(2)}) async-start(bf16[4,16,9088]{2,1,0:T(8,128)(2,1)} %broadcast_in_dim.154), calls=%async_computation | async-start | bytes 2326528 | tf_op jit(solution)/shard_map/all_to_all | solution.py:182
  70.2 0.8 add_compare_fusion
  71.1 0.8 lt.86
  72.4 1.1 fusion.91
  73.8 8.2 %all-to-all-done = bf16[4,16,9088]{2,1,0:T(8,128)(2,1)S(1)} async-done(((bf16[4,16,9088]{2,1,0:T(8,128)(2,1)}), bf16[4,16,9088]{2,1,0:T(8,128)(2,1)S(1)}, u32[]{:S(2)}, u32[]{:S(2)}) %all-to-all-start) | async-done | bytes 1163296 | tf_op jit(solution)/shard_map/all_to_all | solution.py:182
  82.0 2.8 %reshape.589 = bf16[581632]{0:T(1024)(128)(2,1)} reshape(bf16[4,16,9088]{2,1,0:T(8,128)(2,1)S(1)} %all-to-all-done) | data formatting | bytes 2326528 | tf_op jit(solution)/shard_map/reshape | solution.py:182
  84.8 1.1 broadcast_in_dim.156
  85.8 4.3 %all-to-all-start.1 = ((bf16[4,16,8192]{2,1,0:T(8,128)(2,1)}), bf16[4,16,8192]{2,1,0:T(8,128)(2,1)}, u32[]{:S(2)}, u32[]{:S(2)}) async-start(bf16[4,16,8192]{2,1,0:T(8,128)(2,1)} %broadcast_in_dim.156), calls=%async_computation.1 | async-start | bytes 2097152 | tf_op jit(solution)/shard_map/all_to_all | solution.py:182
  90.1 2.1 reshape.590
  93.5 12.1 %all-gather = bf16[1024,64]{0,1:T(8,128)(2,1)S(1)} all-gather(bf16[128,64]{0,1:T(8,128)(2,1)S(1)} %fusion.75), channel_id=2, replica_groups=mesh['dp'=8,'tx'=4,'tz'=16] {'dp'}, dimensions={0}, use_global_device_ids=true | all-gather | bytes 147456 | tf_op jit(solution)/shard_map/all_gather | solution.py:272
  106.9 4.8 %fusion.34 = f32[128,4544]{0,1:T(8,128)} fusion(bf16[142,4544]{1,0:T(8,128)(2,1)S(1)} %copy-done, bf16[128,4544]{1,0:T(8,128)(2,1)S(1)} %reshape.590, bf16[4544,142]{0,1:T(8,128)(2,1)} %param.17), kind=kOutput, calls=%fused_computation.71 | convolution fusion | flops 331548416 | bytes 6070784 | tf_op jit(solution)/shard_map/dot_general | solution.py:277
  111.7 1.6 reshape_reshape_reshape.3
  113.3 1.3 fusion.134
  114.6 1.0 fusion.2
  115.6 1.7 fusion.10
  117.3 20.1 %all-gather.3.cloned.1.call-done = bf16[8,128,8,128]{3,2,1,0:T(8,128)(2,1)} async-done(((bf16[8,8,8,128]{3,2,1,0:T(8,128)(2,1)}), bf16[8,128,8,128]{3,2,1,0:T(8,128)(2,1)}) %all-gather.3.cloned.1.call-update) | async-done | bytes 2097168 | tf_op jit(solution)/shard_map/all_gather | solution.py:231
  137.4 1.1 slice.71
  138.5 4.3 %collective-permute-start.4 = (bf16[8,32,8,128]{3,2,1,0:T(8,128)(2,1)S(1)}, bf16[8,32,8,128]{3,2,1,0:T(8,128)(2,1)}, u32[]{:S(2)}, u32[]{:S(2)}) collective-permute-start(bf16[8,32,8,128]{3,2,1,0:T(8,128)(2,1)S(1)} %slice.71), channel_id=1, source_target_pairs={{0,16},{1,17},{2,18},{3,19},{4,20},{5,21},{6,22},{7,23},{8,24},{9,... | collective-permute-start | bytes 1572872 | tf_op jit(solution)/shard_map/ppermute | solution.py:135
  144.2 1.3 compare_and_fusion
  145.5 3.1 %collective-permute-done.4 = bf16[8,32,8,128]{3,2,1,0:T(8,128)(2,1)} collective-permute-done((bf16[8,32,8,128]{3,2,1,0:T(8,128)(2,1)S(1)}, bf16[8,32,8,128]{3,2,1,0:T(8,128)(2,1)}, u32[]{:S(2)}, u32[]{:S(2)}) %collective-permute-start.4) | collective-permute-done | bytes 524320 | tf_op jit(solution)/shard_map/ppermute | solution.py:135
  148.7 1.5 collective-permute-start.5
  150.2 1.2 iota_compare_fusion
  151.4 1.8 fusion.140
  153.2 3.4 %collective-permute-done.5 = bf16[8,32,8,128]{3,2,1,0:T(8,128)(2,1)S(1)} collective-permute-done((bf16[8,32,8,128]{3,2,1,0:T(8,128)(2,1)S(1)}, bf16[8,32,8,128]{3,2,1,0:T(8,128)(2,1)S(1)}, u32[]{:S(2)}, u32[]{:S(2)}) %collective-permute-start.5) | collective-permute-done | bytes 524320 | tf_op jit(solution)/shard_map/ppermute | solution.py:135
  157.9 0.8 fusion.5
  159.4 4.7 %all-to-all-start.2 = ((f32[8,128,66]{1,2,0:T(8,128)}), f32[8,128,66]{1,2,0:T(8,128)S(1)}, u32[]{:S(2)}, u32[]{:S(2)}) async-start(f32[8,128,66]{1,2,0:T(8,128)} %pad_maximum_fusion.1), calls=%async_computation.2 | async-start | bytes 589824 | tf_op jit(solution)/shard_map/all_to_all | solution.py:299
  164.4 7.5 %all-to-all-done.2 = f32[8,128,66]{1,2,0:T(8,128)S(1)} async-done(((f32[8,128,66]{1,2,0:T(8,128)}), f32[8,128,66]{1,2,0:T(8,128)S(1)}, u32[]{:S(2)}, u32[]{:S(2)}) %all-to-all-start.2) | async-done | bytes 270368 | tf_op jit(solution)/shard_map/all_to_all | solution.py:299
  172.1 3.3 %fusion = bf16[128,4544]{0,1:T(8,128)(2,1)} fusion(f32[128,4544]{0,1:T(8,128)} %fusion.34, bf16[64,4544]{1,0:T(8,128)(2,1)S(1)} %copy-done.5, f32[128,128]{0,1:T(8,128)S(1)} %get-tuple-element.55, f32[128]{0:T(128)S(1)} %get-tuple-element.54, f32[128,64]{0,1:T(8,128)S(1)} %fusion.21, f32[128,128]{0,1:T(8,128)S(1)} %copy-done.8, ...), kind=kOutput, calls=%fused_computation.2 | convolution fusion | flops 77783040 | bytes 4196352 | tf_op jit(solution)/shard_map/dot_general | solution.py:313
  175.4 1.6 copy.52
  176.9 1.3 convert_element_type.81
  178.2 7.6 %all-to-all-start.3 = ((bf16[4,16,2,4544]{3,2,1,0:T(2,128)(2,1)}), bf16[4,16,2,4544]{3,2,1,0:T(2,128)(2,1)S(1)}, u32[]{:S(2)}, u32[]{:S(2)}) async-start(bf16[4,16,2,4544]{3,2,1,0:T(2,128)(2,1)} %convert_element_type.81), calls=%async_computation.3 | async-start | bytes 2359296 | tf_op jit(solution)/shard_map/all_to_all | solution.py:194
  185.8 16.1 %all-to-all-done.3 = bf16[4,16,2,4544]{3,2,1,0:T(2,128)(2,1)S(1)} async-done(((bf16[4,16,2,4544]{3,2,1,0:T(2,128)(2,1)}), bf16[4,16,2,4544]{3,2,1,0:T(2,128)(2,1)S(1)}, u32[]{:S(2)}, u32[]{:S(2)}) %all-to-all-start.3) | async-done | bytes 1163296 | tf_op jit(solution)/shard_map/all_to_all | solution.py:194
  201.9 1.2 convert_reduce_fusion
  203.0 1.1 gather_fusion
  204.2 26.8 %all_to_all.25 = bf16[16,2,4544]{2,1,0:T(2,128)(2,1)S(1)} all-to-all(bf16[16,2,4544]{2,1,0:T(2,128)(2,1)S(1)} %gather_fusion), channel_id=1, replica_groups=mesh['dp'=8,'tx'=4,'tz'=16] {'tz'}, dimensions={0} | all-to-all | bytes 581632 | tf_op jit(solution)/shard_map/all_to_all | solution.py:197
  (111 shorter events, 13.2 us)
Async XLA Ops:
  6.5 100.4 %copy-start = (bf16[142,4544]{1,0:T(8,128)(2,1)S(1)}, bf16[142,4544]{1,0:T(8,128)(2,1)}, u32[]{:S(2)}) copy-start(bf16[142,4544]{1,0:T(8,128)(2,1)} %param.18) | copy-start | bytes 3871492
  6.5 130.8 %all-gather.3.cloned.1.call-start = ((), (), s32[]{:S(2)}) async-start(), calls=%async_computation.5 | async-start | bytes 2228224 | tf_op jit(solution)/shard_map/all_gather | solution.py:231
  15.4 17.1 %collective-permute-start = (bf16[1,17280]{1,0:T(2,128)(2,1)S(1)}, bf16[1,17280]{1,0:T(2,128)(2,1)S(1)}, u32[]{:S(2)}, u32[]{:S(2)}) collective-permute-start(bf16[1,17280]{1,0:T(2,128)(2,1)S(1)} %broadcast_in_dim.153), channel_id=1, source_target_pairs={{0,8},{1,9},{2,10},{3,11},{4,12},{5,13},{6,14},{7,15},{8,0},{9,1},... | collective-permute-start | bytes 103688 | tf_op jit(solution)/shard_map/ppermute | solution.py:164
  32.8 13.2 %collective-permute-start.1 = (bf16[2,17280]{1,0:T(2,128)(2,1)S(1)}, bf16[2,17280]{1,0:T(2,128)(2,1)S(1)}, u32[]{:S(2)}, u32[]{:S(2)}) collective-permute-start(bf16[2,17280]{1,0:T(2,128)(2,1)S(1)} %pad_maximum_fusion.4), channel_id=1, source_target_pairs={{0,4},{1,5},{2,6},{3,7},{4,0},{5,1},{6,2},{7,3},{8,12},{9,13},{10,... | collective-permute-start | bytes 207368 | tf_op jit(solution)/shard_map/ppermute | solution.py:164
  46.4 7.9 %collective-permute-start.2 = (bf16[4,17280]{1,0:T(4,128)(2,1)S(1)}, bf16[4,17280]{1,0:T(4,128)(2,1)S(1)}, u32[]{:S(2)}, u32[]{:S(2)}) collective-permute-start(bf16[4,17280]{1,0:T(4,128)(2,1)S(1)} %pad_maximum_fusion.3), channel_id=1, source_target_pairs={{0,2},{1,3},{2,0},{3,1},{4,6},{5,7},{6,4},{7,5},{8,10},{9,11},{10,... | collective-permute-start | bytes 414728 | tf_op jit(solution)/shard_map/ppermute | solution.py:164
  54.5 8.9 %copy-start.19 = (s32[8]{0:T(128)S(1)}, s32[8]{0:T(128)}, u32[]{:S(2)}) copy-start(s32[8]{0:T(128)} %param.20) | copy-start | bytes 100
  54.7 8.4 %collective-permute-start.3 = (bf16[8,17280]{1,0:T(8,128)(2,1)S(1)}, bf16[8,17280]{1,0:T(8,128)(2,1)S(1)}, u32[]{:S(2)}, u32[]{:S(2)}) collective-permute-start(bf16[8,17280]{1,0:T(8,128)(2,1)S(1)} %pad_maximum_fusion.2), channel_id=1, source_target_pairs={{0,1},{1,0},{2,3},{3,2},{4,5},{5,4},{6,7},{7,6},{8,9},{9,8},{10,11... | collective-permute-start | bytes 829448 | tf_op jit(solution)/shard_map/ppermute | solution.py:164
  63.4 10.3 %copy-start.1 = (bf16[16,17280]{1,0:T(8,128)(2,1)}, bf16[16,17280]{1,0:T(8,128)(2,1)S(1)}, u32[]{:S(2)}) copy-start(bf16[16,17280]{1,0:T(8,128)(2,1)S(1)} %pad_maximum_fusion) | copy-start | bytes 1658884
  65.4 16.6 %all-to-all-start = ((bf16[4,16,9088]{2,1,0:T(8,128)(2,1)}), bf16[4,16,9088]{2,1,0:T(8,128)(2,1)S(1)}, u32[]{:S(2)}, u32[]{:S(2)}) async-start(bf16[4,16,9088]{2,1,0:T(8,128)(2,1)} %broadcast_in_dim.154), calls=%async_computation | async-start | bytes 2326528 | tf_op jit(solution)/shard_map/all_to_all | solution.py:182
  69.7 0.6 copy-start.21
  73.7 19.1 %copy-start.12 = (f32[128,32]{0,1:T(8,128)}, f32[128,32]{0,1:T(8,128)S(1)}, u32[]{:S(2)}) copy-start(f32[128,32]{0,1:T(8,128)S(1)} %get-tuple-element.46) | copy-start | bytes 49156
  73.7 19.1 %copy-start.14 = (f32[128,32]{0,1:T(8,128)}, f32[128,32]{0,1:T(8,128)S(1)}, u32[]{:S(2)}) copy-start(f32[128,32]{0,1:T(8,128)S(1)} %get-tuple-element.47) | copy-start | bytes 49156
  73.7 11.1 %slice-start = ((bf16[16,17280]{1,0:T(8,128)(2,1)}), bf16[16,8192]{1,0:T(8,128)(2,1)S(1)}, s32[]{:S(2)}) async-start(bf16[16,17280]{1,0:T(8,128)(2,1)} %copy-done.1), calls=%async_computation.6 | async-start | bytes 524288 | tf_op jit(solution)/shard_map/slice | solution.py:233
  85.8 25.9 %all-to-all-start.1 = ((bf16[4,16,8192]{2,1,0:T(8,128)(2,1)}), bf16[4,16,8192]{2,1,0:T(8,128)(2,1)}, u32[]{:S(2)}, u32[]{:S(2)}) async-start(bf16[4,16,8192]{2,1,0:T(8,128)(2,1)} %broadcast_in_dim.156), calls=%async_computation.1 | async-start | bytes 2097152 | tf_op jit(solution)/shard_map/all_to_all | solution.py:182
  90.1 2.2 copy-start.4
  92.9 0.6 copy-start.10
  105.6 0.7 copy-start.2
  114.6 1.0 copy-start.16
  138.5 10.2 %collective-permute-start.4 = (bf16[8,32,8,128]{3,2,1,0:T(8,128)(2,1)S(1)}, bf16[8,32,8,128]{3,2,1,0:T(8,128)(2,1)}, u32[]{:S(2)}, u32[]{:S(2)}) collective-permute-start(bf16[8,32,8,128]{3,2,1,0:T(8,128)(2,1)S(1)} %slice.71), channel_id=1, source_target_pairs={{0,16},{1,17},{2,18},{3,19},{4,20},{5,21},{6,22},{7,23},{8,24},{9,... | collective-permute-start | bytes 1572872 | tf_op jit(solution)/shard_map/ppermute | solution.py:135
  148.7 8.0 %collective-permute-start.5 = (bf16[8,32,8,128]{3,2,1,0:T(8,128)(2,1)S(1)}, bf16[8,32,8,128]{3,2,1,0:T(8,128)(2,1)S(1)}, u32[]{:S(2)}, u32[]{:S(2)}) collective-permute-start(bf16[8,32,8,128]{3,2,1,0:T(8,128)(2,1)S(1)} %broadcast_select_fusion), channel_id=1, source_target_pairs={{0,48},{16,32},{1,49},{17,33},{2,50},{18,34},{3,51},{19,35},{4,52}... | collective-permute-start | bytes 1572872 | tf_op jit(solution)/shard_map/ppermute | solution.py:135
  153.2 4.0 %copy-start.7 = (f32[128,128]{0,1:T(8,128)}, f32[128,128]{0,1:T(8,128)S(1)}, u32[]{:S(2)}) copy-start(f32[128,128]{0,1:T(8,128)S(1)} %fusion.140) | copy-start | bytes 196612
  153.2 3.5 %copy-start.3 = (bf16[1024,64]{0,1:T(8,128)(2,1)S(1)}, bf16[1024,64]{0,1:T(8,128)(2,1)}, u32[]{:S(2)}) copy-start(bf16[1024,64]{0,1:T(8,128)(2,1)} %copy-done.2) | copy-start | bytes 393220
  153.2 3.5 %copy-start.18 = (pred[8,256]{1,0:T(8,128)(4,1)S(1)}, pred[8,256]{1,0:T(8,128)(4,1)}, u32[]{:S(2)}) copy-start(pred[8,256]{1,0:T(8,128)(4,1)} %compare_and_fusion) | copy-start | bytes 6148
  156.7 0.9 copy-start.17
  156.8 0.9 copy-start.20
  156.8 0.9 copy-start.22
  156.8 1.0 copy-start.9
  157.8 6.3 %copy-start.8 = (f32[128,128]{0,1:T(8,128)S(1)}, f32[128,128]{0,1:T(8,128)}, u32[]{:S(2)}) copy-start(f32[128,128]{0,1:T(8,128)} %copy-done.7) | copy-start | bytes 196612
  157.8 6.3 %copy-start.11 = (bf16[128,64]{0,1:T(8,128)(2,1)S(1)}, bf16[128,64]{0,1:T(8,128)(2,1)}, u32[]{:S(2)}) copy-start(bf16[128,64]{0,1:T(8,128)(2,1)} %copy-done.10) | copy-start | bytes 49156
  157.8 6.3 %copy-start.13 = (f32[128,32]{0,1:T(8,128)S(1)}, f32[128,32]{0,1:T(8,128)}, u32[]{:S(2)}) copy-start(f32[128,32]{0,1:T(8,128)} %copy-done.12) | copy-start | bytes 49156
  157.8 6.3 %copy-start.15 = (f32[128,32]{0,1:T(8,128)S(1)}, f32[128,32]{0,1:T(8,128)}, u32[]{:S(2)}) copy-start(f32[128,32]{0,1:T(8,128)} %copy-done.14) | copy-start | bytes 49156
  157.9 6.3 %copy-start.24 = (s32[128]{0:T(128)S(1)}, s32[128]{0:T(128)}, u32[]{:S(2)}) copy-start(s32[128]{0:T(128)} %get-tuple-element.56) | copy-start | bytes 1540
  158.6 13.4 %copy-start.5 = (bf16[64,4544]{1,0:T(8,128)(2,1)S(1)}, bf16[64,4544]{1,0:T(8,128)(2,1)}, u32[]{:S(2)}) copy-start(bf16[64,4544]{1,0:T(8,128)(2,1)} %param.16) | copy-start | bytes 1744900
  159.4 12.6 %all-to-all-start.2 = ((f32[8,128,66]{1,2,0:T(8,128)}), f32[8,128,66]{1,2,0:T(8,128)S(1)}, u32[]{:S(2)}, u32[]{:S(2)}) async-start(f32[8,128,66]{1,2,0:T(8,128)} %pad_maximum_fusion.1), calls=%async_computation.2 | async-start | bytes 589824 | tf_op jit(solution)/shard_map/all_to_all | solution.py:299
  178.2 7.6 %copy-start.23 = (s32[16]{0:T(128)S(1)}, s32[16]{0:T(128)}, u32[]{:S(2)}) copy-start(s32[16]{0:T(128)} %constant.238) | copy-start | bytes 196
  178.2 23.6 %all-to-all-start.3 = ((bf16[4,16,2,4544]{3,2,1,0:T(2,128)(2,1)}), bf16[4,16,2,4544]{3,2,1,0:T(2,128)(2,1)S(1)}, u32[]{:S(2)}, u32[]{:S(2)}) async-start(bf16[4,16,2,4544]{3,2,1,0:T(2,128)(2,1)} %convert_element_type.81), calls=%async_computation.3 | async-start | bytes 2359296 | tf_op jit(solution)/shard_map/all_to_all | solution.py:194
  185.8 45.3 %copy-start.6 = (bf16[1,2,4544]{2,1,0:T(2,128)(2,1)S(1)}, bf16[1,2,4544]{2,1,0:T(2,128)(2,1)}, u32[]{:S(2)}) copy-start(bf16[1,2,4544]{2,1,0:T(2,128)(2,1)} %param.11) | copy-start | bytes 54532
Sparse Core Ops, SparseCore 0:
  63.5 73.7 all-gather.2

commit v9 on v5

--- a/solution.py
+++ b/solution.py
@@ -136,6 +136,14 @@
         x = jnp.where((me >= have) & (me < 2 * have), got, x)
         have *= 2
     return x
+
+
+def spread_now(x, name):
+    me = lax.axis_index(name)
+    out = x
+    for k in range(1, lax.axis_size(name)):
+        out = jnp.where(me == k, lax.ppermute(x, name, [(0, k)]), out)
+    return out
 
 
 def partial_state(queries, keys, values, valid):
@@ -227,7 +235,8 @@
     long_keys = long_all.reshape(-1, 2 * width)
 
     short_blocks = -(-SHORT_MAX // inner_all)
-    short_gath = lax.all_gather(kv_cache, "tz", axis=1, tiled=True)[:, :short_blocks]
+    first_row = spread_now(kv_cache, "tx")
+    short_gath = lax.all_gather(first_row, "tz", axis=1, tiled=True)[:, :short_blocks]
     short_pos = (jnp.arange(short_blocks, dtype=jnp.int32)[:, None] * inner_all + inner_pos).reshape(-1)
 
     piece = both[:, :token_cut].reshape(n * per_device, width_model)
@@ -269,7 +278,7 @@
     short_gath, long_v, long_m, long_s, down_part = lax.optimization_barrier(
         (short_gath, long_v, long_m, long_s, down_part)
     )
-    short_keys = spread_from_first(short_gath, "tx").reshape(requests, -1, 2 * width)
+    short_keys = short_gath.reshape(requests, -1, 2 * width)
     which = jnp.arange(requests, dtype=jnp.int32)
     short_valid = (short_pos[None, :] < cache_lengths[:, None]) & (which != longest)[:, None]
     short_state = partial_state(

time: 234 us -> 233 us (level)
  other arithmetic: 15.5 us -> 19.6 us
    all_gather x1, waiting for transfers between devices: 10.3 us -> 26.3 us  [local(): lax.all_gather(first_row, 'tz', axis=1, tiled=True)[:, :short_blocks]]
    ppermute x2 -> x3, waiting for transfers between devices: 8.04 us -> 0.01 us  [spread_now(): out = jnp.where(me == k, lax.ppermute(x, name, [(0, k)]), out)]
    all_to_all x1, waiting for transfers between devices: 16.8 us -> 10.4 us  [gather_tensor(): lax.all_to_all(wide, 'tx', 0, 0, tiled=True).reshape((-1,) + piece.shape)]
    ppermute x2 -> x3, starting transfers between devices: 5.53 us -> 9.21 us  [spread_now(): out = jnp.where(me == k, lax.ppermute(x, name, [(0, k)]), out)]
    ppermute x4, waiting for transfers between devices: 14.7 us -> 11.4 us  [z_rounds(): other = lax.ppermute(buf, 'tz', [(i, i ^ 1 << b) for i in range(size)])]
    all_to_all x1, starting transfers between devices: 7.55 us -> 4.31 us  [scatter_tensor(): lax.all_to_all(buf, 'tx', 0, 0, tiled=True).astype(jnp.float32).sum(0)]
  transfers between devices with their start and end apart: 10 -> 11, of which waited for: 10 -> 7; matrix products, arithmetic and copies ran while one was open for 12% -> 14% of each run, Pallas kernels for 0% -> 0%
where the time goes in v9:
time: 233 us; the launch traced here: 232 us
  waiting for transfers between devices  71.8 us (31%)
  starting transfers between devices  51.7 us (22%)
  blocking collectives  39.3 us (17%)
  local copies, waits for them, and re-layouts  19.8 us (8%)
  other arithmetic  19.6 us (8%)
  between operations  15.7 us (7%)
  matrix products  13.9 us (6%)
    ppermute x4, starting transfers between devices, z_rounds(): other = lax.ppermute(buf, 'tz', [(i, i ^ 1 << b) for i in range(size)])  30.4 us
    all_to_all x1, blocking collectives, scatter_tensor(): lax.all_to_all(ready, 'tz', 0, 0, tiled=True).astype(jnp.float32).sum(0)  27.2 us
    all_gather x1, waiting for transfers between devices, local(): lax.all_gather(first_row, 'tz', axis=1, tiled=True)[:, :short_blocks]  26.3 us
    all_to_all x1, waiting for transfers between devices, scatter_tensor(): lax.all_to_all(buf, 'tx', 0, 0, tiled=True).astype(jnp.float32).sum(0)  16.1 us
    all_gather x1, blocking collectives, local(): q_all = lax.all_gather(query_rows, 'dp', axis=0, tiled=False)  12.1 us
    ppermute x4, waiting for transfers between devices, z_rounds(): other = lax.ppermute(buf, 'tz', [(i, i ^ 1 << b) for i in range(size)])  11.4 us
    all_to_all x1, waiting for transfers between devices, gather_tensor(): lax.all_to_all(wide, 'tx', 0, 0, tiled=True).reshape((-1,) + piece.shape)  10.4 us
    ppermute x3, starting transfers between devices, spread_now(): out = jnp.where(me == k, lax.ppermute(x, name, [(0, k)]), out)  9.21 us
  transfers between devices with their start and end apart: 11, of which 7 were waited for; matrix products, arithmetic and copies ran while one was open for 14% of the time, Pallas kernels for 0%

profile of v9, /device:TPU:64, one launch (start us, length us, event | category | flops | bytes accessed | tf_op | source)
XLA Modules:
  0.0 231.8 jit_solution(15253705192771068206)
XLA Ops:
  6.5 1.0 convert_reduce_fusion.2
  7.5 0.8 reshape.592
  8.3 1.3 iota_reduce_fusion
  10.7 0.7 add.273
  11.6 0.7 mul.258
  12.4 0.9 fusion.38
  15.1 13.9 %collective-permute-start = (bf16[1,17280]{1,0:T(2,128)(2,1)S(1)}, bf16[1,17280]{1,0:T(2,128)(2,1)S(1)}, u32[]{:S(2)}, u32[]{:S(2)}) collective-permute-start(bf16[1,17280]{1,0:T(2,128)(2,1)S(1)} %broadcast_in_dim.147), channel_id=1, source_target_pairs={{0,8},{1,9},{2,10},{3,11},{4,12},{5,13},{6,14},{7,15},{8,0},{9,1},... | collective-permute-start | bytes 103688 | tf_op jit(solution)/shard_map/ppermute | solution.py:172
  29.0 3.2 %collective-permute-done = bf16[1,17280]{1,0:T(2,128)(2,1)S(1)} collective-permute-done((bf16[1,17280]{1,0:T(2,128)(2,1)S(1)}, bf16[1,17280]{1,0:T(2,128)(2,1)S(1)}, u32[]{:S(2)}, u32[]{:S(2)}) %collective-permute-start) | collective-permute-done | bytes 34592 | tf_op jit(solution)/shard_map/ppermute | solution.py:172
  32.5 10.1 %collective-permute-start.1 = (bf16[2,17280]{1,0:T(2,128)(2,1)S(1)}, bf16[2,17280]{1,0:T(2,128)(2,1)S(1)}, u32[]{:S(2)}, u32[]{:S(2)}) collective-permute-start(bf16[2,17280]{1,0:T(2,128)(2,1)S(1)} %pad_maximum_fusion.4), channel_id=1, source_target_pairs={{0,4},{1,5},{2,6},{3,7},{4,0},{5,1},{6,2},{7,3},{8,12},{9,13},{10,... | collective-permute-start | bytes 207368 | tf_op jit(solution)/shard_map/ppermute | solution.py:172
  42.6 3.1 %collective-permute-done.1 = bf16[2,17280]{1,0:T(2,128)(2,1)S(1)} collective-permute-done((bf16[2,17280]{1,0:T(2,128)(2,1)S(1)}, bf16[2,17280]{1,0:T(2,128)(2,1)S(1)}, u32[]{:S(2)}, u32[]{:S(2)}) %collective-permute-start.1) | collective-permute-done | bytes 69152 | tf_op jit(solution)/shard_map/ppermute | solution.py:172
  46.1 4.4 %collective-permute-start.2 = (bf16[4,17280]{1,0:T(4,128)(2,1)S(1)}, bf16[4,17280]{1,0:T(4,128)(2,1)S(1)}, u32[]{:S(2)}, u32[]{:S(2)}) collective-permute-start(bf16[4,17280]{1,0:T(4,128)(2,1)S(1)} %pad_maximum_fusion.3), channel_id=1, source_target_pairs={{0,2},{1,3},{2,0},{3,1},{4,6},{5,7},{6,4},{7,5},{8,10},{9,11},{10,... | collective-permute-start | bytes 414728 | tf_op jit(solution)/shard_map/ppermute | solution.py:172
  50.5 5.3 %collective-permute-start.4 = (bf16[8,8,8,128]{3,2,1,0:T(8,128)(2,1)}, bf16[8,8,8,128]{3,2,1,0:T(8,128)(2,1)}, u32[]{:S(2)}, u32[]{:S(2)}) collective-permute-start(bf16[8,8,8,128]{3,2,1,0:T(8,128)(2,1)} %param.19), channel_id=1, source_target_pairs={{0,48},{1,49},{2,50},{3,51},{4,52},{5,53},{6,54},{7,55},{8,56},{9,... | collective-permute-start | bytes 393224 | tf_op jit(solution)/shard_map/ppermute | solution.py:145
  55.9 2.0 collective-permute-start.5
  57.8 1.9 collective-permute-start.6
  60.1 1.9 collective-permute-start.3
  63.5 5.1 %collective-permute-done.3 = bf16[8,17280]{1,0:T(8,128)(2,1)S(1)} collective-permute-done((bf16[8,17280]{1,0:T(8,128)(2,1)S(1)}, bf16[8,17280]{1,0:T(8,128)(2,1)S(1)}, u32[]{:S(2)}, u32[]{:S(2)}) %collective-permute-start.3) | collective-permute-done | bytes 276512 | tf_op jit(solution)/shard_map/ppermute | solution.py:172
  68.8 1.5 broadcast_in_dim.148
  70.3 3.6 %all-to-all-start = ((bf16[4,16,17280]{2,1,0:T(8,128)(2,1)}), bf16[4,16,17280]{2,1,0:T(8,128)(2,1)S(1)}, u32[]{:S(2)}, u32[]{:S(2)}) async-start(bf16[4,16,17280]{2,1,0:T(8,128)(2,1)} %broadcast_in_dim.148), calls=%async_computation | async-start | bytes 4423680 | tf_op jit(solution)/shard_map/all_to_all | solution.py:184
  74.0 2.2 add_compare_fusion
  76.2 1.6 lt.78
  77.8 1.6 select_select_fusion
  81.4 1.1 iota_compare_fusion
  82.5 1.1 fusion.91
  83.7 1.3 compare_and_fusion
  85.0 0.7 multiply_sine_fusion
  85.8 10.4 %all-to-all-done = bf16[4,16,17280]{2,1,0:T(8,128)(2,1)S(1)} async-done(((bf16[4,16,17280]{2,1,0:T(8,128)(2,1)}), bf16[4,16,17280]{2,1,0:T(8,128)(2,1)S(1)}, u32[]{:S(2)}, u32[]{:S(2)}) %all-to-all-start) | async-done | bytes 2211872 | tf_op jit(solution)/shard_map/all_to_all | solution.py:184
  96.2 1.1 slice.73
  97.3 1.1 slice.69
  98.4 1.6 reshape_reshape.4
  99.9 1.8 reshape.589
  101.8 1.6 fusion.139
  103.4 12.1 %all-gather = bf16[1024,64]{0,1:T(8,128)(2,1)S(1)} all-gather(bf16[128,64]{0,1:T(8,128)(2,1)S(1)} %fusion.75), channel_id=2, replica_groups=mesh['dp'=8,'tx'=4,'tz'=16] {'dp'}, dimensions={0}, use_global_device_ids=true | all-gather | bytes 147456 | tf_op jit(solution)/shard_map/all_gather | solution.py:272
  116.9 0.9 fusion.2
  119.3 1.7 fusion.10
  121.0 4.8 %fusion.34 = f32[128,4544]{0,1:T(8,128)} fusion(bf16[142,4544]{1,0:T(8,128)(2,1)S(1)} %copy-done, bf16[128,4544]{1,0:T(8,128)(2,1)S(1)} %reshape.589, bf16[4544,142]{0,1:T(8,128)(2,1)} %param.17), kind=kOutput, calls=%fused_computation.70 | convolution fusion | flops 331548416 | bytes 6070784 | tf_op jit(solution)/shard_map/dot_general | solution.py:277
  125.9 26.3 %all-gather.3.cloned.1.call-done = bf16[8,128,8,128]{3,2,1,0:T(8,128)(2,1)} async-done(((bf16[8,8,8,128]{3,2,1,0:T(8,128)(2,1)}), bf16[8,128,8,128]{3,2,1,0:T(8,128)(2,1)}) %all-gather.3.cloned.1.call-update) | async-done | bytes 2097168 | tf_op jit(solution)/shard_map/all_gather | solution.py:239
  152.2 1.1 slice.72
  154.4 0.8 fusion.5
  155.9 4.2 %all-to-all-start.1 = ((f32[8,128,66]{1,2,0:T(8,128)}), f32[8,128,66]{1,2,0:T(8,128)S(1)}, u32[]{:S(2)}, u32[]{:S(2)}) async-start(f32[8,128,66]{1,2,0:T(8,128)} %pad_maximum_fusion.1), calls=%async_computation.1 | async-start | bytes 589824 | tf_op jit(solution)/shard_map/all_to_all | solution.py:299
  160.5 7.5 %all-to-all-done.1 = f32[8,128,66]{1,2,0:T(8,128)S(1)} async-done(((f32[8,128,66]{1,2,0:T(8,128)}), f32[8,128,66]{1,2,0:T(8,128)S(1)}, u32[]{:S(2)}, u32[]{:S(2)}) %all-to-all-start.1) | async-done | bytes 270368 | tf_op jit(solution)/shard_map/all_to_all | solution.py:299
  168.1 3.3 %fusion = bf16[128,4544]{0,1:T(8,128)(2,1)} fusion(f32[128,4544]{0,1:T(8,128)} %fusion.34, bf16[64,4544]{1,0:T(8,128)(2,1)S(1)} %copy-done.4, f32[128,128]{0,1:T(8,128)S(1)} %get-tuple-element.47, f32[128]{0:T(128)S(1)} %get-tuple-element.46, f32[128,64]{0,1:T(8,128)S(1)} %fusion.21, f32[128,128]{0,1:T(8,128)S(1)} %copy-done.7, ...), kind=kOutput, calls=%fused_computation.2 | convolution fusion | flops 77783040 | bytes 4196352 | tf_op jit(solution)/shard_map/dot_general | solution.py:313
  171.4 1.6 copy.52
  173.0 1.3 convert_element_type.81
  174.3 4.3 %all-to-all-start.2 = ((bf16[4,16,2,4544]{3,2,1,0:T(2,128)(2,1)}), bf16[4,16,2,4544]{3,2,1,0:T(2,128)(2,1)S(1)}, u32[]{:S(2)}, u32[]{:S(2)}) async-start(bf16[4,16,2,4544]{3,2,1,0:T(2,128)(2,1)} %convert_element_type.81), calls=%async_computation.2 | async-start | bytes 2359296 | tf_op jit(solution)/shard_map/all_to_all | solution.py:196
  178.6 16.1 %all-to-all-done.2 = bf16[4,16,2,4544]{3,2,1,0:T(2,128)(2,1)S(1)} async-done(((bf16[4,16,2,4544]{3,2,1,0:T(2,128)(2,1)}), bf16[4,16,2,4544]{3,2,1,0:T(2,128)(2,1)S(1)}, u32[]{:S(2)}, u32[]{:S(2)}) %all-to-all-start.2) | async-done | bytes 1163296 | tf_op jit(solution)/shard_map/all_to_all | solution.py:196
  194.7 1.2 convert_reduce_fusion
  195.8 1.1 gather_fusion
  197.0 27.2 %all_to_all.20 = bf16[16,2,4544]{2,1,0:T(2,128)(2,1)S(1)} all-to-all(bf16[16,2,4544]{2,1,0:T(2,128)(2,1)S(1)} %gather_fusion), channel_id=1, replica_groups=mesh['dp'=8,'tx'=4,'tz'=16] {'tz'}, dimensions={0} | all-to-all | bytes 581632 | tf_op jit(solution)/shard_map/all_to_all | solution.py:199
  (111 shorter events, 11.7 us)
Async XLA Ops:
  6.5 114.5 %copy-start = (bf16[142,4544]{1,0:T(8,128)(2,1)S(1)}, bf16[142,4544]{1,0:T(8,128)(2,1)}, u32[]{:S(2)}) copy-start(bf16[142,4544]{1,0:T(8,128)(2,1)} %param.18) | copy-start | bytes 3871492
  14.3 47.8 %copy-start.21 = (s32[8]{0:T(128)S(1)}, s32[8]{0:T(128)}, u32[]{:S(2)}) copy-start(s32[8]{0:T(128)} %param.20) | copy-start | bytes 100
  15.1 17.1 %collective-permute-start = (bf16[1,17280]{1,0:T(2,128)(2,1)S(1)}, bf16[1,17280]{1,0:T(2,128)(2,1)S(1)}, u32[]{:S(2)}, u32[]{:S(2)}) collective-permute-start(bf16[1,17280]{1,0:T(2,128)(2,1)S(1)} %broadcast_in_dim.147), channel_id=1, source_target_pairs={{0,8},{1,9},{2,10},{3,11},{4,12},{5,13},{6,14},{7,15},{8,0},{9,1},... | collective-permute-start | bytes 103688 | tf_op jit(solution)/shard_map/ppermute | solution.py:172
  32.5 13.2 %collective-permute-start.1 = (bf16[2,17280]{1,0:T(2,128)(2,1)S(1)}, bf16[2,17280]{1,0:T(2,128)(2,1)S(1)}, u32[]{:S(2)}, u32[]{:S(2)}) collective-permute-start(bf16[2,17280]{1,0:T(2,128)(2,1)S(1)} %pad_maximum_fusion.4), channel_id=1, source_target_pairs={{0,4},{1,5},{2,6},{3,7},{4,0},{5,1},{6,2},{7,3},{8,12},{9,13},{10,... | collective-permute-start | bytes 207368 | tf_op jit(solution)/shard_map/ppermute | solution.py:172
  46.1 13.7 %collective-permute-start.2 = (bf16[4,17280]{1,0:T(4,128)(2,1)S(1)}, bf16[4,17280]{1,0:T(4,128)(2,1)S(1)}, u32[]{:S(2)}, u32[]{:S(2)}) collective-permute-start(bf16[4,17280]{1,0:T(4,128)(2,1)S(1)} %pad_maximum_fusion.3), channel_id=1, source_target_pairs={{0,2},{1,3},{2,0},{3,1},{4,6},{5,7},{6,4},{7,5},{8,10},{9,11},{10,... | collective-permute-start | bytes 414728 | tf_op jit(solution)/shard_map/ppermute | solution.py:172
  50.5 27.2 %collective-permute-start.4 = (bf16[8,8,8,128]{3,2,1,0:T(8,128)(2,1)}, bf16[8,8,8,128]{3,2,1,0:T(8,128)(2,1)}, u32[]{:S(2)}, u32[]{:S(2)}) collective-permute-start(bf16[8,8,8,128]{3,2,1,0:T(8,128)(2,1)} %param.19), channel_id=1, source_target_pairs={{0,48},{1,49},{2,50},{3,51},{4,52},{5,53},{6,54},{7,55},{8,56},{9,... | collective-permute-start | bytes 393224 | tf_op jit(solution)/shard_map/ppermute | solution.py:145
  55.9 21.9 %collective-permute-start.5 = (bf16[8,8,8,128]{3,2,1,0:T(8,128)(2,1)}, bf16[8,8,8,128]{3,2,1,0:T(8,128)(2,1)}, u32[]{:S(2)}, u32[]{:S(2)}) collective-permute-start(bf16[8,8,8,128]{3,2,1,0:T(8,128)(2,1)} %param.19), channel_id=1, source_target_pairs={{0,32},{1,33},{2,34},{3,35},{4,36},{5,37},{6,38},{7,39},{8,40},{9,... | collective-permute-start | bytes 393224 | tf_op jit(solution)/shard_map/ppermute | solution.py:145
  57.8 20.0 %collective-permute-start.6 = (bf16[8,8,8,128]{3,2,1,0:T(8,128)(2,1)}, bf16[8,8,8,128]{3,2,1,0:T(8,128)(2,1)}, u32[]{:S(2)}, u32[]{:S(2)}) collective-permute-start(bf16[8,8,8,128]{3,2,1,0:T(8,128)(2,1)} %param.19), channel_id=1, source_target_pairs={{0,16},{1,17},{2,18},{3,19},{4,20},{5,21},{6,22},{7,23},{8,24},{9,... | collective-permute-start | bytes 393224 | tf_op jit(solution)/shard_map/ppermute | solution.py:145
  60.1 8.4 %collective-permute-start.3 = (bf16[8,17280]{1,0:T(8,128)(2,1)S(1)}, bf16[8,17280]{1,0:T(8,128)(2,1)S(1)}, u32[]{:S(2)}, u32[]{:S(2)}) collective-permute-start(bf16[8,17280]{1,0:T(8,128)(2,1)S(1)} %pad_maximum_fusion.2), channel_id=1, source_target_pairs={{0,1},{1,0},{2,3},{3,2},{4,5},{5,4},{6,7},{7,6},{8,9},{9,8},{10,11... | collective-permute-start | bytes 829448 | tf_op jit(solution)/shard_map/ppermute | solution.py:172
  62.1 11.9 %copy-start.23 = (s32[8]{0:T(128)}, s32[8]{0:T(128)S(1)}, u32[]{:S(2)}) copy-start(s32[8]{0:T(128)S(1)} %iota_add_fusion) | copy-start | bytes 100
  70.3 25.9 %all-to-all-start = ((bf16[4,16,17280]{2,1,0:T(8,128)(2,1)}), bf16[4,16,17280]{2,1,0:T(8,128)(2,1)S(1)}, u32[]{:S(2)}, u32[]{:S(2)}) async-start(bf16[4,16,17280]{2,1,0:T(8,128)(2,1)} %broadcast_in_dim.148), calls=%async_computation | async-start | bytes 4423680 | tf_op jit(solution)/shard_map/all_to_all | solution.py:184
  73.9 78.3 %all-gather.3.cloned.1.call-start = ((), (), s32[]{:S(2)}) async-start(), calls=%async_computation.4 | async-start | bytes 2228224 | tf_op jit(solution)/shard_map/all_gather | solution.py:239
  101.8 1.6 copy-start.11
  101.8 1.6 copy-start.13
  101.8 14.5 %copy-start.15 = (pred[4096]{0:T(1024)(128)(4,1)S(1)}, pred[4096]{0:T(1024)(128)(4,1)}, u32[]{:S(2)}) copy-start(pred[4096]{0:T(1024)(128)(4,1)} %lt.78) | copy-start | bytes 12292
  103.4 12.2 %copy-start.9 = (bf16[128,64]{0,1:T(8,128)(2,1)}, bf16[128,64]{0,1:T(8,128)(2,1)S(1)}, u32[]{:S(2)}) copy-start(bf16[128,64]{0,1:T(8,128)(2,1)S(1)} %fusion.75) | copy-start | bytes 49156
  115.6 0.7 copy-start.1
  116.8 2.5 %copy-start.18 = (f32[128]{0:T(128)}, f32[128]{0:T(128)S(1)}, u32[]{:S(2)}) copy-start(f32[128]{0:T(128)S(1)} %get-tuple-element.13) | copy-start | bytes 1540
  116.9 1.3 copy-start.3
  118.7 0.6 copy-start.6
  121.0 32.3 %copy-start.2 = (bf16[1024,64]{0,1:T(8,128)(2,1)S(1)}, bf16[1024,64]{0,1:T(8,128)(2,1)}, u32[]{:S(2)}) copy-start(bf16[1024,64]{0,1:T(8,128)(2,1)} %copy-done.1) | copy-start | bytes 393220
  121.0 32.3 %copy-start.20 = (pred[8,256]{1,0:T(8,128)(4,1)S(1)}, pred[8,256]{1,0:T(8,128)(4,1)}, u32[]{:S(2)}) copy-start(pred[8,256]{1,0:T(8,128)(4,1)} %compare_and_fusion) | copy-start | bytes 6148
  153.3 0.9 copy-start.19
  153.3 0.9 copy-start.22
  153.3 0.9 copy-start.24
  153.3 1.0 copy-start.8
  154.4 5.8 %copy-start.7 = (f32[128,128]{0,1:T(8,128)S(1)}, f32[128,128]{0,1:T(8,128)}, u32[]{:S(2)}) copy-start(f32[128,128]{0,1:T(8,128)} %copy-done.6) | copy-start | bytes 196612
  154.4 5.8 %copy-start.10 = (bf16[128,64]{0,1:T(8,128)(2,1)S(1)}, bf16[128,64]{0,1:T(8,128)(2,1)}, u32[]{:S(2)}) copy-start(bf16[128,64]{0,1:T(8,128)(2,1)} %copy-done.9) | copy-start | bytes 49156
  154.4 5.8 %copy-start.12 = (f32[128,32]{0,1:T(8,128)S(1)}, f32[128,32]{0,1:T(8,128)}, u32[]{:S(2)}) copy-start(f32[128,32]{0,1:T(8,128)} %get-tuple-element.38) | copy-start | bytes 49156
  154.4 5.8 %copy-start.14 = (f32[128,32]{0,1:T(8,128)S(1)}, f32[128,32]{0,1:T(8,128)}, u32[]{:S(2)}) copy-start(f32[128,32]{0,1:T(8,128)} %get-tuple-element.39) | copy-start | bytes 49156
  154.4 5.8 %copy-start.16 = (f32[128,32]{0,1:T(8,128)S(1)}, f32[128,32]{0,1:T(8,128)}, u32[]{:S(2)}) copy-start(f32[128,32]{0,1:T(8,128)} %get-tuple-element.30) | copy-start | bytes 49156
  154.4 5.8 %copy-start.17 = (f32[128,32]{0,1:T(8,128)S(1)}, f32[128,32]{0,1:T(8,128)}, u32[]{:S(2)}) copy-start(f32[128,32]{0,1:T(8,128)} %get-tuple-element.31) | copy-start | bytes 49156
  154.4 5.8 %copy-start.26 = (s32[128]{0:T(128)S(1)}, s32[128]{0:T(128)}, u32[]{:S(2)}) copy-start(s32[128]{0:T(128)} %get-tuple-element.48) | copy-start | bytes 1540
  155.2 12.9 %copy-start.4 = (bf16[64,4544]{1,0:T(8,128)(2,1)S(1)}, bf16[64,4544]{1,0:T(8,128)(2,1)}, u32[]{:S(2)}) copy-start(bf16[64,4544]{1,0:T(8,128)(2,1)} %param.16) | copy-start | bytes 1744900
  155.9 12.0 %all-to-all-start.1 = ((f32[8,128,66]{1,2,0:T(8,128)}), f32[8,128,66]{1,2,0:T(8,128)S(1)}, u32[]{:S(2)}, u32[]{:S(2)}) async-start(f32[8,128,66]{1,2,0:T(8,128)} %pad_maximum_fusion.1), calls=%async_computation.1 | async-start | bytes 589824 | tf_op jit(solution)/shard_map/all_to_all | solution.py:299
  174.3 4.3 %copy-start.25 = (s32[16]{0:T(128)S(1)}, s32[16]{0:T(128)}, u32[]{:S(2)}) copy-start(s32[16]{0:T(128)} %constant.237) | copy-start | bytes 196
  174.3 20.4 %all-to-all-start.2 = ((bf16[4,16,2,4544]{3,2,1,0:T(2,128)(2,1)}), bf16[4,16,2,4544]{3,2,1,0:T(2,128)(2,1)S(1)}, u32[]{:S(2)}, u32[]{:S(2)}) async-start(bf16[4,16,2,4544]{3,2,1,0:T(2,128)(2,1)} %convert_element_type.81), calls=%async_computation.2 | async-start | bytes 2359296 | tf_op jit(solution)/shard_map/all_to_all | solution.py:196
  178.6 45.7 %copy-start.5 = (bf16[1,2,4544]{2,1,0:T(2,128)(2,1)S(1)}, bf16[1,2,4544]{2,1,0:T(2,128)(2,1)}, u32[]{:S(2)}) copy-start(bf16[1,2,4544]{2,1,0:T(2,128)(2,1)} %param.11) | copy-start | bytes 54532
Sparse Core Ops, SparseCore 0:
  79.5 72.6 all-gather.2
